TPU v7x, 1024 devices: a whole 4x8x16 slice. The times are simulated.
1024 devices in a mesh: seq: 128 (over y_hi, z, core), head: 8 (over y_lo, x).
Axes of the slice: x: 4, y: 8 (y_hi: 4, y_lo: 2; y = y_hi * 2 + y_lo), z: 16, core: 2. Of those that a mesh axis runs over, the one named last changes fastest.
Arguments:
- teacher_query: bfloat16 [16384, 2048], P('seq', 'head'), may hold values from -98 to 98
- teacher_key: bfloat16 [16384, 2048], P('seq', 'head'), may hold values from -98 to 98
- teacher_value: bfloat16 [16384, 2048], P('seq', 'head'), may hold values from -6 to 6
- student_query: bfloat16 [16384, 2048], P('seq', 'head'), may hold values from -80 to 80
- student_key: bfloat16 [16384, 2048], P('seq', 'head'), may hold values from -80 to 80
- student_value: bfloat16 [16384, 2048], P('seq', 'head'), may hold values from -6 to 6
- segment_ids: int32 [16384], P('seq'), may hold values from 0 to 7, never falling along the last dimension, each value on 1 to 4096 neighbouring positions
- language_ids: int32 [16384], P('seq'), may hold values from 0 to 15
- language_weight: float32 [16], replicated, may hold values from 1 to 16
- teacher_out_proj: bfloat16 [4608, 2048], P('head'), may hold values from -0.125 to 0.125
- student_out_proj: bfloat16 [2048, 2304], P('head'), may hold values from -0.125 to 0.125
- match_proj: bfloat16 [4608, 2304], P('head'), may hold values from -0.09375 to 0.09375
Outputs:
- grad_query: float32 [16384, 2048], P('seq', 'head')
- grad_key: float32 [16384, 2048], P('seq', 'head')
- grad_value: float32 [16384, 2048], P('seq', 'head')
All inputs are finite; a program needn't handle non-finite values.
Results may differ from a plain program's by a relative error of at most 0.02.
Values may be sent and summed in bfloat16 or wider, within the bound.
No kernel may reach another device: no remote copies, remote signals or barrier semaphores. Data moves between devices by JAX's collectives and lax.ppermute only.
A program may use at most 64 MiB of HBM per device.

v0:
```python
import jax
import jax.numpy as jnp
from jax import lax
from jax.sharding import PartitionSpec as P

DH_T = 128
DH_S = 256
WINDOW = 1024


teacher_scale = 144.0 ** (-0.5)
negative = -1e30


def shifted(value, axis, by):
    length = lax.axis_size(axis)
    pairs = [(i, i + by) for i in range(length) if 0 <= i + by < length]
    return lax.ppermute(value, axis, pairs)


def for_sending(value):

    def short(part):
        return part.astype(jnp.bfloat16) if part.dtype == jnp.float32 else part

    return jax.tree.map(short, value)


def window_probs(queries, keys_all, marks_query, marks_all, heads, depth, scale, block_rows):
    query_part = queries.reshape(block_rows, heads, depth)
    key_part = keys_all.reshape(block_rows + WINDOW, heads, depth)
    scores = (
        jnp.einsum("qhd,khd->hqk", query_part, key_part, preferred_element_type=jnp.float32) * scale
    )
    row_index = lax.broadcasted_iota(jnp.int32, (block_rows, block_rows + WINDOW), 0)
    col_index = lax.broadcasted_iota(jnp.int32, (block_rows, block_rows + WINDOW), 1)
    same_doc = marks_query[:, None] == marks_all[None, :]
    allowed = same_doc & (col_index > row_index) & (col_index <= row_index + WINDOW)
    highest = jnp.max(jnp.where(allowed[None], scores, negative), axis=-1, keepdims=True)
    weights = jnp.where(allowed[None], jnp.exp(scores - highest), 0.0)
    totals = jnp.sum(weights, axis=-1, keepdims=True)
    probability = weights / totals
    return (probability, query_part, key_part, highest, totals)


def mix_values(probability, values_all, block_rows, heads, depth):
    value_part = values_all.reshape(block_rows + WINDOW, heads, depth)
    rounded = probability.astype(jnp.bfloat16)
    mixed = jnp.einsum("hqk,khd->qhd", rounded, value_part, preferred_element_type=jnp.float32)
    return (mixed.astype(jnp.bfloat16).reshape(block_rows, heads * depth), rounded, value_part)


def shards(
    teacher_query,
    teacher_key,
    teacher_value,
    student_query,
    student_key,
    student_value,
    segment_ids,
    language_ids,
    language_weight,
    teacher_out_proj,
    student_out_proj,
    match_proj,
):
    tokens_here = teacher_query.shape[0]
    reach = WINDOW // tokens_here
    block_rows = min(tokens_here, 512)
    starts = list(range(0, tokens_here, block_rows))
    heads_t = teacher_query.shape[1] // DH_T
    heads_s = student_query.shape[1] // DH_S
    student_scale = DH_S ** (-0.5)
    doc_marks = segment_ids + 1
    local_part = (teacher_key, teacher_value, student_key, student_value, doc_marks)
    arrived = [
        shifted(
            (local_part[0], local_part[1], local_part[2], local_part[3], local_part[4]),
            "seq",
            distance,
        )
        for distance in range(reach, 0, -1)
    ]
    joined = [
        jnp.concatenate([incoming[member] for incoming in arrived] + [local_part[member]], 0)
        for member in range(5)
    ]
    keys_teacher, values_teacher, keys_student, values_student, marks_all = joined
    teacher_blocks = []
    for first in starts:
        probability, query_part, key_part, highest, totals = window_probs(
            teacher_query,
            keys_teacher,
            doc_marks,
            marks_all,
            heads_t,
            DH_T,
            teacher_scale,
            block_rows,
        )
        mixed, rounded, value_part = mix_values(
            probability, values_teacher, block_rows, heads_t, DH_T
        )
        teacher_blocks.append(mixed)
    teacher_mix = teacher_blocks[0]
    target_cols = lax.dot_general(
        lax.all_gather(teacher_mix, "head", axis=1, tiled=True),
        teacher_out_proj,
        (((1,), (1,)), ((), ())),
        preferred_element_type=jnp.float32,
    ).astype(jnp.bfloat16)
    saved = []
    student_blocks = []
    highest_list = []
    totals_list = []
    for first in starts:
        probability, query_part, key_part, highest, totals = window_probs(
            student_query,
            keys_student,
            doc_marks,
            marks_all,
            heads_s,
            DH_S,
            student_scale,
            block_rows,
        )
        mixed, rounded, value_part = mix_values(
            probability, values_student, block_rows, heads_s, DH_S
        )
        student_blocks.append(mixed)
        highest_list.append(highest[..., 0])
        totals_list.append(totals[..., 0])
        saved.append((probability, rounded, query_part, key_part, value_part))
    student_mix = student_blocks[0]
    share_rows = tokens_here // lax.axis_size("head")
    residual = lax.psum_scatter(
        (
            jnp.dot(student_mix, student_out_proj, preferred_element_type=jnp.float32)
            - jnp.dot(target_cols, match_proj, preferred_element_type=jnp.float32)
        ).astype(jnp.bfloat16),
        "head",
        scatter_dimension=0,
        tiled=True,
    ).astype(jnp.float32)
    my_langs = lax.dynamic_slice_in_dim(
        language_ids, lax.axis_index("head") * share_rows, share_rows, 0
    )
    lang_table = lax.broadcasted_iota(jnp.int32, (share_rows, language_weight.shape[0]), 1)
    token_weight = jnp.sum(
        jnp.where(my_langs[:, None] == lang_table, language_weight[None, :], 0.0), axis=1
    )
    grad_mix = (token_weight[:, None] * residual).astype(jnp.bfloat16)
    grad_heads = lax.dot_general(
        lax.all_gather(grad_mix, "head", axis=0, tiled=True),
        student_out_proj,
        (((1,), (1,)), ((), ())),
        preferred_element_type=jnp.float32,
    ).astype(jnp.bfloat16)
    width_s = student_key.shape[1]
    key_grads = jnp.zeros((tokens_here + WINDOW, width_s), jnp.float32)
    value_grads = jnp.zeros((tokens_here + WINDOW, width_s), jnp.float32)
    query_blocks = []
    inner_list = []
    for first, stored in zip(starts, saved):
        probability, rounded, query_part, key_part, value_part = stored
        grad_part = grad_heads.reshape(block_rows, heads_s, DH_S)
        grad_probs = jnp.einsum(
            "qhd,khd->hqk", grad_part, value_part, preferred_element_type=jnp.float32
        )
        inner = jnp.sum(probability * grad_probs, axis=-1, keepdims=True)
        inner_list.append(inner[..., 0])
        grad_scores = (probability * (grad_probs - inner)).astype(jnp.bfloat16)
        grad_q = student_scale * jnp.einsum(
            "hqk,khd->qhd", grad_scores, key_part, preferred_element_type=jnp.float32
        )
        grad_k = student_scale * jnp.einsum(
            "hqk,qhd->khd", grad_scores, query_part, preferred_element_type=jnp.float32
        )
        grad_v = jnp.einsum("hqk,qhd->khd", rounded, grad_part, preferred_element_type=jnp.float32)
        query_blocks.append(grad_q.reshape(block_rows, width_s))
        key_grads = key_grads.at[first : first + block_rows + WINDOW].add(
            grad_k.reshape(block_rows + WINDOW, width_s)
        )
        value_grads = value_grads.at[first : first + block_rows + WINDOW].add(
            grad_v.reshape(block_rows + WINDOW, width_s)
        )
    own_keys = key_grads[WINDOW:]
    own_values = value_grads[WINDOW:]
    for distance in range(1, reach + 1):
        begin = (reach - distance) * tokens_here
        moved = shifted(
            for_sending(
                (key_grads[begin : begin + tokens_here], value_grads[begin : begin + tokens_here])
            ),
            "seq",
            -distance,
        )
        own_keys = own_keys + moved[0]
        own_values = own_values + moved[1]
    return (query_blocks[0], own_keys, own_values)


def solution(mesh):
    in_specs = (
        P("seq", "head"),
        P("seq", "head"),
        P("seq", "head"),
        P("seq", "head"),
        P("seq", "head"),
        P("seq", "head"),
        P("seq"),
        P("seq"),
        P(),
        P("head", None),
        P("head", None),
        P("head", None),
    )
    out_specs = (P("seq", "head"), P("seq", "head"), P("seq", "head"))
    return jax.shard_map(shards, mesh=mesh, in_specs=in_specs, out_specs=out_specs, check_vma=False)
```

profile of v0, /device:TPU:49, one launch (start us, length us, event | category | flops | bytes accessed | tf_op | source)
XLA Modules:
  0.0 392.7 jit_solution(14988951981614553780)
XLA Ops:
  8.0 10.6 %collective-permute-start.8 = (s32[128]{0:T(128)S(1)}, s32[128]{0:T(128)S(1)}, u32[]{:S(2)}, u32[]{:S(2)}) collective-permute-start(s32[128]{0:T(128)S(1)} %broadcast_add_fusion), channel_id=1, source_target_pairs={{0,64},{8,72},{16,80},{24,88},{32,96},{40,104},{48,112},{56,120},{... | collective-permute-start | bytes 1544 | tf_op jit(solution)/shard_map/ppermute | solution.py:18
  18.7 11.5 %collective-permute-start.9 = (s32[128]{0:T(128)S(1)}, s32[128]{0:T(128)S(1)}, u32[]{:S(2)}, u32[]{:S(2)}) collective-permute-start(s32[128]{0:T(128)S(1)} %broadcast_add_fusion), channel_id=1, source_target_pairs={{0,56},{8,64},{16,72},{24,80},{32,88},{40,96},{48,104},{56,112},{6... | collective-permute-start | bytes 1544 | tf_op jit(solution)/shard_map/ppermute | solution.py:18
  30.2 4.9 %collective-permute-start.10 = (s32[128]{0:T(128)S(1)}, s32[128]{0:T(128)S(1)}, u32[]{:S(2)}, u32[]{:S(2)}) collective-permute-start(s32[128]{0:T(128)S(1)} %broadcast_add_fusion), channel_id=1, source_target_pairs={{0,48},{8,56},{16,64},{24,72},{32,80},{40,88},{48,96},{56,104},{64... | collective-permute-start | bytes 1544 | tf_op jit(solution)/shard_map/ppermute | solution.py:18
  35.1 3.7 collective-permute-start.11
  38.8 4.0 %collective-permute-start.12 = (s32[128]{0:T(128)S(1)}, s32[128]{0:T(128)S(1)}, u32[]{:S(2)}, u32[]{:S(2)}) collective-permute-start(s32[128]{0:T(128)S(1)} %broadcast_add_fusion), channel_id=1, source_target_pairs={{0,32},{8,40},{16,48},{24,56},{32,64},{40,72},{48,80},{56,88},{64,... | collective-permute-start | bytes 1544 | tf_op jit(solution)/shard_map/ppermute | solution.py:18
  63.4 7.2 %collective-permute-start.37 = (bf16[128,256]{0,1:T(8,128)(2,1)S(1)}, bf16[128,256]{0,1:T(8,128)(2,1)S(1)}, u32[]{:S(2)}, u32[]{:S(2)}) collective-permute-start(bf16[128,256]{0,1:T(8,128)(2,1)S(1)} %copy.40), channel_id=1, source_target_pairs={{0,24},{8,32},{16,40},{24,48},{32,56},{40,64},{48,72},{56,80},{64,... | collective-permute-start | bytes 196616 | tf_op jit(solution)/shard_map/ppermute | solution.py:18
  100.1 3.7 collective-permute-start.31
  104.4 4.8 %collective-permute-start = (bf16[128,256]{1,0:T(8,128)(2,1)}, bf16[128,256]{1,0:T(8,128)(2,1)}, u32[]{:S(2)}, u32[]{:S(2)}) collective-permute-start(bf16[128,256]{1,0:T(8,128)(2,1)} %param.24), channel_id=1, source_target_pairs={{0,64},{8,72},{16,80},{24,88},{32,96},{40,104},{48,112},{56,120},{... | collective-permute-start | bytes 196616 | tf_op jit(solution)/shard_map/ppermute | solution.py:18
  124.8 25.9 %all_gather.6 = bf16[128,2048]{0,1:T(8,128)(2,1)} all-gather(bf16[128,256]{0,1:T(8,128)(2,1)S(1)} %bitcast.128), channel_id=1, replica_groups=mesh['seq'=128,'head'=8] {'head'}, dimensions={1}, use_global_device_ids=true | all-gather | bytes 589824 | tf_op jit(solution)/shard_map/all_gather | solution.py:107
  150.6 7.6 %collective-permute-start.5 = (bf16[128,256]{1,0:T(8,128)(2,1)}, bf16[128,256]{1,0:T(8,128)(2,1)S(1)}, u32[]{:S(2)}, u32[]{:S(2)}) collective-permute-start(bf16[128,256]{1,0:T(8,128)(2,1)} %param.24), channel_id=1, source_target_pairs={{0,24},{8,32},{16,40},{24,48},{32,56},{40,64},{48,72},{56,80},{64,... | collective-permute-start | bytes 196616 | tf_op jit(solution)/shard_map/ppermute | solution.py:18
  177.9 7.4 %collective-permute-start.21 = (bf16[128,256]{1,0:T(8,128)(2,1)S(1)}, bf16[128,256]{1,0:T(8,128)(2,1)S(1)}, u32[]{:S(2)}, u32[]{:S(2)}) collective-permute-start(bf16[128,256]{1,0:T(8,128)(2,1)S(1)} %copy-done.10), channel_id=1, source_target_pairs={{0,24},{8,32},{16,40},{24,48},{32,56},{40,64},{48,72},{56,80},{64,... | collective-permute-start | bytes 196616 | tf_op jit(solution)/shard_map/ppermute | solution.py:18
  189.3 4.8 %collective-permute-start.23 = (bf16[128,256]{1,0:T(8,128)(2,1)S(1)}, bf16[128,256]{1,0:T(8,128)(2,1)S(1)}, u32[]{:S(2)}, u32[]{:S(2)}) collective-permute-start(bf16[128,256]{1,0:T(8,128)(2,1)S(1)} %copy-done.10), channel_id=1, source_target_pairs={{0,8},{8,16},{16,24},{24,32},{32,40},{40,48},{48,56},{56,64},{64,7... | collective-permute-start | bytes 196616 | tf_op jit(solution)/shard_map/ppermute | solution.py:18
  206.4 5.2 %fusion.1 = bf16[128,2304]{1,0:T(8,128)(2,1)} fusion(f32[128,2304]{1,0:T(8,128)} %fusion.11, bf16[576,2304]{1,0:T(8,128)(2,1)S(1)} %copy-done, bf16[576,2048]{1,0:T(8,128)(2,1)} %param.29, bf16[128,2048]{0,1:T(8,128)(2,1)} %all_gather.6), kind=kOutput, calls=%fused_computation.2 | convolution fusion | flops 642392064 | bytes 7307264 | tf_op jit(solution)/shard_map/dot_general | solution.py:139
  211.9 50.9 %reduce-scatter.2.cloned.1.call-done = bf16[16,2304]{1,0:T(8,128)(2,1)} async-done(((bf16[128,2304]{1,0:T(8,128)(2,1)}), bf16[16,2304]{1,0:T(8,128)(2,1)}) %reduce-scatter.2.cloned.1.call-update) | async-done | bytes 73744 | tf_op jit(solution)/shard_map/reduce_scatter | solution.py:136
  263.7 23.1 %all_gather.7 = bf16[128,2304]{1,0:T(8,128)(2,1)S(1)} all-gather(bf16[16,2304]{1,0:T(8,128)(2,1)S(1)} %multiply_convert_fusion.1), channel_id=1, replica_groups=mesh['seq'=128,'head'=8] {'head'}, dimensions={0}, use_global_device_ids=true | all-gather | bytes 663552 | tf_op jit(solution)/shard_map/all_gather | solution.py:154
  292.5 13.4 %collective-permute-start.48 = (bf16[128,256]{0,1:T(8,128)(2,1)S(1)}, bf16[128,256]{0,1:T(8,128)(2,1)S(1)}, u32[]{:S(2)}, u32[]{:S(2)}) collective-permute-start(bf16[128,256]{0,1:T(8,128)(2,1)S(1)} %get-tuple-element.52), channel_id=1, source_target_pairs={{8,0},{16,8},{24,16},{32,24},{40,32},{48,40},{56,48},{64,56},{72,6... | collective-permute-start | bytes 196616 | tf_op jit(solution)/shard_map/ppermute | solution.py:18
  305.9 8.8 %collective-permute-start.49 = (bf16[128,256]{0,1:T(8,128)(2,1)S(1)}, bf16[128,256]{0,1:T(8,128)(2,1)S(1)}, u32[]{:S(2)}, u32[]{:S(2)}) collective-permute-start(bf16[128,256]{0,1:T(8,128)(2,1)S(1)} %get-tuple-element.59), channel_id=1, source_target_pairs={{16,0},{24,8},{32,16},{40,24},{48,32},{56,40},{64,48},{72,56},{80,... | collective-permute-start | bytes 196616 | tf_op jit(solution)/shard_map/ppermute | solution.py:18
  317.7 3.7 collective-permute-start.51
  321.4 5.9 %collective-permute-start.52 = (bf16[128,256]{0,1:T(8,128)(2,1)S(1)}, bf16[128,256]{0,1:T(8,128)(2,1)S(1)}, u32[]{:S(2)}, u32[]{:S(2)}) collective-permute-start(bf16[128,256]{0,1:T(8,128)(2,1)S(1)} %get-tuple-element.56), channel_id=1, source_target_pairs={{40,0},{48,8},{56,16},{64,24},{72,32},{80,40},{88,48},{96,56},{104... | collective-permute-start | bytes 196616 | tf_op jit(solution)/shard_map/ppermute | solution.py:18
  334.4 6.9 %collective-permute-start.55 = (bf16[128,256]{0,1:T(8,128)(2,1)}, bf16[128,256]{0,1:T(8,128)(2,1)}, u32[]{:S(2)}, u32[]{:S(2)}) collective-permute-start(bf16[128,256]{0,1:T(8,128)(2,1)} %get-tuple-element.53), channel_id=1, source_target_pairs={{64,0},{72,8},{80,16},{88,24},{96,32},{104,40},{112,48},{120,56},{... | collective-permute-start | bytes 196616 | tf_op jit(solution)/shard_map/ppermute | solution.py:18
  351.8 4.9 %collective-permute-start.43 = (bf16[128,256]{1,0:T(8,128)(2,1)S(1)}, bf16[128,256]{1,0:T(8,128)(2,1)}, u32[]{:S(2)}, u32[]{:S(2)}) collective-permute-start(bf16[128,256]{1,0:T(8,128)(2,1)S(1)} %get-tuple-element.65), channel_id=1, source_target_pairs={{32,0},{40,8},{48,16},{56,24},{64,32},{72,40},{80,48},{88,56},{96,... | collective-permute-start | bytes 196616 | tf_op jit(solution)/shard_map/ppermute | solution.py:18
  356.7 3.9 collective-permute-start.44
  364.9 7.4 %collective-permute-start.47 = (bf16[128,256]{1,0:T(8,128)(2,1)S(1)}, bf16[128,256]{1,0:T(8,128)(2,1)}, u32[]{:S(2)}, u32[]{:S(2)}) collective-permute-start(bf16[128,256]{1,0:T(8,128)(2,1)S(1)} %get-tuple-element.61), channel_id=1, source_target_pairs={{64,0},{72,8},{80,16},{88,24},{96,32},{104,40},{112,48},{120,56},{... | collective-permute-start | bytes 196616 | tf_op jit(solution)/shard_map/ppermute | solution.py:18
  374.1 8.4 %collective-permute-done.46 = bf16[128,256]{1,0:T(8,128)(2,1)} collective-permute-done((bf16[128,256]{1,0:T(8,128)(2,1)S(1)}, bf16[128,256]{1,0:T(8,128)(2,1)}, u32[]{:S(2)}, u32[]{:S(2)}) %collective-permute-start.46) | collective-permute-done | bytes 65568 | tf_op jit(solution)/shard_map/ppermute | solution.py:18
  (192 shorter events, 139.1 us)
Async XLA Ops:
  7.2 255.6 %reduce-scatter.2.cloned.1.call-start = ((), (), s32[]{:S(2)}) async-start(), calls=%async_computation.1 | async-start | bytes 663552 | tf_op jit(solution)/shard_map/reduce_scatter | solution.py:136
  8.0 35.8 %collective-permute-start.8 = (s32[128]{0:T(128)S(1)}, s32[128]{0:T(128)S(1)}, u32[]{:S(2)}, u32[]{:S(2)}) collective-permute-start(s32[128]{0:T(128)S(1)} %broadcast_add_fusion), channel_id=1, source_target_pairs={{0,64},{8,72},{16,80},{24,88},{32,96},{40,104},{48,112},{56,120},{... | collective-permute-start | bytes 1544 | tf_op jit(solution)/shard_map/ppermute | solution.py:18
  18.7 27.7 %collective-permute-start.9 = (s32[128]{0:T(128)S(1)}, s32[128]{0:T(128)S(1)}, u32[]{:S(2)}, u32[]{:S(2)}) collective-permute-start(s32[128]{0:T(128)S(1)} %broadcast_add_fusion), channel_id=1, source_target_pairs={{0,56},{8,64},{16,72},{24,80},{32,88},{40,96},{48,104},{56,112},{6... | collective-permute-start | bytes 1544 | tf_op jit(solution)/shard_map/ppermute | solution.py:18
  57.2 21.6 %collective-permute-start.35 = (bf16[128,256]{0,1:T(8,128)(2,1)S(1)}, bf16[128,256]{0,1:T(8,128)(2,1)S(1)}, u32[]{:S(2)}, u32[]{:S(2)}) collective-permute-start(bf16[128,256]{0,1:T(8,128)(2,1)S(1)} %copy.40), channel_id=1, source_target_pairs={{0,40},{8,48},{16,56},{24,64},{32,72},{40,80},{48,88},{56,96},{64,... | collective-permute-start | bytes 196616 | tf_op jit(solution)/shard_map/ppermute | solution.py:18
  59.2 22.2 %collective-permute-start.36 = (bf16[128,256]{0,1:T(8,128)(2,1)S(1)}, bf16[128,256]{0,1:T(8,128)(2,1)S(1)}, u32[]{:S(2)}, u32[]{:S(2)}) collective-permute-start(bf16[128,256]{0,1:T(8,128)(2,1)S(1)} %copy.40), channel_id=1, source_target_pairs={{0,32},{8,40},{16,48},{24,56},{32,64},{40,72},{48,80},{56,88},{64,... | collective-permute-start | bytes 196616 | tf_op jit(solution)/shard_map/ppermute | solution.py:18
  63.4 20.3 %collective-permute-start.37 = (bf16[128,256]{0,1:T(8,128)(2,1)S(1)}, bf16[128,256]{0,1:T(8,128)(2,1)S(1)}, u32[]{:S(2)}, u32[]{:S(2)}) collective-permute-start(bf16[128,256]{0,1:T(8,128)(2,1)S(1)} %copy.40), channel_id=1, source_target_pairs={{0,24},{8,32},{16,40},{24,48},{32,56},{40,64},{48,72},{56,80},{64,... | collective-permute-start | bytes 196616 | tf_op jit(solution)/shard_map/ppermute | solution.py:18
  88.3 21.6 %collective-permute-start.28 = (bf16[128,256]{1,0:T(8,128)(2,1)S(1)}, bf16[128,256]{1,0:T(8,128)(2,1)S(1)}, u32[]{:S(2)}, u32[]{:S(2)}) collective-permute-start(bf16[128,256]{1,0:T(8,128)(2,1)S(1)} %copy-done.9), channel_id=1, source_target_pairs={{0,32},{8,40},{16,48},{24,56},{32,64},{40,72},{48,80},{56,88},{64,... | collective-permute-start | bytes 196616 | tf_op jit(solution)/shard_map/ppermute | solution.py:18
  92.3 20.1 %collective-permute-start.29 = (bf16[128,256]{1,0:T(8,128)(2,1)S(1)}, bf16[128,256]{1,0:T(8,128)(2,1)S(1)}, u32[]{:S(2)}, u32[]{:S(2)}) collective-permute-start(bf16[128,256]{1,0:T(8,128)(2,1)S(1)} %copy-done.9), channel_id=1, source_target_pairs={{0,24},{8,32},{16,40},{24,48},{32,56},{40,64},{48,72},{56,80},{64,... | collective-permute-start | bytes 196616 | tf_op jit(solution)/shard_map/ppermute | solution.py:18
  104.4 46.2 %collective-permute-start = (bf16[128,256]{1,0:T(8,128)(2,1)}, bf16[128,256]{1,0:T(8,128)(2,1)}, u32[]{:S(2)}, u32[]{:S(2)}) collective-permute-start(bf16[128,256]{1,0:T(8,128)(2,1)} %param.24), channel_id=1, source_target_pairs={{0,64},{8,72},{16,80},{24,88},{32,96},{40,104},{48,112},{56,120},{... | collective-permute-start | bytes 196616 | tf_op jit(solution)/shard_map/ppermute | solution.py:18
  109.9 49.2 %collective-permute-start.1 = (bf16[128,256]{1,0:T(8,128)(2,1)}, bf16[128,256]{1,0:T(8,128)(2,1)}, u32[]{:S(2)}, u32[]{:S(2)}) collective-permute-start(bf16[128,256]{1,0:T(8,128)(2,1)} %param.24), channel_id=1, source_target_pairs={{0,56},{8,64},{16,72},{24,80},{32,88},{40,96},{48,104},{56,112},{6... | collective-permute-start | bytes 196616 | tf_op jit(solution)/shard_map/ppermute | solution.py:18
  112.5 49.4 %collective-permute-start.2 = (bf16[128,256]{1,0:T(8,128)(2,1)}, bf16[128,256]{1,0:T(8,128)(2,1)}, u32[]{:S(2)}, u32[]{:S(2)}) collective-permute-start(bf16[128,256]{1,0:T(8,128)(2,1)} %param.24), channel_id=1, source_target_pairs={{0,48},{8,56},{16,64},{24,72},{32,80},{40,88},{48,96},{56,104},{64... | collective-permute-start | bytes 196616 | tf_op jit(solution)/shard_map/ppermute | solution.py:18
  115.0 50.1 %collective-permute-start.3 = (bf16[128,256]{1,0:T(8,128)(2,1)}, bf16[128,256]{1,0:T(8,128)(2,1)}, u32[]{:S(2)}, u32[]{:S(2)}) collective-permute-start(bf16[128,256]{1,0:T(8,128)(2,1)} %param.24), channel_id=1, source_target_pairs={{0,40},{8,48},{16,56},{24,64},{32,72},{40,80},{48,88},{56,96},{64,... | collective-permute-start | bytes 196616 | tf_op jit(solution)/shard_map/ppermute | solution.py:18
  117.7 50.3 %collective-permute-start.4 = (bf16[128,256]{1,0:T(8,128)(2,1)}, bf16[128,256]{1,0:T(8,128)(2,1)}, u32[]{:S(2)}, u32[]{:S(2)}) collective-permute-start(bf16[128,256]{1,0:T(8,128)(2,1)} %param.24), channel_id=1, source_target_pairs={{0,32},{8,40},{16,48},{24,56},{32,64},{40,72},{48,80},{56,88},{64,... | collective-permute-start | bytes 196616 | tf_op jit(solution)/shard_map/ppermute | solution.py:18
  150.6 20.1 %collective-permute-start.5 = (bf16[128,256]{1,0:T(8,128)(2,1)}, bf16[128,256]{1,0:T(8,128)(2,1)S(1)}, u32[]{:S(2)}, u32[]{:S(2)}) collective-permute-start(bf16[128,256]{1,0:T(8,128)(2,1)} %param.24), channel_id=1, source_target_pairs={{0,24},{8,32},{16,40},{24,48},{32,56},{40,64},{48,72},{56,80},{64,... | collective-permute-start | bytes 196616 | tf_op jit(solution)/shard_map/ppermute | solution.py:18
  172.6 22.1 %collective-permute-start.19 = (bf16[128,256]{1,0:T(8,128)(2,1)S(1)}, bf16[128,256]{1,0:T(8,128)(2,1)S(1)}, u32[]{:S(2)}, u32[]{:S(2)}) collective-permute-start(bf16[128,256]{1,0:T(8,128)(2,1)S(1)} %copy-done.10), channel_id=1, source_target_pairs={{0,40},{8,48},{16,56},{24,64},{32,72},{40,80},{48,88},{56,96},{64,... | collective-permute-start | bytes 196616 | tf_op jit(solution)/shard_map/ppermute | solution.py:18
  174.6 20.8 %collective-permute-start.20 = (bf16[128,256]{1,0:T(8,128)(2,1)S(1)}, bf16[128,256]{1,0:T(8,128)(2,1)S(1)}, u32[]{:S(2)}, u32[]{:S(2)}) collective-permute-start(bf16[128,256]{1,0:T(8,128)(2,1)S(1)} %copy-done.10), channel_id=1, source_target_pairs={{0,32},{8,40},{16,48},{24,56},{32,64},{40,72},{48,80},{56,88},{64,... | collective-permute-start | bytes 196616 | tf_op jit(solution)/shard_map/ppermute | solution.py:18
  292.5 36.6 %collective-permute-start.48 = (bf16[128,256]{0,1:T(8,128)(2,1)S(1)}, bf16[128,256]{0,1:T(8,128)(2,1)S(1)}, u32[]{:S(2)}, u32[]{:S(2)}) collective-permute-start(bf16[128,256]{0,1:T(8,128)(2,1)S(1)} %get-tuple-element.52), channel_id=1, source_target_pairs={{8,0},{16,8},{24,16},{32,24},{40,32},{48,40},{56,48},{64,56},{72,6... | collective-permute-start | bytes 196616 | tf_op jit(solution)/shard_map/ppermute | solution.py:18
  305.9 26.4 %collective-permute-start.49 = (bf16[128,256]{0,1:T(8,128)(2,1)S(1)}, bf16[128,256]{0,1:T(8,128)(2,1)S(1)}, u32[]{:S(2)}, u32[]{:S(2)}) collective-permute-start(bf16[128,256]{0,1:T(8,128)(2,1)S(1)} %get-tuple-element.59), channel_id=1, source_target_pairs={{16,0},{24,8},{32,16},{40,24},{48,32},{56,40},{64,48},{72,56},{80,... | collective-permute-start | bytes 196616 | tf_op jit(solution)/shard_map/ppermute | solution.py:18
  314.7 19.6 %collective-permute-start.50 = (bf16[128,256]{0,1:T(8,128)(2,1)S(1)}, bf16[128,256]{0,1:T(8,128)(2,1)S(1)}, u32[]{:S(2)}, u32[]{:S(2)}) collective-permute-start(bf16[128,256]{0,1:T(8,128)(2,1)S(1)} %get-tuple-element.58), channel_id=1, source_target_pairs={{24,0},{32,8},{40,16},{48,24},{56,32},{64,40},{72,48},{80,56},{88,... | collective-permute-start | bytes 196616 | tf_op jit(solution)/shard_map/ppermute | solution.py:18
  317.7 23.5 %collective-permute-start.51 = (bf16[128,256]{0,1:T(8,128)(2,1)S(1)}, bf16[128,256]{0,1:T(8,128)(2,1)S(1)}, u32[]{:S(2)}, u32[]{:S(2)}) collective-permute-start(bf16[128,256]{0,1:T(8,128)(2,1)S(1)} %get-tuple-element.57), channel_id=1, source_target_pairs={{32,0},{40,8},{48,16},{56,24},{64,32},{72,40},{80,48},{88,56},{96,... | collective-permute-start | bytes 196616 | tf_op jit(solution)/shard_map/ppermute | solution.py:18
  321.4 23.0 %collective-permute-start.52 = (bf16[128,256]{0,1:T(8,128)(2,1)S(1)}, bf16[128,256]{0,1:T(8,128)(2,1)S(1)}, u32[]{:S(2)}, u32[]{:S(2)}) collective-permute-start(bf16[128,256]{0,1:T(8,128)(2,1)S(1)} %get-tuple-element.56), channel_id=1, source_target_pairs={{40,0},{48,8},{56,16},{64,24},{72,32},{80,40},{88,48},{96,56},{104... | collective-permute-start | bytes 196616 | tf_op jit(solution)/shard_map/ppermute | solution.py:18
  334.4 22.3 %collective-permute-start.55 = (bf16[128,256]{0,1:T(8,128)(2,1)}, bf16[128,256]{0,1:T(8,128)(2,1)}, u32[]{:S(2)}, u32[]{:S(2)}) collective-permute-start(bf16[128,256]{0,1:T(8,128)(2,1)} %get-tuple-element.53), channel_id=1, source_target_pairs={{64,0},{72,8},{80,16},{88,24},{96,32},{104,40},{112,48},{120,56},{... | collective-permute-start | bytes 196616 | tf_op jit(solution)/shard_map/ppermute | solution.py:18
  351.8 22.3 %collective-permute-start.43 = (bf16[128,256]{1,0:T(8,128)(2,1)S(1)}, bf16[128,256]{1,0:T(8,128)(2,1)}, u32[]{:S(2)}, u32[]{:S(2)}) collective-permute-start(bf16[128,256]{1,0:T(8,128)(2,1)S(1)} %get-tuple-element.65), channel_id=1, source_target_pairs={{32,0},{40,8},{48,16},{56,24},{64,32},{72,40},{80,48},{88,56},{96,... | collective-permute-start | bytes 196616 | tf_op jit(solution)/shard_map/ppermute | solution.py:18
  362.6 19.9 %collective-permute-start.46 = (bf16[128,256]{1,0:T(8,128)(2,1)S(1)}, bf16[128,256]{1,0:T(8,128)(2,1)}, u32[]{:S(2)}, u32[]{:S(2)}) collective-permute-start(bf16[128,256]{1,0:T(8,128)(2,1)S(1)} %get-tuple-element.62), channel_id=1, source_target_pairs={{56,0},{64,8},{72,16},{80,24},{88,32},{96,40},{104,48},{112,56},{1... | collective-permute-start | bytes 196616 | tf_op jit(solution)/shard_map/ppermute | solution.py:18
  (46 other events, 1021.4 us)
Sparse Core Ops, SparseCore 0:
  211.7 51.0 reduce-scatter.1
where the time goes:
time: 395 us; the launch traced here: 393 us
  starting transfers between devices  208 us (53%)
  waiting for transfers between devices  74.2 us (19%)
  blocking collectives  49 us (12%)
  local copies, waits for them, and re-layouts  23.3 us (6%)
  matrix products  16.3 us (4%)
  between operations  15 us (4%)
  other arithmetic  6.9 us (2%)
    ppermute x56, starting transfers between devices, shifted(): return lax.ppermute(value, axis, pairs)  208 us
    reduce_scatter x1, waiting for transfers between devices, shards(): lax.psum_scatter((jnp.dot(student_mix, student_out_proj, preferred_elemen...  50.9 us
    all_gather x1, blocking collectives, shards(): lax.all_gather(teacher_mix, 'head', axis=1, tiled=True)  25.9 us
    ppermute x56, waiting for transfers between devices, shifted(): return lax.ppermute(value, axis, pairs)  23.2 us
    all_gather x1, blocking collectives, shards(): lax.all_gather(grad_mix, 'head', axis=0, tiled=True)  23.1 us
    unnamed x69, local copies, waits for them, and re-layouts  17.5 us
  transfers between devices with their start and end apart: 57, of which 15 were waited for; matrix products, arithmetic and copies ran while one was open for 7% of the time, Pallas kernels for 0%

commit v1 on v0

v1 whole, which is shorter than its diff:
```python
import jax
import jax.numpy as jnp
from jax import lax
from jax.sharding import PartitionSpec as P

DH_T = 128
DH_S = 256
WINDOW = 1024


teacher_scale = 144.0 ** (-0.5)
negative = -1e30


def shifted(value, axis, by):
    length = lax.axis_size(axis)
    pairs = [(i, i + by) for i in range(length) if 0 <= i + by < length]
    return lax.ppermute(value, axis, pairs)


def swapped(value, axis, bit):
    length = lax.axis_size(axis)
    return lax.ppermute(value, axis, [(i, i ^ bit) for i in range(length)])


def gather_doubling(value, axis, along):
    size = lax.axis_size(axis)
    me = lax.axis_index(axis)
    bit = 1
    while bit < size:
        incoming = swapped(value, axis, bit)
        upper = (me // bit) % 2 == 1
        value = jnp.where(
            upper,
            jnp.concatenate([incoming, value], along),
            jnp.concatenate([value, incoming], along),
        )
        bit *= 2
    return value


def scatter_halving(value, axis):
    size = lax.axis_size(axis)
    me = lax.axis_index(axis)
    bit = size // 2
    while bit >= 1:
        half = value.shape[0] // 2
        low, high = value[:half], value[half:]
        upper = (me // bit) % 2 == 1
        send = jnp.where(upper, low, high)
        keep = jnp.where(upper, high, low)
        incoming = swapped(send.astype(jnp.bfloat16), axis, bit)
        value = keep + incoming.astype(jnp.float32)
        bit //= 2
    return value


def window_probs(queries, keys_all, marks_query, marks_all, heads, depth, scale, block_rows):
    query_part = queries.reshape(block_rows, heads, depth)
    key_part = keys_all.reshape(block_rows + WINDOW, heads, depth)
    scores = (
        jnp.einsum("qhd,khd->hqk", query_part, key_part, preferred_element_type=jnp.float32) * scale
    )
    row_index = lax.broadcasted_iota(jnp.int32, (block_rows, block_rows + WINDOW), 0)
    col_index = lax.broadcasted_iota(jnp.int32, (block_rows, block_rows + WINDOW), 1)
    same_doc = marks_query[:, None] == marks_all[None, :]
    allowed = same_doc & (col_index > row_index) & (col_index <= row_index + WINDOW)
    highest = jnp.max(jnp.where(allowed[None], scores, negative), axis=-1, keepdims=True)
    weights = jnp.where(allowed[None], jnp.exp(scores - highest), 0.0)
    totals = jnp.sum(weights, axis=-1, keepdims=True)
    probability = weights / totals
    return (probability, query_part, key_part)


def mix_values(probability, values_all, block_rows, heads, depth):
    value_part = values_all.reshape(block_rows + WINDOW, heads, depth)
    rounded = probability.astype(jnp.bfloat16)
    mixed = jnp.einsum("hqk,khd->qhd", rounded, value_part, preferred_element_type=jnp.float32)
    return (mixed.astype(jnp.bfloat16).reshape(block_rows, heads * depth), rounded, value_part)


def shards(
    teacher_query,
    teacher_key,
    teacher_value,
    student_query,
    student_key,
    student_value,
    segment_ids,
    language_ids,
    language_weight,
    teacher_out_proj,
    student_out_proj,
    match_proj,
):
    rows = teacher_query.shape[0]
    width = teacher_key.shape[1]
    reach = WINDOW // rows
    steps = reach // 2
    heads_t = teacher_query.shape[1] // DH_T
    heads_s = student_query.shape[1] // DH_S
    student_scale = DH_S ** (-0.5)
    doc_marks = segment_ids + 1
    mark_rows = jnp.pad(doc_marks.astype(jnp.bfloat16), (0, 8 * width - rows)).reshape(8, width)
    own = jnp.concatenate([teacher_key, teacher_value, student_key, student_value, mark_rows], 0)
    chain = [own]
    for _ in range(steps):
        chain.append(shifted(chain[-1], "seq", 2))
    core = lax.axis_index("seq") % 2
    stacked = jnp.stack(chain)
    partner = swapped(lax.dynamic_slice_in_dim(stacked, core, steps, 0), "seq", 1)
    pieces = []
    for k in range(steps, 0, -1):
        pieces.append(chain[k])
        pieces.append(partner[k - 1])
    pieces.append(own)
    window = jnp.stack(pieces)
    span = window.shape[0] * rows
    keys_teacher = window[:, 0:rows].reshape(span, width)
    values_teacher = window[:, rows : 2 * rows].reshape(span, width)
    keys_student = window[:, 2 * rows : 3 * rows].reshape(span, width)
    values_student = window[:, 3 * rows : 4 * rows].reshape(span, width)
    marks_all = (
        window[:, 4 * rows :].reshape(window.shape[0], 8 * width)[:, :rows].reshape(span)
    ).astype(jnp.int32)

    probability, _, _ = window_probs(
        teacher_query, keys_teacher, doc_marks, marks_all, heads_t, DH_T, teacher_scale, rows
    )
    teacher_mix, _, _ = mix_values(probability, values_teacher, rows, heads_t, DH_T)
    target_cols = lax.dot_general(
        gather_doubling(teacher_mix, "head", 1),
        teacher_out_proj,
        (((1,), (1,)), ((), ())),
        preferred_element_type=jnp.float32,
    ).astype(jnp.bfloat16)

    probability, query_part, key_part = window_probs(
        student_query, keys_student, doc_marks, marks_all, heads_s, DH_S, student_scale, rows
    )
    student_mix, rounded, value_part = mix_values(
        probability, values_student, rows, heads_s, DH_S
    )
    share_rows = rows // lax.axis_size("head")
    residual = scatter_halving(
        jnp.dot(student_mix, student_out_proj, preferred_element_type=jnp.float32)
        - jnp.dot(target_cols, match_proj, preferred_element_type=jnp.float32),
        "head",
    )
    my_langs = lax.dynamic_slice_in_dim(
        language_ids, lax.axis_index("head") * share_rows, share_rows, 0
    )
    lang_table = lax.broadcasted_iota(jnp.int32, (share_rows, language_weight.shape[0]), 1)
    token_weight = jnp.sum(
        jnp.where(my_langs[:, None] == lang_table, language_weight[None, :], 0.0), axis=1
    )
    grad_mix = (token_weight[:, None] * residual).astype(jnp.bfloat16)
    grad_heads = lax.dot_general(
        gather_doubling(grad_mix, "head", 0),
        student_out_proj,
        (((1,), (1,)), ((), ())),
        preferred_element_type=jnp.float32,
    ).astype(jnp.bfloat16)

    grad_part = grad_heads.reshape(rows, heads_s, DH_S)
    grad_probs = jnp.einsum(
        "qhd,khd->hqk", grad_part, value_part, preferred_element_type=jnp.float32
    )
    inner = jnp.sum(probability * grad_probs, axis=-1, keepdims=True)
    grad_scores = (probability * (grad_probs - inner)).astype(jnp.bfloat16)
    grad_q = student_scale * jnp.einsum(
        "hqk,khd->qhd", grad_scores, key_part, preferred_element_type=jnp.float32
    )
    grad_k = student_scale * jnp.einsum(
        "hqk,qhd->khd", grad_scores, query_part, preferred_element_type=jnp.float32
    )
    grad_v = jnp.einsum("hqk,qhd->khd", rounded, grad_part, preferred_element_type=jnp.float32)
    blocks = span // rows
    grads = jnp.concatenate(
        [grad_k.reshape(blocks, rows, width), grad_v.reshape(blocks, rows, width)], 1
    )
    from_partner = swapped(grads[1::2], "seq", 1)
    nothing = jnp.zeros_like(from_partner[:1])
    added = jnp.where(
        core == 1,
        jnp.concatenate([from_partner, nothing], 0),
        jnp.concatenate([nothing, from_partner], 0),
    )
    even = grads[0::2] + added
    total = even[0]
    for k in range(1, steps + 1):
        total = even[k] + shifted(total.astype(jnp.bfloat16), "seq", -2).astype(jnp.float32)
    return (grad_q.reshape(rows, width), total[:rows], total[rows:])


def solution(mesh):
    in_specs = (
        P("seq", "head"),
        P("seq", "head"),
        P("seq", "head"),
        P("seq", "head"),
        P("seq", "head"),
        P("seq", "head"),
        P("seq"),
        P("seq"),
        P(),
        P("head", None),
        P("head", None),
        P("head", None),
    )
    out_specs = (P("seq", "head"), P("seq", "head"), P("seq", "head"))
    return jax.shard_map(shards, mesh=mesh, in_specs=in_specs, out_specs=out_specs, check_vma=False)
```

time: 395 us -> 258 us (0.65)
  the two profiles are of different devices: /device:TPU:49 before, /device:TPU:46 now
where the time goes in v1:
time: 258 us; the launch traced here: 257 us
  waiting for transfers between devices  116 us (45%)
  starting transfers between devices  76.1 us (29%)
  local copies, waits for them, and re-layouts  37.4 us (14%)
  matrix products  15.5 us (6%)
  other arithmetic  10.6 us (4%)
    ppermute x8, waiting for transfers between devices, shifted(): return lax.ppermute(value, axis, pairs)  75.6 us
    ppermute x8, starting transfers between devices, shifted(): return lax.ppermute(value, axis, pairs)  41.6 us
    ppermute x11, waiting for transfers between devices, swapped(): return lax.ppermute(value, axis, [(i, i ^ bit) for i in range(length)])  40.3 us
    ppermute x11, starting transfers between devices, swapped(): return lax.ppermute(value, axis, [(i, i ^ bit) for i in range(length)])  34.4 us
    unnamed x56, local copies, waits for them, and re-layouts  19.6 us
    dot_general x1, matrix products, shards(): jnp.dot(target_cols, match_proj, preferred_element_type=jnp.float32)  5.4 us
  transfers between devices with their start and end apart: 19, of which 19 were waited for; matrix products, arithmetic and copies ran while one was open for 4% of the time, Pallas kernels for 0%

profile of v1, /device:TPU:46, one launch (start us, length us, event | category | flops | bytes accessed | tf_op | source)
XLA Modules:
  0.0 256.6 jit_solution(6401349327613257080)
XLA Ops:
  4.9 4.3 %collective-permute-start = (bf16[520,256]{1,0:T(8,128)(2,1)S(1)}, bf16[520,256]{1,0:T(8,128)(2,1)S(1)}, u32[]{:S(2)}, u32[]{:S(2)}) collective-permute-start(bf16[520,256]{1,0:T(8,128)(2,1)S(1)} %constant_dynamic-update-slice_fusion), channel_id=1, source_target_pairs={{0,16},{8,24},{16,32},{24,40},{32,48},{40,56},{48,64},{56,72},{64,... | collective-permute-start | bytes 798728 | tf_op jit(solution)/shard_map/ppermute | solution.py:18
  9.1 26.8 %collective-permute-done = bf16[520,256]{1,0:T(8,128)(2,1)S(1)} collective-permute-done((bf16[520,256]{1,0:T(8,128)(2,1)S(1)}, bf16[520,256]{1,0:T(8,128)(2,1)S(1)}, u32[]{:S(2)}, u32[]{:S(2)}) %collective-permute-start) | collective-permute-done | bytes 266272 | tf_op jit(solution)/shard_map/ppermute | solution.py:18
  37.8 15.9 %collective-permute-done.1 = bf16[520,256]{1,0:T(8,128)(2,1)S(1)} collective-permute-done((bf16[520,256]{1,0:T(8,128)(2,1)S(1)}, bf16[520,256]{1,0:T(8,128)(2,1)S(1)}, u32[]{:S(2)}, u32[]{:S(2)}) %collective-permute-start.1) | collective-permute-done | bytes 266272 | tf_op jit(solution)/shard_map/ppermute | solution.py:18
  57.1 11.5 %collective-permute-done.2 = bf16[520,256]{1,0:T(8,128)(2,1)} collective-permute-done((bf16[520,256]{1,0:T(8,128)(2,1)S(1)}, bf16[520,256]{1,0:T(8,128)(2,1)}, u32[]{:S(2)}, u32[]{:S(2)}) %collective-permute-start.2) | collective-permute-done | bytes 266272 | tf_op jit(solution)/shard_map/ppermute | solution.py:18
  73.0 9.6 %collective-permute-done.3 = bf16[520,256]{1,0:T(8,128)(2,1)S(1)} collective-permute-done((bf16[520,256]{1,0:T(8,128)(2,1)}, bf16[520,256]{1,0:T(8,128)(2,1)S(1)}, u32[]{:S(2)}, u32[]{:S(2)}) %collective-permute-start.3) | collective-permute-done | bytes 266272 | tf_op jit(solution)/shard_map/ppermute | solution.py:18
  118.8 3.3 %collective-permute-start.6 = (bf16[128,512]{0,1:T(8,128)(2,1)S(1)}, bf16[128,512]{0,1:T(8,128)(2,1)S(1)}, u32[]{:S(2)}, u32[]{:S(2)}) collective-permute-start(bf16[128,512]{0,1:T(8,128)(2,1)S(1)} %maximum_select_fusion.8), channel_id=1, source_target_pairs={{0,2},{1,3},{2,0},{3,1},{4,6},{5,7},{6,4},{7,5},{8,10},{9,11},{10,... | collective-permute-start | bytes 393224 | tf_op jit(solution)/shard_map/ppermute | solution.py:23
  122.5 4.7 %collective-permute-done.6 = bf16[128,512]{0,1:T(8,128)(2,1)S(1)} collective-permute-done((bf16[128,512]{0,1:T(8,128)(2,1)S(1)}, bf16[128,512]{0,1:T(8,128)(2,1)S(1)}, u32[]{:S(2)}, u32[]{:S(2)}) %collective-permute-start.6) | collective-permute-done | bytes 131104 | tf_op jit(solution)/shard_map/ppermute | solution.py:23
  127.3 4.2 %collective-permute-start.7 = (bf16[128,1024]{0,1:T(8,128)(2,1)S(1)}, bf16[128,1024]{0,1:T(8,128)(2,1)}, u32[]{:S(2)}, u32[]{:S(2)}) collective-permute-start(bf16[128,1024]{0,1:T(8,128)(2,1)S(1)} %maximum_select_fusion.6), channel_id=1, source_target_pairs={{0,4},{1,5},{2,6},{3,7},{4,0},{5,1},{6,2},{7,3},{8,12},{9,13},{10,... | collective-permute-start | bytes 786440 | tf_op jit(solution)/shard_map/ppermute | solution.py:23
  131.5 3.4 %fusion.9 = f32[128,2304]{1,0:T(8,128)} fusion(bf16[256,2304]{1,0:T(8,128)(2,1)} %param.22, bf16[1152,256]{1,0:T(8,128)(2,1)S(1)} %bitcast.107, f32[128,1152]{0,1:T(8,128)} %copy-done.6, f32[128]{0:T(128)S(1)} %fusion.35, f32[128]{0:T(128)S(1)} %get-tuple-element.22, s32[128]{0:T(128)S(1)} %get-tuple-element.28, s32[1152]{0:T(1024)S(1)} %fusion.49, ...), kind=kOutput, calls=%fused_computation.23 | convolution fusion | flops 227852288 | bytes 3545600 | tf_op jit(solution)/shard_map/dot_general | solution.py:146
  135.9 5.4 %convolution_subtract_fusion = f32[128,2304]{1,0:T(8,128)} fusion(f32[128,2304]{1,0:T(8,128)} %fusion.9, bf16[576,2304]{1,0:T(8,128)(2,1)S(1)} %copy-done, bf16[576,2048]{1,0:T(8,128)(2,1)} %param.21, bf16[128,1024]{0,1:T(8,128)(2,1)S(1)} %maximum_select_fusion.6, bf16[128,1024]{0,1:T(8,128)(2,1)} %collective-permute-done.7, pred[]{:T(512)S(6)} %eq.64), kind=kOutput, calls=%fused_computation.1 | convolution fusion | flops 644456448 | bytes 7897089 | tf_op jit(solution)/shard_map/dot_general | solution.py:147
  142.6 3.9 %collective-permute-start.8 = (bf16[64,2304]{1,0:T(8,128)(2,1)S(1)}, bf16[64,2304]{1,0:T(8,128)(2,1)S(1)}, u32[]{:S(2)}, u32[]{:S(2)}) collective-permute-start(bf16[64,2304]{1,0:T(8,128)(2,1)S(1)} %select_convert_fusion), channel_id=1, source_target_pairs={{0,4},{1,5},{2,6},{3,7},{4,0},{5,1},{6,2},{7,3},{8,12},{9,13},{10,... | collective-permute-start | bytes 884744 | tf_op jit(solution)/shard_map/ppermute | solution.py:23
  146.6 4.7 %collective-permute-done.8 = bf16[64,2304]{1,0:T(8,128)(2,1)S(1)} collective-permute-done((bf16[64,2304]{1,0:T(8,128)(2,1)S(1)}, bf16[64,2304]{1,0:T(8,128)(2,1)S(1)}, u32[]{:S(2)}, u32[]{:S(2)}) %collective-permute-start.8) | collective-permute-done | bytes 294944 | tf_op jit(solution)/shard_map/ppermute | solution.py:23
  152.6 3.3 %collective-permute-start.9 = (bf16[32,2304]{1,0:T(8,128)(2,1)S(1)}, bf16[32,2304]{1,0:T(8,128)(2,1)S(1)}, u32[]{:S(2)}, u32[]{:S(2)}) collective-permute-start(bf16[32,2304]{1,0:T(8,128)(2,1)S(1)} %select_convert_fusion.1), channel_id=1, source_target_pairs={{0,2},{1,3},{2,0},{3,1},{4,6},{5,7},{6,4},{7,5},{8,10},{9,11},{10,... | collective-permute-start | bytes 442376 | tf_op jit(solution)/shard_map/ppermute | solution.py:23
  156.8 5.2 %collective-permute-done.9 = bf16[32,2304]{1,0:T(8,128)(2,1)S(1)} collective-permute-done((bf16[32,2304]{1,0:T(8,128)(2,1)S(1)}, bf16[32,2304]{1,0:T(8,128)(2,1)S(1)}, u32[]{:S(2)}, u32[]{:S(2)}) %collective-permute-start.9) | collective-permute-done | bytes 147488 | tf_op jit(solution)/shard_map/ppermute | solution.py:23
  171.1 3.5 %collective-permute-done.11 = bf16[16,2304]{1,0:T(8,128)(2,1)S(1)} collective-permute-done((bf16[16,2304]{1,0:T(8,128)(2,1)S(1)}, bf16[16,2304]{1,0:T(8,128)(2,1)S(1)}, u32[]{:S(2)}, u32[]{:S(2)}) %collective-permute-start.11) | collective-permute-done | bytes 73760 | tf_op jit(solution)/shard_map/ppermute | solution.py:23
  174.6 3.6 %collective-permute-start.12 = (bf16[32,2304]{1,0:T(8,128)(2,1)S(1)}, bf16[32,2304]{1,0:T(8,128)(2,1)S(1)}, u32[]{:S(2)}, u32[]{:S(2)}) collective-permute-start(bf16[32,2304]{1,0:T(8,128)(2,1)S(1)} %maximum_select_fusion.7), channel_id=1, source_target_pairs={{0,2},{1,3},{2,0},{3,1},{4,6},{5,7},{6,4},{7,5},{8,10},{9,11},{10,... | collective-permute-start | bytes 442376 | tf_op jit(solution)/shard_map/ppermute | solution.py:23
  178.2 4.9 %collective-permute-done.12 = bf16[32,2304]{1,0:T(8,128)(2,1)S(1)} collective-permute-done((bf16[32,2304]{1,0:T(8,128)(2,1)S(1)}, bf16[32,2304]{1,0:T(8,128)(2,1)S(1)}, u32[]{:S(2)}, u32[]{:S(2)}) %collective-permute-start.12) | collective-permute-done | bytes 147488 | tf_op jit(solution)/shard_map/ppermute | solution.py:23
  183.2 4.1 %collective-permute-start.13 = (bf16[64,2304]{1,0:T(8,128)(2,1)S(1)}, bf16[64,2304]{1,0:T(8,128)(2,1)S(1)}, u32[]{:S(2)}, u32[]{:S(2)}) collective-permute-start(bf16[64,2304]{1,0:T(8,128)(2,1)S(1)} %maximum_select_fusion.5), channel_id=1, source_target_pairs={{0,4},{1,5},{2,6},{3,7},{4,0},{5,1},{6,2},{7,3},{8,12},{9,13},{10,... | collective-permute-start | bytes 884744 | tf_op jit(solution)/shard_map/ppermute | solution.py:23
  187.3 4.7 %collective-permute-done.13 = bf16[64,2304]{1,0:T(8,128)(2,1)S(1)} collective-permute-done((bf16[64,2304]{1,0:T(8,128)(2,1)S(1)}, bf16[64,2304]{1,0:T(8,128)(2,1)S(1)}, u32[]{:S(2)}, u32[]{:S(2)}) %collective-permute-start.13) | collective-permute-done | bytes 294944 | tf_op jit(solution)/shard_map/ppermute | solution.py:23
  205.0 3.0 %collective-permute-done.14 = f32[4,256,256]{2,1,0:T(8,128)} collective-permute-done((f32[4,256,256]{2,1,0:T(8,128)}, f32[4,256,256]{2,1,0:T(8,128)}, u32[]{:S(2)}, u32[]{:S(2)}) %collective-permute-start.14) | collective-permute-done | bytes 1048608 | tf_op jit(solution)/shard_map/ppermute | solution.py:23
  212.2 5.5 %collective-permute-done.15 = bf16[256,256]{1,0:T(8,128)(2,1)S(1)} collective-permute-done((bf16[256,256]{1,0:T(8,128)(2,1)S(1)}, bf16[256,256]{1,0:T(8,128)(2,1)S(1)}, u32[]{:S(2)}, u32[]{:S(2)}) %collective-permute-start.15) | collective-permute-done | bytes 131104 | tf_op jit(solution)/shard_map/ppermute | solution.py:18
  217.7 9.6 %collective-permute-start.16 = (bf16[256,256]{1,0:T(8,128)(2,1)S(1)}, bf16[256,256]{1,0:T(8,128)(2,1)S(1)}, u32[]{:S(2)}, u32[]{:S(2)}) collective-permute-start(bf16[256,256]{1,0:T(8,128)(2,1)S(1)} %fusion.37), channel_id=1, source_target_pairs={{16,0},{24,8},{32,16},{40,24},{48,32},{56,40},{64,48},{72,56},{80,... | collective-permute-start | bytes 393224 | tf_op jit(solution)/shard_map/ppermute | solution.py:18
  229.8 10.5 %collective-permute-start.17 = (bf16[256,256]{1,0:T(8,128)(2,1)S(1)}, bf16[256,256]{1,0:T(8,128)(2,1)S(1)}, u32[]{:S(2)}, u32[]{:S(2)}) collective-permute-start(bf16[256,256]{1,0:T(8,128)(2,1)S(1)} %fusion.39), channel_id=1, source_target_pairs={{16,0},{24,8},{32,16},{40,24},{48,32},{56,40},{64,48},{72,56},{80,... | collective-permute-start | bytes 393224 | tf_op jit(solution)/shard_map/ppermute | solution.py:18
  242.9 9.5 %collective-permute-start.18 = (bf16[256,256]{1,0:T(8,128)(2,1)S(1)}, bf16[256,256]{1,0:T(8,128)(2,1)S(1)}, u32[]{:S(2)}, u32[]{:S(2)}) collective-permute-start(bf16[256,256]{1,0:T(8,128)(2,1)S(1)} %fusion.41), channel_id=1, source_target_pairs={{16,0},{24,8},{32,16},{40,24},{48,32},{56,40},{64,48},{72,56},{80,... | collective-permute-start | bytes 393224 | tf_op jit(solution)/shard_map/ppermute | solution.py:18
  (118 shorter events, 90.4 us)
Async XLA Ops:
  0.6 135.3 %copy-start = (bf16[576,2304]{1,0:T(8,128)(2,1)S(1)}, bf16[576,2304]{1,0:T(8,128)(2,1)}, u32[]{:S(2)}) copy-start(bf16[576,2304]{1,0:T(8,128)(2,1)} %param.23) | copy-start | bytes 7962628
  4.9 31.0 %collective-permute-start = (bf16[520,256]{1,0:T(8,128)(2,1)S(1)}, bf16[520,256]{1,0:T(8,128)(2,1)S(1)}, u32[]{:S(2)}, u32[]{:S(2)}) collective-permute-start(bf16[520,256]{1,0:T(8,128)(2,1)S(1)} %constant_dynamic-update-slice_fusion), channel_id=1, source_target_pairs={{0,16},{8,24},{16,32},{24,40},{32,48},{40,56},{48,64},{56,72},{64,... | collective-permute-start | bytes 798728 | tf_op jit(solution)/shard_map/ppermute | solution.py:18
  35.9 17.9 %collective-permute-start.1 = (bf16[520,256]{1,0:T(8,128)(2,1)S(1)}, bf16[520,256]{1,0:T(8,128)(2,1)S(1)}, u32[]{:S(2)}, u32[]{:S(2)}) collective-permute-start(bf16[520,256]{1,0:T(8,128)(2,1)S(1)} %collective-permute-done), channel_id=1, source_target_pairs={{0,16},{8,24},{16,32},{24,40},{32,48},{40,56},{48,64},{56,72},{64,... | collective-permute-start | bytes 798728 | tf_op jit(solution)/shard_map/ppermute | solution.py:18
  53.8 14.9 %collective-permute-start.2 = (bf16[520,256]{1,0:T(8,128)(2,1)S(1)}, bf16[520,256]{1,0:T(8,128)(2,1)}, u32[]{:S(2)}, u32[]{:S(2)}) collective-permute-start(bf16[520,256]{1,0:T(8,128)(2,1)S(1)} %collective-permute-done.1), channel_id=1, source_target_pairs={{0,16},{8,24},{16,32},{24,40},{32,48},{40,56},{48,64},{56,72},{64,... | collective-permute-start | bytes 798728 | tf_op jit(solution)/shard_map/ppermute | solution.py:18
  68.7 13.9 %collective-permute-start.3 = (bf16[520,256]{1,0:T(8,128)(2,1)}, bf16[520,256]{1,0:T(8,128)(2,1)S(1)}, u32[]{:S(2)}, u32[]{:S(2)}) collective-permute-start(bf16[520,256]{1,0:T(8,128)(2,1)} %collective-permute-done.2), channel_id=1, source_target_pairs={{0,16},{8,24},{16,32},{24,40},{32,48},{40,56},{48,64},{56,72},{64,... | collective-permute-start | bytes 798728 | tf_op jit(solution)/shard_map/ppermute | solution.py:18
  85.6 4.9 %collective-permute-start.4 = (bf16[4,520,256]{2,1,0:T(8,128)(2,1)}, bf16[4,520,256]{2,1,0:T(8,128)(2,1)}, u32[]{:S(2)}, u32[]{:S(2)}) collective-permute-start(bf16[4,520,256]{2,1,0:T(8,128)(2,1)} %constant_dynamic-slice_fusion), channel_id=1, source_target_pairs={{0,8},{8,0},{16,24},{24,16},{32,40},{40,32},{48,56},{56,48},{64,72... | collective-permute-start | bytes 3194888 | tf_op jit(solution)/shard_map/ppermute | solution.py:23
  112.6 6.2 %collective-permute-start.5 = (bf16[128,256]{0,1:T(8,128)(2,1)S(1)}, bf16[128,256]{0,1:T(8,128)(2,1)S(1)}, u32[]{:S(2)}, u32[]{:S(2)}) collective-permute-start(bf16[128,256]{0,1:T(8,128)(2,1)S(1)} %bitcast.111), channel_id=1, source_target_pairs={{0,1},{1,0},{2,3},{3,2},{4,5},{5,4},{6,7},{7,6},{8,9},{9,8},{10,11... | collective-permute-start | bytes 196616 | tf_op jit(solution)/shard_map/ppermute | solution.py:23
  115.8 19.1 %copy-start.14 = (f32[128]{0:T(128)}, f32[128]{0:T(128)S(1)}, u32[]{:S(2)}) copy-start(f32[128]{0:T(128)S(1)} %get-tuple-element.22) | copy-start | bytes 1540
  118.8 8.4 %collective-permute-start.6 = (bf16[128,512]{0,1:T(8,128)(2,1)S(1)}, bf16[128,512]{0,1:T(8,128)(2,1)S(1)}, u32[]{:S(2)}, u32[]{:S(2)}) collective-permute-start(bf16[128,512]{0,1:T(8,128)(2,1)S(1)} %maximum_select_fusion.8), channel_id=1, source_target_pairs={{0,2},{1,3},{2,0},{3,1},{4,6},{5,7},{6,4},{7,5},{8,10},{9,11},{10,... | collective-permute-start | bytes 393224 | tf_op jit(solution)/shard_map/ppermute | solution.py:23
  127.3 8.7 %collective-permute-start.7 = (bf16[128,1024]{0,1:T(8,128)(2,1)S(1)}, bf16[128,1024]{0,1:T(8,128)(2,1)}, u32[]{:S(2)}, u32[]{:S(2)}) collective-permute-start(bf16[128,1024]{0,1:T(8,128)(2,1)S(1)} %maximum_select_fusion.6), channel_id=1, source_target_pairs={{0,4},{1,5},{2,6},{3,7},{4,0},{5,1},{6,2},{7,3},{8,12},{9,13},{10,... | collective-permute-start | bytes 786440 | tf_op jit(solution)/shard_map/ppermute | solution.py:23
  142.6 8.6 %collective-permute-start.8 = (bf16[64,2304]{1,0:T(8,128)(2,1)S(1)}, bf16[64,2304]{1,0:T(8,128)(2,1)S(1)}, u32[]{:S(2)}, u32[]{:S(2)}) collective-permute-start(bf16[64,2304]{1,0:T(8,128)(2,1)S(1)} %select_convert_fusion), channel_id=1, source_target_pairs={{0,4},{1,5},{2,6},{3,7},{4,0},{5,1},{6,2},{7,3},{8,12},{9,13},{10,... | collective-permute-start | bytes 884744 | tf_op jit(solution)/shard_map/ppermute | solution.py:23
  152.6 9.3 %collective-permute-start.9 = (bf16[32,2304]{1,0:T(8,128)(2,1)S(1)}, bf16[32,2304]{1,0:T(8,128)(2,1)S(1)}, u32[]{:S(2)}, u32[]{:S(2)}) collective-permute-start(bf16[32,2304]{1,0:T(8,128)(2,1)S(1)} %select_convert_fusion.1), channel_id=1, source_target_pairs={{0,2},{1,3},{2,0},{3,1},{4,6},{5,7},{6,4},{7,5},{8,10},{9,11},{10,... | collective-permute-start | bytes 442376 | tf_op jit(solution)/shard_map/ppermute | solution.py:23
  155.9 36.1 %copy-start.18 = (bf16[256,2304]{1,0:T(8,128)(2,1)S(1)}, bf16[256,2304]{1,0:T(8,128)(2,1)}, u32[]{:S(2)}) copy-start(bf16[256,2304]{1,0:T(8,128)(2,1)} %param.22) | copy-start | bytes 3538948
  162.0 6.2 %collective-permute-start.10 = (bf16[16,2304]{1,0:T(8,128)(2,1)S(1)}, bf16[16,2304]{1,0:T(8,128)(2,1)S(1)}, u32[]{:S(2)}, u32[]{:S(2)}) collective-permute-start(bf16[16,2304]{1,0:T(8,128)(2,1)S(1)} %select_convert_fusion.2), channel_id=1, source_target_pairs={{0,1},{1,0},{2,3},{3,2},{4,5},{5,4},{6,7},{7,6},{8,9},{9,8},{10,11... | collective-permute-start | bytes 221192 | tf_op jit(solution)/shard_map/ppermute | solution.py:23
  168.3 6.2 %collective-permute-start.11 = (bf16[16,2304]{1,0:T(8,128)(2,1)S(1)}, bf16[16,2304]{1,0:T(8,128)(2,1)S(1)}, u32[]{:S(2)}, u32[]{:S(2)}) collective-permute-start(bf16[16,2304]{1,0:T(8,128)(2,1)S(1)} %multiply_convert_fusion.1), channel_id=1, source_target_pairs={{0,1},{1,0},{2,3},{3,2},{4,5},{5,4},{6,7},{7,6},{8,9},{9,8},{10,11... | collective-permute-start | bytes 221192 | tf_op jit(solution)/shard_map/ppermute | solution.py:23
  174.6 8.5 %collective-permute-start.12 = (bf16[32,2304]{1,0:T(8,128)(2,1)S(1)}, bf16[32,2304]{1,0:T(8,128)(2,1)S(1)}, u32[]{:S(2)}, u32[]{:S(2)}) collective-permute-start(bf16[32,2304]{1,0:T(8,128)(2,1)S(1)} %maximum_select_fusion.7), channel_id=1, source_target_pairs={{0,2},{1,3},{2,0},{3,1},{4,6},{5,7},{6,4},{7,5},{8,10},{9,11},{10,... | collective-permute-start | bytes 442376 | tf_op jit(solution)/shard_map/ppermute | solution.py:23
  183.2 8.7 %collective-permute-start.13 = (bf16[64,2304]{1,0:T(8,128)(2,1)S(1)}, bf16[64,2304]{1,0:T(8,128)(2,1)S(1)}, u32[]{:S(2)}, u32[]{:S(2)}) collective-permute-start(bf16[64,2304]{1,0:T(8,128)(2,1)S(1)} %maximum_select_fusion.5), channel_id=1, source_target_pairs={{0,4},{1,5},{2,6},{3,7},{4,0},{5,1},{6,2},{7,3},{8,12},{9,13},{10,... | collective-permute-start | bytes 884744 | tf_op jit(solution)/shard_map/ppermute | solution.py:23
  203.0 4.9 %collective-permute-start.14 = (f32[4,256,256]{2,1,0:T(8,128)}, f32[4,256,256]{2,1,0:T(8,128)}, u32[]{:S(2)}, u32[]{:S(2)}) collective-permute-start(f32[4,256,256]{2,1,0:T(8,128)} %slice.93), channel_id=1, source_target_pairs={{0,8},{8,0},{16,24},{24,16},{32,40},{40,32},{48,56},{56,48},{64,72... | collective-permute-start | bytes 3145736 | tf_op jit(solution)/shard_map/ppermute | solution.py:23
  210.1 32.8 %copy-start.2 = (f32[5,256,256]{2,1,0:T(8,128)}, f32[5,256,256]{2,1,0:T(8,128)S(1)}, u32[]{:S(2)}) copy-start(f32[5,256,256]{2,1,0:T(8,128)S(1)} %select_add_fusion) | copy-start | bytes 3932164
  210.1 42.3 %copy-start.5 = (bf16[9,128,256]{2,1,0:T(8,128)(2,1)S(1)}, bf16[9,128,256]{2,1,0:T(8,128)(2,1)}, u32[]{:S(2)}) copy-start(bf16[9,128,256]{2,1,0:T(8,128)(2,1)} %copy-done.4) | copy-start | bytes 1769476
  210.1 7.6 %collective-permute-start.15 = (bf16[256,256]{1,0:T(8,128)(2,1)S(1)}, bf16[256,256]{1,0:T(8,128)(2,1)S(1)}, u32[]{:S(2)}, u32[]{:S(2)}) collective-permute-start(bf16[256,256]{1,0:T(8,128)(2,1)S(1)} %fusion.46), channel_id=1, source_target_pairs={{16,0},{24,8},{32,16},{40,24},{48,32},{56,40},{64,48},{72,56},{80,... | collective-permute-start | bytes 393224 | tf_op jit(solution)/shard_map/ppermute | solution.py:18
  217.7 12.1 %collective-permute-start.16 = (bf16[256,256]{1,0:T(8,128)(2,1)S(1)}, bf16[256,256]{1,0:T(8,128)(2,1)S(1)}, u32[]{:S(2)}, u32[]{:S(2)}) collective-permute-start(bf16[256,256]{1,0:T(8,128)(2,1)S(1)} %fusion.37), channel_id=1, source_target_pairs={{16,0},{24,8},{32,16},{40,24},{48,32},{56,40},{64,48},{72,56},{80,... | collective-permute-start | bytes 393224 | tf_op jit(solution)/shard_map/ppermute | solution.py:18
  229.8 13.0 %collective-permute-start.17 = (bf16[256,256]{1,0:T(8,128)(2,1)S(1)}, bf16[256,256]{1,0:T(8,128)(2,1)S(1)}, u32[]{:S(2)}, u32[]{:S(2)}) collective-permute-start(bf16[256,256]{1,0:T(8,128)(2,1)S(1)} %fusion.39), channel_id=1, source_target_pairs={{16,0},{24,8},{32,16},{40,24},{48,32},{56,40},{64,48},{72,56},{80,... | collective-permute-start | bytes 393224 | tf_op jit(solution)/shard_map/ppermute | solution.py:18
  242.9 12.0 %collective-permute-start.18 = (bf16[256,256]{1,0:T(8,128)(2,1)S(1)}, bf16[256,256]{1,0:T(8,128)(2,1)S(1)}, u32[]{:S(2)}, u32[]{:S(2)}) collective-permute-start(bf16[256,256]{1,0:T(8,128)(2,1)S(1)} %fusion.41), channel_id=1, source_target_pairs={{16,0},{24,8},{32,16},{40,24},{48,32},{56,40},{64,48},{72,56},{80,... | collective-permute-start | bytes 393224 | tf_op jit(solution)/shard_map/ppermute | solution.py:18
  (14 other events, 89.6 us)

commit v2 on v1

--- a/solution.py
+++ b/solution.py
@@ -23,36 +23,29 @@
     return lax.ppermute(value, axis, [(i, i ^ bit) for i in range(length)])
 
 
-def gather_doubling(value, axis, along):
+def rotated(value, axis, by):
+    length = lax.axis_size(axis)
+    return lax.ppermute(value, axis, [(i, (i + by) % length) for i in range(length)])
+
+
+def gather_direct(value, axis, along):
     size = lax.axis_size(axis)
     me = lax.axis_index(axis)
-    bit = 1
-    while bit < size:
-        incoming = swapped(value, axis, bit)
-        upper = (me // bit) % 2 == 1
-        value = jnp.where(
-            upper,
-            jnp.concatenate([incoming, value], along),
-            jnp.concatenate([value, incoming], along),
-        )
-        bit *= 2
-    return value
-
-
-def scatter_halving(value, axis):
+    got = [value] + [rotated(value, axis, by) for by in range(1, size)]
+    ordered = jnp.stack([got[(-by) % size] for by in range(size)])
+    placed = jnp.roll(ordered, me, axis=0)
+    return jnp.concatenate([placed[j] for j in range(size)], along)
+
+
+def scatter_direct(value, axis):
     size = lax.axis_size(axis)
     me = lax.axis_index(axis)
-    bit = size // 2
-    while bit >= 1:
-        half = value.shape[0] // 2
-        low, high = value[:half], value[half:]
-        upper = (me // bit) % 2 == 1
-        send = jnp.where(upper, low, high)
-        keep = jnp.where(upper, high, low)
-        incoming = swapped(send.astype(jnp.bfloat16), axis, bit)
-        value = keep + incoming.astype(jnp.float32)
-        bit //= 2
-    return value
+    blocks = value.reshape(size, value.shape[0] // size, value.shape[1])
+    total = lax.dynamic_index_in_dim(blocks, me, 0, keepdims=False)
+    for by in range(1, size):
+        send = lax.dynamic_index_in_dim(blocks, (me + by) % size, 0, keepdims=False)
+        total = total + rotated(send.astype(jnp.bfloat16), axis, by).astype(jnp.float32)
+    return total
 
 
 def window_probs(queries, keys_all, marks_query, marks_all, heads, depth, scale, block_rows):
@@ -129,7 +122,7 @@
     )
     teacher_mix, _, _ = mix_values(probability, values_teacher, rows, heads_t, DH_T)
     target_cols = lax.dot_general(
-        gather_doubling(teacher_mix, "head", 1),
+        gather_direct(teacher_mix, "head", 1),
         teacher_out_proj,
         (((1,), (1,)), ((), ())),
         preferred_element_type=jnp.float32,
@@ -142,7 +135,7 @@
         probability, values_student, rows, heads_s, DH_S
     )
     share_rows = rows // lax.axis_size("head")
-    residual = scatter_halving(
+    residual = scatter_direct(
         jnp.dot(student_mix, student_out_proj, preferred_element_type=jnp.float32)
         - jnp.dot(target_cols, match_proj, preferred_element_type=jnp.float32),
         "head",
@@ -156,7 +149,7 @@
     )
     grad_mix = (token_weight[:, None] * residual).astype(jnp.bfloat16)
     grad_heads = lax.dot_general(
-        gather_doubling(grad_mix, "head", 0),
+        gather_direct(grad_mix, "head", 0),
         student_out_proj,
         (((1,), (1,)), ((), ())),
         preferred_element_type=jnp.float32,

time: 258 us -> 292 us (1.13)
  the two profiles are of different devices: /device:TPU:46 before, /device:TPU:40 now
where the time goes in v2:
time: 292 us; the launch traced here: 290 us
  starting transfers between devices  120 us (41%)
  waiting for transfers between devices  92.3 us (32%)
  local copies, waits for them, and re-layouts  51 us (17%)
  matrix products  16.2 us (6%)
  other arithmetic  9.54 us (3%)
    ppermute x21, starting transfers between devices, rotated(): lax.ppermute(value, axis, [(i, (i + by) % length) for i in range(length)])  74.6 us
    ppermute x8, waiting for transfers between devices, shifted(): return lax.ppermute(value, axis, pairs)  74.4 us
    ppermute x8, starting transfers between devices, shifted(): return lax.ppermute(value, axis, pairs)  41.4 us
    unnamed x93, local copies, waits for them, and re-layouts  30.6 us
    ppermute x21, waiting for transfers between devices, rotated(): lax.ppermute(value, axis, [(i, (i + by) % length) for i in range(length)])  12 us
    ppermute x2, waiting for transfers between devices, swapped(): return lax.ppermute(value, axis, [(i, i ^ bit) for i in range(length)])  5.85 us
  transfers between devices with their start and end apart: 31, of which 15 were waited for; matrix products, arithmetic and copies ran while one was open for 5% of the time, Pallas kernels for 0%

profile of v2, /device:TPU:40, one launch (start us, length us, event | category | flops | bytes accessed | tf_op | source)
XLA Modules:
  0.0 290.4 jit_solution(12425259106926926533)
XLA Ops:
  4.9 4.3 %collective-permute-start = (bf16[520,256]{1,0:T(8,128)(2,1)S(1)}, bf16[520,256]{1,0:T(8,128)(2,1)S(1)}, u32[]{:S(2)}, u32[]{:S(2)}) collective-permute-start(bf16[520,256]{1,0:T(8,128)(2,1)S(1)} %constant_dynamic-update-slice_fusion), channel_id=1, source_target_pairs={{0,16},{8,24},{16,32},{24,40},{32,48},{40,56},{48,64},{56,72},{64,... | collective-permute-start | bytes 798728 | tf_op jit(solution)/shard_map/ppermute | solution.py:18
  9.1 26.8 %collective-permute-done = bf16[520,256]{1,0:T(8,128)(2,1)S(1)} collective-permute-done((bf16[520,256]{1,0:T(8,128)(2,1)S(1)}, bf16[520,256]{1,0:T(8,128)(2,1)S(1)}, u32[]{:S(2)}, u32[]{:S(2)}) %collective-permute-start) | collective-permute-done | bytes 266272 | tf_op jit(solution)/shard_map/ppermute | solution.py:18
  37.8 15.9 %collective-permute-done.1 = bf16[520,256]{1,0:T(8,128)(2,1)S(1)} collective-permute-done((bf16[520,256]{1,0:T(8,128)(2,1)S(1)}, bf16[520,256]{1,0:T(8,128)(2,1)S(1)}, u32[]{:S(2)}, u32[]{:S(2)}) %collective-permute-start.1) | collective-permute-done | bytes 266272 | tf_op jit(solution)/shard_map/ppermute | solution.py:18
  57.1 11.5 %collective-permute-done.2 = bf16[520,256]{1,0:T(8,128)(2,1)} collective-permute-done((bf16[520,256]{1,0:T(8,128)(2,1)S(1)}, bf16[520,256]{1,0:T(8,128)(2,1)}, u32[]{:S(2)}, u32[]{:S(2)}) %collective-permute-start.2) | collective-permute-done | bytes 266272 | tf_op jit(solution)/shard_map/ppermute | solution.py:18
  73.0 9.5 %collective-permute-done.3 = bf16[520,256]{1,0:T(8,128)(2,1)S(1)} collective-permute-done((bf16[520,256]{1,0:T(8,128)(2,1)}, bf16[520,256]{1,0:T(8,128)(2,1)S(1)}, u32[]{:S(2)}, u32[]{:S(2)}) %collective-permute-start.3) | collective-permute-done | bytes 266272 | tf_op jit(solution)/shard_map/ppermute | solution.py:18
  112.9 6.4 %collective-permute-start.5 = (bf16[128,256]{0,1:T(8,128)(2,1)S(1)}, bf16[128,256]{0,1:T(8,128)(2,1)S(1)}, u32[]{:S(2)}, u32[]{:S(2)}) collective-permute-start(bf16[128,256]{0,1:T(8,128)(2,1)S(1)} %bitcast.258), channel_id=1, source_target_pairs={{0,7},{1,0},{2,1},{3,2},{4,3},{5,4},{6,5},{7,6},{8,15},{9,8},{10,9... | collective-permute-start | bytes 196616 | tf_op jit(solution)/shard_map/ppermute | solution.py:28
  124.0 4.2 %collective-permute-start.8 = (bf16[128,256]{0,1:T(8,128)(2,1)S(1)}, bf16[128,256]{0,1:T(8,128)(2,1)}, u32[]{:S(2)}, u32[]{:S(2)}) collective-permute-start(bf16[128,256]{0,1:T(8,128)(2,1)S(1)} %bitcast.261), channel_id=1, source_target_pairs={{0,4},{1,5},{2,6},{3,7},{4,0},{5,1},{6,2},{7,3},{8,12},{9,13},{10,... | collective-permute-start | bytes 196616 | tf_op jit(solution)/shard_map/ppermute | solution.py:28
  132.5 3.6 %fusion.9 = f32[128,2304]{1,0:T(8,128)} fusion(bf16[256,2304]{1,0:T(8,128)(2,1)} %param.22, bf16[1152,256]{1,0:T(8,128)(2,1)} %bitcast.256, f32[128,1152]{0,1:T(8,128)} %copy-done.4, f32[128]{0:T(128)S(1)} %fusion.17, f32[128]{0:T(128)S(1)} %get-tuple-element.31, s32[128]{0:T(128)S(1)} %get-tuple-element.37, s32[1152]{0:T(1024)S(1)} %fusion.46, ...), kind=kOutput, calls=%fused_computation.23 | convolution fusion | flops 227852288 | bytes 3545600 | tf_op jit(solution)/shard_map/dot_general | solution.py:139
  136.1 4.3 %collective-permute-start.10 = (bf16[128,256]{0,1:T(8,128)(2,1)S(1)}, bf16[128,256]{0,1:T(8,128)(2,1)S(1)}, u32[]{:S(2)}, u32[]{:S(2)}) collective-permute-start(bf16[128,256]{0,1:T(8,128)(2,1)S(1)} %bitcast.264), channel_id=1, source_target_pairs={{0,2},{1,3},{2,4},{3,5},{4,6},{5,7},{6,0},{7,1},{8,10},{9,11},{10,... | collective-permute-start | bytes 196616 | tf_op jit(solution)/shard_map/ppermute | solution.py:28
  144.7 4.1 %collective-permute-done.11 = bf16[128,256]{0,1:T(8,128)(2,1)S(1)} collective-permute-done((bf16[128,256]{0,1:T(8,128)(2,1)S(1)}, bf16[128,256]{0,1:T(8,128)(2,1)S(1)}, u32[]{:S(2)}, u32[]{:S(2)}) %collective-permute-start.11) | collective-permute-done | bytes 65568 | tf_op jit(solution)/shard_map/ppermute | solution.py:28
  155.7 5.4 %convolution_subtract_fusion = f32[128,2304]{1,0:T(8,128)} fusion(f32[128,2304]{1,0:T(8,128)} %fusion.9, bf16[576,2304]{1,0:T(8,128)(2,1)S(1)} %copy-done, bf16[576,2048]{1,0:T(8,128)(2,1)} %param.21, bf16[128,2048]{0,1:T(8,128)(2,1)} %constant_dynamic-update-slice_fusion.21), kind=kOutput, calls=%fused_computation.1 | convolution fusion | flops 642097152 | bytes 7897088 | tf_op jit(solution)/shard_map/dot_general | solution.py:140
  165.0 3.6 %collective-permute-start.13 = (bf16[16,2304]{1,0:T(8,128)(2,1)}, bf16[16,2304]{1,0:T(8,128)(2,1)}, u32[]{:S(2)}, u32[]{:S(2)}) collective-permute-start(bf16[16,2304]{1,0:T(8,128)(2,1)} %get-tuple-element.24), channel_id=1, source_target_pairs={{0,2},{1,3},{2,4},{3,5},{4,6},{5,7},{6,0},{7,1},{8,10},{9,11},{10,... | collective-permute-start | bytes 221192 | tf_op jit(solution)/shard_map/ppermute | solution.py:28
  169.3 4.9 %collective-permute-start.14 = (bf16[16,2304]{1,0:T(8,128)(2,1)}, bf16[16,2304]{1,0:T(8,128)(2,1)S(1)}, u32[]{:S(2)}, u32[]{:S(2)}) collective-permute-start(bf16[16,2304]{1,0:T(8,128)(2,1)} %get-tuple-element.23), channel_id=1, source_target_pairs={{0,3},{1,4},{2,5},{3,6},{4,7},{5,0},{6,1},{7,2},{8,11},{9,12},{10,... | collective-permute-start | bytes 221192 | tf_op jit(solution)/shard_map/ppermute | solution.py:28
  176.2 4.2 %collective-permute-start.16 = (bf16[16,2304]{1,0:T(8,128)(2,1)S(1)}, bf16[16,2304]{1,0:T(8,128)(2,1)S(1)}, u32[]{:S(2)}, u32[]{:S(2)}) collective-permute-start(bf16[16,2304]{1,0:T(8,128)(2,1)S(1)} %get-tuple-element.21), channel_id=1, source_target_pairs={{0,5},{1,6},{2,7},{3,0},{4,1},{5,2},{6,3},{7,4},{8,13},{9,14},{10,... | collective-permute-start | bytes 221192 | tf_op jit(solution)/shard_map/ppermute | solution.py:28
  180.4 4.3 %collective-permute-start.17 = (bf16[16,2304]{1,0:T(8,128)(2,1)S(1)}, bf16[16,2304]{1,0:T(8,128)(2,1)S(1)}, u32[]{:S(2)}, u32[]{:S(2)}) collective-permute-start(bf16[16,2304]{1,0:T(8,128)(2,1)S(1)} %get-tuple-element.20), channel_id=1, source_target_pairs={{0,6},{1,7},{2,0},{3,1},{4,2},{5,3},{6,4},{7,5},{8,14},{9,15},{10,... | collective-permute-start | bytes 221192 | tf_op jit(solution)/shard_map/ppermute | solution.py:28
  184.7 5.1 %collective-permute-start.18 = (bf16[16,2304]{1,0:T(8,128)(2,1)S(1)}, bf16[16,2304]{1,0:T(8,128)(2,1)S(1)}, u32[]{:S(2)}, u32[]{:S(2)}) collective-permute-start(bf16[16,2304]{1,0:T(8,128)(2,1)S(1)} %get-tuple-element.19), channel_id=1, source_target_pairs={{0,7},{1,0},{2,1},{3,2},{4,3},{5,4},{6,5},{7,6},{8,15},{9,8},{10,9... | collective-permute-start | bytes 221192 | tf_op jit(solution)/shard_map/ppermute | solution.py:28
  192.8 6.4 %collective-permute-start.19 = (bf16[16,2304]{1,0:T(8,128)(2,1)S(1)}, bf16[16,2304]{1,0:T(8,128)(2,1)S(1)}, u32[]{:S(2)}, u32[]{:S(2)}) collective-permute-start(bf16[16,2304]{1,0:T(8,128)(2,1)S(1)} %get-tuple-element.13), channel_id=1, source_target_pairs={{0,7},{1,0},{2,1},{3,2},{4,3},{5,4},{6,5},{7,6},{8,15},{9,8},{10,9... | collective-permute-start | bytes 221192 | tf_op jit(solution)/shard_map/ppermute | solution.py:28
  203.4 3.9 %collective-permute-start.22 = (bf16[16,2304]{1,0:T(8,128)(2,1)S(1)}, bf16[16,2304]{1,0:T(8,128)(2,1)S(1)}, u32[]{:S(2)}, u32[]{:S(2)}) collective-permute-start(bf16[16,2304]{1,0:T(8,128)(2,1)S(1)} %get-tuple-element.13), channel_id=1, source_target_pairs={{0,4},{1,5},{2,6},{3,7},{4,0},{5,1},{6,2},{7,3},{8,12},{9,13},{10,... | collective-permute-start | bytes 221192 | tf_op jit(solution)/shard_map/ppermute | solution.py:28
  210.2 5.1 %collective-permute-start.24 = (bf16[16,2304]{1,0:T(8,128)(2,1)S(1)}, bf16[16,2304]{1,0:T(8,128)(2,1)S(1)}, u32[]{:S(2)}, u32[]{:S(2)}) collective-permute-start(bf16[16,2304]{1,0:T(8,128)(2,1)S(1)} %get-tuple-element.13), channel_id=1, source_target_pairs={{0,2},{1,3},{2,4},{3,5},{4,6},{5,7},{6,0},{7,1},{8,10},{9,11},{10,... | collective-permute-start | bytes 221192 | tf_op jit(solution)/shard_map/ppermute | solution.py:28
  219.1 4.6 %collective-permute-done.25 = bf16[16,2304]{1,0:T(8,128)(2,1)S(1)} collective-permute-done((bf16[16,2304]{1,0:T(8,128)(2,1)S(1)}, bf16[16,2304]{1,0:T(8,128)(2,1)S(1)}, u32[]{:S(2)}, u32[]{:S(2)}) %collective-permute-start.25) | collective-permute-done | bytes 73760 | tf_op jit(solution)/shard_map/ppermute | solution.py:28
  245.1 5.5 %collective-permute-done.27 = bf16[256,256]{1,0:T(8,128)(2,1)S(1)} collective-permute-done((bf16[256,256]{1,0:T(8,128)(2,1)S(1)}, bf16[256,256]{1,0:T(8,128)(2,1)S(1)}, u32[]{:S(2)}, u32[]{:S(2)}) %collective-permute-start.27) | collective-permute-done | bytes 131104 | tf_op jit(solution)/shard_map/ppermute | solution.py:18
  250.7 9.6 %collective-permute-start.28 = (bf16[256,256]{1,0:T(8,128)(2,1)S(1)}, bf16[256,256]{1,0:T(8,128)(2,1)S(1)}, u32[]{:S(2)}, u32[]{:S(2)}) collective-permute-start(bf16[256,256]{1,0:T(8,128)(2,1)S(1)} %fusion.19), channel_id=1, source_target_pairs={{16,0},{24,8},{32,16},{40,24},{48,32},{56,40},{64,48},{72,56},{80,... | collective-permute-start | bytes 393224 | tf_op jit(solution)/shard_map/ppermute | solution.py:18
  262.8 10.5 %collective-permute-start.29 = (bf16[256,256]{1,0:T(8,128)(2,1)S(1)}, bf16[256,256]{1,0:T(8,128)(2,1)S(1)}, u32[]{:S(2)}, u32[]{:S(2)}) collective-permute-start(bf16[256,256]{1,0:T(8,128)(2,1)S(1)} %fusion.21), channel_id=1, source_target_pairs={{16,0},{24,8},{32,16},{40,24},{48,32},{56,40},{64,48},{72,56},{80,... | collective-permute-start | bytes 393224 | tf_op jit(solution)/shard_map/ppermute | solution.py:18
  276.4 9.5 %collective-permute-start.30 = (bf16[256,256]{1,0:T(8,128)(2,1)}, bf16[256,256]{1,0:T(8,128)(2,1)}, u32[]{:S(2)}, u32[]{:S(2)}) collective-permute-start(bf16[256,256]{1,0:T(8,128)(2,1)} %fusion.23), channel_id=1, source_target_pairs={{16,0},{24,8},{32,16},{40,24},{48,32},{56,40},{64,48},{72,56},{80,... | collective-permute-start | bytes 393224 | tf_op jit(solution)/shard_map/ppermute | solution.py:18
  (175 shorter events, 115.7 us)
Async XLA Ops:
  4.9 31.0 %collective-permute-start = (bf16[520,256]{1,0:T(8,128)(2,1)S(1)}, bf16[520,256]{1,0:T(8,128)(2,1)S(1)}, u32[]{:S(2)}, u32[]{:S(2)}) collective-permute-start(bf16[520,256]{1,0:T(8,128)(2,1)S(1)} %constant_dynamic-update-slice_fusion), channel_id=1, source_target_pairs={{0,16},{8,24},{16,32},{24,40},{32,48},{40,56},{48,64},{56,72},{64,... | collective-permute-start | bytes 798728 | tf_op jit(solution)/shard_map/ppermute | solution.py:18
  35.9 17.9 %collective-permute-start.1 = (bf16[520,256]{1,0:T(8,128)(2,1)S(1)}, bf16[520,256]{1,0:T(8,128)(2,1)S(1)}, u32[]{:S(2)}, u32[]{:S(2)}) collective-permute-start(bf16[520,256]{1,0:T(8,128)(2,1)S(1)} %collective-permute-done), channel_id=1, source_target_pairs={{0,16},{8,24},{16,32},{24,40},{32,48},{40,56},{48,64},{56,72},{64,... | collective-permute-start | bytes 798728 | tf_op jit(solution)/shard_map/ppermute | solution.py:18
  53.8 14.9 %collective-permute-start.2 = (bf16[520,256]{1,0:T(8,128)(2,1)S(1)}, bf16[520,256]{1,0:T(8,128)(2,1)}, u32[]{:S(2)}, u32[]{:S(2)}) collective-permute-start(bf16[520,256]{1,0:T(8,128)(2,1)S(1)} %collective-permute-done.1), channel_id=1, source_target_pairs={{0,16},{8,24},{16,32},{24,40},{32,48},{40,56},{48,64},{56,72},{64,... | collective-permute-start | bytes 798728 | tf_op jit(solution)/shard_map/ppermute | solution.py:18
  68.7 13.9 %collective-permute-start.3 = (bf16[520,256]{1,0:T(8,128)(2,1)}, bf16[520,256]{1,0:T(8,128)(2,1)S(1)}, u32[]{:S(2)}, u32[]{:S(2)}) collective-permute-start(bf16[520,256]{1,0:T(8,128)(2,1)} %collective-permute-done.2), channel_id=1, source_target_pairs={{0,16},{8,24},{16,32},{24,40},{32,48},{40,56},{48,64},{56,72},{64,... | collective-permute-start | bytes 798728 | tf_op jit(solution)/shard_map/ppermute | solution.py:18
  112.9 23.2 %collective-permute-start.5 = (bf16[128,256]{0,1:T(8,128)(2,1)S(1)}, bf16[128,256]{0,1:T(8,128)(2,1)S(1)}, u32[]{:S(2)}, u32[]{:S(2)}) collective-permute-start(bf16[128,256]{0,1:T(8,128)(2,1)S(1)} %bitcast.258), channel_id=1, source_target_pairs={{0,7},{1,0},{2,1},{3,2},{4,3},{5,4},{6,5},{7,6},{8,15},{9,8},{10,9... | collective-permute-start | bytes 196616 | tf_op jit(solution)/shard_map/ppermute | solution.py:28
  119.3 21.2 %collective-permute-start.6 = (bf16[128,256]{0,1:T(8,128)(2,1)S(1)}, bf16[128,256]{0,1:T(8,128)(2,1)S(1)}, u32[]{:S(2)}, u32[]{:S(2)}) collective-permute-start(bf16[128,256]{0,1:T(8,128)(2,1)S(1)} %bitcast.259), channel_id=1, source_target_pairs={{0,6},{1,7},{2,0},{3,1},{4,2},{5,3},{6,4},{7,5},{8,14},{9,15},{10,... | collective-permute-start | bytes 196616 | tf_op jit(solution)/shard_map/ppermute | solution.py:28
  122.0 20.4 %collective-permute-start.7 = (bf16[128,256]{0,1:T(8,128)(2,1)S(1)}, bf16[128,256]{0,1:T(8,128)(2,1)S(1)}, u32[]{:S(2)}, u32[]{:S(2)}) collective-permute-start(bf16[128,256]{0,1:T(8,128)(2,1)S(1)} %bitcast.260), channel_id=1, source_target_pairs={{0,5},{1,6},{2,7},{3,0},{4,1},{5,2},{6,3},{7,4},{8,13},{9,14},{10,... | collective-permute-start | bytes 196616 | tf_op jit(solution)/shard_map/ppermute | solution.py:28
  124.0 18.5 %collective-permute-start.8 = (bf16[128,256]{0,1:T(8,128)(2,1)S(1)}, bf16[128,256]{0,1:T(8,128)(2,1)}, u32[]{:S(2)}, u32[]{:S(2)}) collective-permute-start(bf16[128,256]{0,1:T(8,128)(2,1)S(1)} %bitcast.261), channel_id=1, source_target_pairs={{0,4},{1,5},{2,6},{3,7},{4,0},{5,1},{6,2},{7,3},{8,12},{9,13},{10,... | collective-permute-start | bytes 196616 | tf_op jit(solution)/shard_map/ppermute | solution.py:28
  128.2 15.2 %collective-permute-start.9 = (bf16[128,256]{0,1:T(8,128)(2,1)S(1)}, bf16[128,256]{0,1:T(8,128)(2,1)}, u32[]{:S(2)}, u32[]{:S(2)}) collective-permute-start(bf16[128,256]{0,1:T(8,128)(2,1)S(1)} %bitcast.262), channel_id=1, source_target_pairs={{0,3},{1,4},{2,5},{3,6},{4,7},{5,0},{6,1},{7,2},{8,11},{9,12},{10,... | collective-permute-start | bytes 196616 | tf_op jit(solution)/shard_map/ppermute | solution.py:28
  163.1 17.3 %collective-permute-start.12 = (bf16[16,2304]{1,0:T(8,128)(2,1)}, bf16[16,2304]{1,0:T(8,128)(2,1)S(1)}, u32[]{:S(2)}, u32[]{:S(2)}) collective-permute-start(bf16[16,2304]{1,0:T(8,128)(2,1)} %get-tuple-element.18), channel_id=1, source_target_pairs={{0,1},{1,2},{2,3},{3,4},{4,5},{5,6},{6,7},{7,0},{8,9},{9,10},{10,1... | collective-permute-start | bytes 221192 | tf_op jit(solution)/shard_map/ppermute | solution.py:28
  165.0 19.7 %collective-permute-start.13 = (bf16[16,2304]{1,0:T(8,128)(2,1)}, bf16[16,2304]{1,0:T(8,128)(2,1)}, u32[]{:S(2)}, u32[]{:S(2)}) collective-permute-start(bf16[16,2304]{1,0:T(8,128)(2,1)} %get-tuple-element.24), channel_id=1, source_target_pairs={{0,2},{1,3},{2,4},{3,5},{4,6},{5,7},{6,0},{7,1},{8,10},{9,11},{10,... | collective-permute-start | bytes 221192 | tf_op jit(solution)/shard_map/ppermute | solution.py:28
  169.3 21.4 %collective-permute-start.14 = (bf16[16,2304]{1,0:T(8,128)(2,1)}, bf16[16,2304]{1,0:T(8,128)(2,1)S(1)}, u32[]{:S(2)}, u32[]{:S(2)}) collective-permute-start(bf16[16,2304]{1,0:T(8,128)(2,1)} %get-tuple-element.23), channel_id=1, source_target_pairs={{0,3},{1,4},{2,5},{3,6},{4,7},{5,0},{6,1},{7,2},{8,11},{9,12},{10,... | collective-permute-start | bytes 221192 | tf_op jit(solution)/shard_map/ppermute | solution.py:28
  174.2 16.4 %collective-permute-start.15 = (bf16[16,2304]{1,0:T(8,128)(2,1)}, bf16[16,2304]{1,0:T(8,128)(2,1)S(1)}, u32[]{:S(2)}, u32[]{:S(2)}) collective-permute-start(bf16[16,2304]{1,0:T(8,128)(2,1)} %get-tuple-element.22), channel_id=1, source_target_pairs={{0,4},{1,5},{2,6},{3,7},{4,0},{5,1},{6,2},{7,3},{8,12},{9,13},{10,... | collective-permute-start | bytes 221192 | tf_op jit(solution)/shard_map/ppermute | solution.py:28
  176.2 14.5 %collective-permute-start.16 = (bf16[16,2304]{1,0:T(8,128)(2,1)S(1)}, bf16[16,2304]{1,0:T(8,128)(2,1)S(1)}, u32[]{:S(2)}, u32[]{:S(2)}) collective-permute-start(bf16[16,2304]{1,0:T(8,128)(2,1)S(1)} %get-tuple-element.21), channel_id=1, source_target_pairs={{0,5},{1,6},{2,7},{3,0},{4,1},{5,2},{6,3},{7,4},{8,13},{9,14},{10,... | collective-permute-start | bytes 221192 | tf_op jit(solution)/shard_map/ppermute | solution.py:28
  180.4 10.3 %collective-permute-start.17 = (bf16[16,2304]{1,0:T(8,128)(2,1)S(1)}, bf16[16,2304]{1,0:T(8,128)(2,1)S(1)}, u32[]{:S(2)}, u32[]{:S(2)}) collective-permute-start(bf16[16,2304]{1,0:T(8,128)(2,1)S(1)} %get-tuple-element.20), channel_id=1, source_target_pairs={{0,6},{1,7},{2,0},{3,1},{4,2},{5,3},{6,4},{7,5},{8,14},{9,15},{10,... | collective-permute-start | bytes 221192 | tf_op jit(solution)/shard_map/ppermute | solution.py:28
  192.8 17.3 %collective-permute-start.19 = (bf16[16,2304]{1,0:T(8,128)(2,1)S(1)}, bf16[16,2304]{1,0:T(8,128)(2,1)S(1)}, u32[]{:S(2)}, u32[]{:S(2)}) collective-permute-start(bf16[16,2304]{1,0:T(8,128)(2,1)S(1)} %get-tuple-element.13), channel_id=1, source_target_pairs={{0,7},{1,0},{2,1},{3,2},{4,3},{5,4},{6,5},{7,6},{8,15},{9,8},{10,9... | collective-permute-start | bytes 221192 | tf_op jit(solution)/shard_map/ppermute | solution.py:28
  199.2 16.1 %collective-permute-start.20 = (bf16[16,2304]{1,0:T(8,128)(2,1)S(1)}, bf16[16,2304]{1,0:T(8,128)(2,1)S(1)}, u32[]{:S(2)}, u32[]{:S(2)}) collective-permute-start(bf16[16,2304]{1,0:T(8,128)(2,1)S(1)} %get-tuple-element.13), channel_id=1, source_target_pairs={{0,6},{1,7},{2,0},{3,1},{4,2},{5,3},{6,4},{7,5},{8,14},{9,15},{10,... | collective-permute-start | bytes 221192 | tf_op jit(solution)/shard_map/ppermute | solution.py:28
  201.1 16.1 %collective-permute-start.21 = (bf16[16,2304]{1,0:T(8,128)(2,1)S(1)}, bf16[16,2304]{1,0:T(8,128)(2,1)S(1)}, u32[]{:S(2)}, u32[]{:S(2)}) collective-permute-start(bf16[16,2304]{1,0:T(8,128)(2,1)S(1)} %get-tuple-element.13), channel_id=1, source_target_pairs={{0,5},{1,6},{2,7},{3,0},{4,1},{5,2},{6,3},{7,4},{8,13},{9,14},{10,... | collective-permute-start | bytes 221192 | tf_op jit(solution)/shard_map/ppermute | solution.py:28
  203.4 13.9 %collective-permute-start.22 = (bf16[16,2304]{1,0:T(8,128)(2,1)S(1)}, bf16[16,2304]{1,0:T(8,128)(2,1)S(1)}, u32[]{:S(2)}, u32[]{:S(2)}) collective-permute-start(bf16[16,2304]{1,0:T(8,128)(2,1)S(1)} %get-tuple-element.13), channel_id=1, source_target_pairs={{0,4},{1,5},{2,6},{3,7},{4,0},{5,1},{6,2},{7,3},{8,12},{9,13},{10,... | collective-permute-start | bytes 221192 | tf_op jit(solution)/shard_map/ppermute | solution.py:28
  207.3 10.0 %collective-permute-start.23 = (bf16[16,2304]{1,0:T(8,128)(2,1)S(1)}, bf16[16,2304]{1,0:T(8,128)(2,1)S(1)}, u32[]{:S(2)}, u32[]{:S(2)}) collective-permute-start(bf16[16,2304]{1,0:T(8,128)(2,1)S(1)} %get-tuple-element.13), channel_id=1, source_target_pairs={{0,3},{1,4},{2,5},{3,6},{4,7},{5,0},{6,1},{7,2},{8,11},{9,12},{10,... | collective-permute-start | bytes 221192 | tf_op jit(solution)/shard_map/ppermute | solution.py:28
  210.2 8.9 %collective-permute-start.24 = (bf16[16,2304]{1,0:T(8,128)(2,1)S(1)}, bf16[16,2304]{1,0:T(8,128)(2,1)S(1)}, u32[]{:S(2)}, u32[]{:S(2)}) collective-permute-start(bf16[16,2304]{1,0:T(8,128)(2,1)S(1)} %get-tuple-element.13), channel_id=1, source_target_pairs={{0,2},{1,3},{2,4},{3,5},{4,6},{5,7},{6,0},{7,1},{8,10},{9,11},{10,... | collective-permute-start | bytes 221192 | tf_op jit(solution)/shard_map/ppermute | solution.py:28
  250.7 12.1 %collective-permute-start.28 = (bf16[256,256]{1,0:T(8,128)(2,1)S(1)}, bf16[256,256]{1,0:T(8,128)(2,1)S(1)}, u32[]{:S(2)}, u32[]{:S(2)}) collective-permute-start(bf16[256,256]{1,0:T(8,128)(2,1)S(1)} %fusion.19), channel_id=1, source_target_pairs={{16,0},{24,8},{32,16},{40,24},{48,32},{56,40},{64,48},{72,56},{80,... | collective-permute-start | bytes 393224 | tf_op jit(solution)/shard_map/ppermute | solution.py:18
  262.8 13.0 %collective-permute-start.29 = (bf16[256,256]{1,0:T(8,128)(2,1)S(1)}, bf16[256,256]{1,0:T(8,128)(2,1)S(1)}, u32[]{:S(2)}, u32[]{:S(2)}) collective-permute-start(bf16[256,256]{1,0:T(8,128)(2,1)S(1)} %fusion.21), channel_id=1, source_target_pairs={{16,0},{24,8},{32,16},{40,24},{48,32},{56,40},{64,48},{72,56},{80,... | collective-permute-start | bytes 393224 | tf_op jit(solution)/shard_map/ppermute | solution.py:18
  276.4 12.3 %collective-permute-start.30 = (bf16[256,256]{1,0:T(8,128)(2,1)}, bf16[256,256]{1,0:T(8,128)(2,1)}, u32[]{:S(2)}, u32[]{:S(2)}) collective-permute-start(bf16[256,256]{1,0:T(8,128)(2,1)} %fusion.23), channel_id=1, source_target_pairs={{16,0},{24,8},{32,16},{40,24},{48,32},{56,40},{64,48},{72,56},{80,... | collective-permute-start | bytes 393224 | tf_op jit(solution)/shard_map/ppermute | solution.py:18
  (23 other events, 283.6 us)

commit v3 on v1

--- a/solution.py
+++ b/solution.py
@@ -52,6 +52,15 @@
         incoming = swapped(send.astype(jnp.bfloat16), axis, bit)
         value = keep + incoming.astype(jnp.float32)
         bit //= 2
+    return value
+
+
+def reduce_doubling(value, axis):
+    size = lax.axis_size(axis)
+    bit = 1
+    while bit < size:
+        value = value + swapped(value.astype(jnp.bfloat16), axis, bit).astype(jnp.float32)
+        bit *= 2
     return value
 
 
@@ -141,22 +150,17 @@
     student_mix, rounded, value_part = mix_values(
         probability, values_student, rows, heads_s, DH_S
     )
-    share_rows = rows // lax.axis_size("head")
-    residual = scatter_halving(
+    lang_table = lax.broadcasted_iota(jnp.int32, (rows, language_weight.shape[0]), 1)
+    token_weight = jnp.sum(
+        jnp.where(language_ids[:, None] == lang_table, language_weight[None, :], 0.0), axis=1
+    )
+    weighted = token_weight[:, None] * (
         jnp.dot(student_mix, student_out_proj, preferred_element_type=jnp.float32)
-        - jnp.dot(target_cols, match_proj, preferred_element_type=jnp.float32),
-        "head",
-    )
-    my_langs = lax.dynamic_slice_in_dim(
-        language_ids, lax.axis_index("head") * share_rows, share_rows, 0
-    )
-    lang_table = lax.broadcasted_iota(jnp.int32, (share_rows, language_weight.shape[0]), 1)
-    token_weight = jnp.sum(
-        jnp.where(my_langs[:, None] == lang_table, language_weight[None, :], 0.0), axis=1
-    )
-    grad_mix = (token_weight[:, None] * residual).astype(jnp.bfloat16)
+        - jnp.dot(target_cols, match_proj, preferred_element_type=jnp.float32)
+    )
+    grad_mix = reduce_doubling(weighted, "head").astype(jnp.bfloat16)
     grad_heads = lax.dot_general(
-        gather_doubling(grad_mix, "head", 0),
+        grad_mix,
         student_out_proj,
         (((1,), (1,)), ((), ())),
         preferred_element_type=jnp.float32,

time: 258 us -> 250 us (0.969)
  starting transfers between devices: 76.1 us -> 64 us
  waiting for transfers between devices: 116 us -> 120 us
    ppermute x11 -> x8, starting transfers between devices: 34.4 us -> 23.8 us  [swapped(): return lax.ppermute(value, axis, [(i, i ^ bit) for i in range(length)])]
    ppermute x11 -> x8, waiting for transfers between devices: 40.3 us -> 45.7 us  [swapped(): return lax.ppermute(value, axis, [(i, i ^ bit) for i in range(length)])]
    unnamed x56 -> x54, local copies, waits for them, and re-layouts: 19.6 us -> 20.5 us
  transfers between devices with their start and end apart: 19 -> 16, of which waited for: 19 -> 16; matrix products, arithmetic and copies ran while one was open for 4% -> 5% of each run, Pallas kernels for 0% -> 0%
where the time goes in v3:
time: 250 us; the launch traced here: 249 us
  waiting for transfers between devices  120 us (48%)
  starting transfers between devices  64 us (26%)
  local copies, waits for them, and re-layouts  37.5 us (15%)
  matrix products  16.4 us (7%)
  other arithmetic  9.95 us (4%)
    ppermute x8, waiting for transfers between devices, shifted(): return lax.ppermute(value, axis, pairs)  74.4 us
    ppermute x8, waiting for transfers between devices, swapped(): return lax.ppermute(value, axis, [(i, i ^ bit) for i in range(length)])  45.7 us
    ppermute x8, starting transfers between devices, shifted(): return lax.ppermute(value, axis, pairs)  40.1 us
    ppermute x8, starting transfers between devices, swapped(): return lax.ppermute(value, axis, [(i, i ^ bit) for i in range(length)])  23.8 us
    unnamed x54, local copies, waits for them, and re-layouts  20.5 us
    dot_general x1, matrix products, shards(): jnp.dot(target_cols, match_proj, preferred_element_type=jnp.float32)  5.58 us
  transfers between devices with their start and end apart: 16, of which 16 were waited for; matrix products, arithmetic and copies ran while one was open for 5% of the time, Pallas kernels for 0%

profile of v3, /device:TPU:46, one launch (start us, length us, event | category | flops | bytes accessed | tf_op | source)
XLA Modules:
  0.0 249.0 jit_solution(11429555397748036403)
XLA Ops:
  4.9 4.3 %collective-permute-start = (bf16[520,256]{1,0:T(8,128)(2,1)S(1)}, bf16[520,256]{1,0:T(8,128)(2,1)S(1)}, u32[]{:S(2)}, u32[]{:S(2)}) collective-permute-start(bf16[520,256]{1,0:T(8,128)(2,1)S(1)} %constant_dynamic-update-slice_fusion), channel_id=1, source_target_pairs={{0,16},{8,24},{16,32},{24,40},{32,48},{40,56},{48,64},{56,72},{64,... | collective-permute-start | bytes 798728 | tf_op jit(solution)/shard_map/ppermute | solution.py:18
  9.1 26.8 %collective-permute-done = bf16[520,256]{1,0:T(8,128)(2,1)S(1)} collective-permute-done((bf16[520,256]{1,0:T(8,128)(2,1)S(1)}, bf16[520,256]{1,0:T(8,128)(2,1)S(1)}, u32[]{:S(2)}, u32[]{:S(2)}) %collective-permute-start) | collective-permute-done | bytes 266272 | tf_op jit(solution)/shard_map/ppermute | solution.py:18
  37.8 15.9 %collective-permute-done.1 = bf16[520,256]{1,0:T(8,128)(2,1)S(1)} collective-permute-done((bf16[520,256]{1,0:T(8,128)(2,1)S(1)}, bf16[520,256]{1,0:T(8,128)(2,1)S(1)}, u32[]{:S(2)}, u32[]{:S(2)}) %collective-permute-start.1) | collective-permute-done | bytes 266272 | tf_op jit(solution)/shard_map/ppermute | solution.py:18
  57.1 11.5 %collective-permute-done.2 = bf16[520,256]{1,0:T(8,128)(2,1)} collective-permute-done((bf16[520,256]{1,0:T(8,128)(2,1)S(1)}, bf16[520,256]{1,0:T(8,128)(2,1)}, u32[]{:S(2)}, u32[]{:S(2)}) %collective-permute-start.2) | collective-permute-done | bytes 266272 | tf_op jit(solution)/shard_map/ppermute | solution.py:18
  73.0 9.5 %collective-permute-done.3 = bf16[520,256]{1,0:T(8,128)(2,1)S(1)} collective-permute-done((bf16[520,256]{1,0:T(8,128)(2,1)}, bf16[520,256]{1,0:T(8,128)(2,1)S(1)}, u32[]{:S(2)}, u32[]{:S(2)}) %collective-permute-start.3) | collective-permute-done | bytes 266272 | tf_op jit(solution)/shard_map/ppermute | solution.py:18
  101.1 2.8 %fusion.54 = (bf16[9,128,256]{2,1,0:T(8,128)(2,1)}, bf16[9,128,256]{2,1,0:T(8,128)(2,1)}, bf16[9,128,256]{2,1,0:T(8,128)(2,1)}, bf16[9,128,256]{2,1,0:T(8,128)(2,1)S(1)}) fusion(bf16[9,520,256]{2,1,0:T(8,128)(2,1)} %bitcast_dynamic-update-slice_fusion.6), kind=kLoop, calls=%fused_computation.99 | loop fusion | bytes 4718592 | tf_op jit(solution)/shard_map/slice | solution.py:128
  112.7 2.7 %collective-permute-start.5 = (bf16[128,256]{0,1:T(8,128)(2,1)S(1)}, bf16[128,256]{0,1:T(8,128)(2,1)S(1)}, u32[]{:S(2)}, u32[]{:S(2)}) collective-permute-start(bf16[128,256]{0,1:T(8,128)(2,1)S(1)} %bitcast.111), channel_id=1, source_target_pairs={{0,1},{1,0},{2,3},{3,2},{4,5},{5,4},{6,7},{7,6},{8,9},{9,8},{10,11... | collective-permute-start | bytes 196616 | tf_op jit(solution)/shard_map/ppermute | solution.py:23
  115.8 3.0 %collective-permute-done.5 = bf16[128,256]{0,1:T(8,128)(2,1)S(1)} collective-permute-done((bf16[128,256]{0,1:T(8,128)(2,1)S(1)}, bf16[128,256]{0,1:T(8,128)(2,1)S(1)}, u32[]{:S(2)}, u32[]{:S(2)}) %collective-permute-start.5) | collective-permute-done | bytes 65568 | tf_op jit(solution)/shard_map/ppermute | solution.py:23
  118.9 3.3 %collective-permute-start.6 = (bf16[128,512]{0,1:T(8,128)(2,1)S(1)}, bf16[128,512]{0,1:T(8,128)(2,1)S(1)}, u32[]{:S(2)}, u32[]{:S(2)}) collective-permute-start(bf16[128,512]{0,1:T(8,128)(2,1)S(1)} %maximum_select_fusion.4), channel_id=1, source_target_pairs={{0,2},{1,3},{2,0},{3,1},{4,6},{5,7},{6,4},{7,5},{8,10},{9,11},{10,... | collective-permute-start | bytes 393224 | tf_op jit(solution)/shard_map/ppermute | solution.py:23
  122.5 4.8 %collective-permute-done.6 = bf16[128,512]{0,1:T(8,128)(2,1)S(1)} collective-permute-done((bf16[128,512]{0,1:T(8,128)(2,1)S(1)}, bf16[128,512]{0,1:T(8,128)(2,1)S(1)}, u32[]{:S(2)}, u32[]{:S(2)}) %collective-permute-start.6) | collective-permute-done | bytes 131104 | tf_op jit(solution)/shard_map/ppermute | solution.py:23
  127.3 4.2 %collective-permute-start.7 = (bf16[128,1024]{0,1:T(8,128)(2,1)S(1)}, bf16[128,1024]{0,1:T(8,128)(2,1)}, u32[]{:S(2)}, u32[]{:S(2)}) collective-permute-start(bf16[128,1024]{0,1:T(8,128)(2,1)S(1)} %maximum_select_fusion.3), channel_id=1, source_target_pairs={{0,4},{1,5},{2,6},{3,7},{4,0},{5,1},{6,2},{7,3},{8,12},{9,13},{10,... | collective-permute-start | bytes 786440 | tf_op jit(solution)/shard_map/ppermute | solution.py:23
  131.5 3.6 %fusion.10 = f32[128,2304]{1,0:T(8,128)} fusion(bf16[256,2304]{1,0:T(8,128)(2,1)} %param.22, bf16[1152,256]{1,0:T(8,128)(2,1)} %bitcast.107, f32[128,1152]{0,1:T(8,128)} %copy-done.5, f32[128]{0:T(128)S(1)} %fusion.32, f32[128]{0:T(128)S(1)} %get-tuple-element.22, s32[128]{0:T(128)S(1)} %get-tuple-element.30, s32[1152]{0:T(1024)S(1)} %fusion.46, ...), kind=kOutput, calls=%fused_computation.27 | convolution fusion | flops 227852288 | bytes 3545600 | tf_op jit(solution)/shard_map/dot_general | solution.py:158
  136.0 5.6 %fusion.57 = (bf16[128,2304]{1,0:T(8,128)(2,1)}, f32[128,2304]{1,0:T(8,128)}) fusion(f32[128,2304]{1,0:T(8,128)} %fusion.10, bf16[576,2304]{1,0:T(8,128)(2,1)S(1)} %copy-done, bf16[576,2048]{1,0:T(8,128)(2,1)} %param.21, bf16[128,1024]{0,1:T(8,128)(2,1)S(1)} %maximum_select_fusion.3, bf16[128,1024]{0,1:T(8,128)(2,1)} %collective-permute-done.7, ...), kind=kOutput, calls=%fused_computation.102 | convolution fusion | flops 645046272 | bytes 8487425 | tf_op jit(solution)/shard_map/dot_general | solution.py:159
  141.5 2.9 %collective-permute-start.8 = (bf16[128,2304]{1,0:T(8,128)(2,1)}, bf16[128,2304]{1,0:T(8,128)(2,1)S(1)}, u32[]{:S(2)}, u32[]{:S(2)}) collective-permute-start(bf16[128,2304]{1,0:T(8,128)(2,1)} %get-tuple-element.26), channel_id=1, source_target_pairs={{0,1},{1,0},{2,3},{3,2},{4,5},{5,4},{6,7},{7,6},{8,9},{9,8},{10,11... | collective-permute-start | bytes 1769480 | tf_op jit(solution)/shard_map/ppermute | solution.py:23
  144.4 11.6 %collective-permute-done.8 = bf16[128,2304]{1,0:T(8,128)(2,1)S(1)} collective-permute-done((bf16[128,2304]{1,0:T(8,128)(2,1)}, bf16[128,2304]{1,0:T(8,128)(2,1)S(1)}, u32[]{:S(2)}, u32[]{:S(2)}) %collective-permute-start.8) | collective-permute-done | bytes 589856 | tf_op jit(solution)/shard_map/ppermute | solution.py:23
  157.4 3.4 %collective-permute-start.9 = (bf16[128,2304]{1,0:T(8,128)(2,1)S(1)}, bf16[128,2304]{1,0:T(8,128)(2,1)S(1)}, u32[]{:S(2)}, u32[]{:S(2)}) collective-permute-start(bf16[128,2304]{1,0:T(8,128)(2,1)S(1)} %fusion.11), channel_id=1, source_target_pairs={{0,2},{1,3},{2,0},{3,1},{4,6},{5,7},{6,4},{7,5},{8,10},{9,11},{10,... | collective-permute-start | bytes 1769480 | tf_op jit(solution)/shard_map/ppermute | solution.py:23
  160.8 11.4 %collective-permute-done.9 = bf16[128,2304]{1,0:T(8,128)(2,1)S(1)} collective-permute-done((bf16[128,2304]{1,0:T(8,128)(2,1)S(1)}, bf16[128,2304]{1,0:T(8,128)(2,1)S(1)}, u32[]{:S(2)}, u32[]{:S(2)}) %collective-permute-start.9) | collective-permute-done | bytes 589856 | tf_op jit(solution)/shard_map/ppermute | solution.py:23
  172.4 3.5 %collective-permute-start.10 = (bf16[128,2304]{1,0:T(8,128)(2,1)S(1)}, bf16[128,2304]{1,0:T(8,128)(2,1)S(1)}, u32[]{:S(2)}, u32[]{:S(2)}) collective-permute-start(bf16[128,2304]{1,0:T(8,128)(2,1)S(1)} %fusion.30), channel_id=1, source_target_pairs={{0,4},{1,5},{2,6},{3,7},{4,0},{5,1},{6,2},{7,3},{8,12},{9,13},{10,... | collective-permute-start | bytes 1769480 | tf_op jit(solution)/shard_map/ppermute | solution.py:23
  175.9 8.9 %collective-permute-done.10 = bf16[128,2304]{1,0:T(8,128)(2,1)S(1)} collective-permute-done((bf16[128,2304]{1,0:T(8,128)(2,1)S(1)}, bf16[128,2304]{1,0:T(8,128)(2,1)S(1)}, u32[]{:S(2)}, u32[]{:S(2)}) %collective-permute-start.10) | collective-permute-done | bytes 589856 | tf_op jit(solution)/shard_map/ppermute | solution.py:23
  197.9 3.0 %collective-permute-done.11 = f32[4,256,256]{2,1,0:T(8,128)} collective-permute-done((f32[4,256,256]{2,1,0:T(8,128)}, f32[4,256,256]{2,1,0:T(8,128)}, u32[]{:S(2)}, u32[]{:S(2)}) %collective-permute-start.11) | collective-permute-done | bytes 1048608 | tf_op jit(solution)/shard_map/ppermute | solution.py:23
  205.0 5.5 %collective-permute-done.12 = bf16[256,256]{1,0:T(8,128)(2,1)S(1)} collective-permute-done((bf16[256,256]{1,0:T(8,128)(2,1)S(1)}, bf16[256,256]{1,0:T(8,128)(2,1)S(1)}, u32[]{:S(2)}, u32[]{:S(2)}) %collective-permute-start.12) | collective-permute-done | bytes 131104 | tf_op jit(solution)/shard_map/ppermute | solution.py:18
  210.5 8.9 %collective-permute-start.13 = (bf16[256,256]{1,0:T(8,128)(2,1)S(1)}, bf16[256,256]{1,0:T(8,128)(2,1)S(1)}, u32[]{:S(2)}, u32[]{:S(2)}) collective-permute-start(bf16[256,256]{1,0:T(8,128)(2,1)S(1)} %fusion.34), channel_id=1, source_target_pairs={{16,0},{24,8},{32,16},{40,24},{48,32},{56,40},{64,48},{72,56},{80,... | collective-permute-start | bytes 393224 | tf_op jit(solution)/shard_map/ppermute | solution.py:18
  222.0 9.9 %collective-permute-start.14 = (bf16[256,256]{1,0:T(8,128)(2,1)S(1)}, bf16[256,256]{1,0:T(8,128)(2,1)S(1)}, u32[]{:S(2)}, u32[]{:S(2)}) collective-permute-start(bf16[256,256]{1,0:T(8,128)(2,1)S(1)} %fusion.36), channel_id=1, source_target_pairs={{16,0},{24,8},{32,16},{40,24},{48,32},{56,40},{64,48},{72,56},{80,... | collective-permute-start | bytes 393224 | tf_op jit(solution)/shard_map/ppermute | solution.py:18
  235.1 9.4 %collective-permute-start.15 = (bf16[256,256]{1,0:T(8,128)(2,1)}, bf16[256,256]{1,0:T(8,128)(2,1)}, u32[]{:S(2)}, u32[]{:S(2)}) collective-permute-start(bf16[256,256]{1,0:T(8,128)(2,1)} %fusion.38), channel_id=1, source_target_pairs={{16,0},{24,8},{32,16},{40,24},{48,32},{56,40},{64,48},{72,56},{80,... | collective-permute-start | bytes 393224 | tf_op jit(solution)/shard_map/ppermute | solution.py:18
  (103 shorter events, 71.7 us)
Async XLA Ops:
  0.6 135.3 %copy-start = (bf16[576,2304]{1,0:T(8,128)(2,1)S(1)}, bf16[576,2304]{1,0:T(8,128)(2,1)}, u32[]{:S(2)}) copy-start(bf16[576,2304]{1,0:T(8,128)(2,1)} %param.23) | copy-start | bytes 7962628
  4.9 31.0 %collective-permute-start = (bf16[520,256]{1,0:T(8,128)(2,1)S(1)}, bf16[520,256]{1,0:T(8,128)(2,1)S(1)}, u32[]{:S(2)}, u32[]{:S(2)}) collective-permute-start(bf16[520,256]{1,0:T(8,128)(2,1)S(1)} %constant_dynamic-update-slice_fusion), channel_id=1, source_target_pairs={{0,16},{8,24},{16,32},{24,40},{32,48},{40,56},{48,64},{56,72},{64,... | collective-permute-start | bytes 798728 | tf_op jit(solution)/shard_map/ppermute | solution.py:18
  35.9 17.9 %collective-permute-start.1 = (bf16[520,256]{1,0:T(8,128)(2,1)S(1)}, bf16[520,256]{1,0:T(8,128)(2,1)S(1)}, u32[]{:S(2)}, u32[]{:S(2)}) collective-permute-start(bf16[520,256]{1,0:T(8,128)(2,1)S(1)} %collective-permute-done), channel_id=1, source_target_pairs={{0,16},{8,24},{16,32},{24,40},{32,48},{40,56},{48,64},{56,72},{64,... | collective-permute-start | bytes 798728 | tf_op jit(solution)/shard_map/ppermute | solution.py:18
  53.8 14.9 %collective-permute-start.2 = (bf16[520,256]{1,0:T(8,128)(2,1)S(1)}, bf16[520,256]{1,0:T(8,128)(2,1)}, u32[]{:S(2)}, u32[]{:S(2)}) collective-permute-start(bf16[520,256]{1,0:T(8,128)(2,1)S(1)} %collective-permute-done.1), channel_id=1, source_target_pairs={{0,16},{8,24},{16,32},{24,40},{32,48},{40,56},{48,64},{56,72},{64,... | collective-permute-start | bytes 798728 | tf_op jit(solution)/shard_map/ppermute | solution.py:18
  68.7 13.9 %collective-permute-start.3 = (bf16[520,256]{1,0:T(8,128)(2,1)}, bf16[520,256]{1,0:T(8,128)(2,1)S(1)}, u32[]{:S(2)}, u32[]{:S(2)}) collective-permute-start(bf16[520,256]{1,0:T(8,128)(2,1)} %collective-permute-done.2), channel_id=1, source_target_pairs={{0,16},{8,24},{16,32},{24,40},{32,48},{40,56},{48,64},{56,72},{64,... | collective-permute-start | bytes 798728 | tf_op jit(solution)/shard_map/ppermute | solution.py:18
  85.7 4.9 %collective-permute-start.4 = (bf16[4,520,256]{2,1,0:T(8,128)(2,1)}, bf16[4,520,256]{2,1,0:T(8,128)(2,1)}, u32[]{:S(2)}, u32[]{:S(2)}) collective-permute-start(bf16[4,520,256]{2,1,0:T(8,128)(2,1)} %constant_dynamic-slice_fusion), channel_id=1, source_target_pairs={{0,8},{8,0},{16,24},{24,16},{32,40},{40,32},{48,56},{56,48},{64,72... | collective-permute-start | bytes 3194888 | tf_op jit(solution)/shard_map/ppermute | solution.py:23
  112.7 6.2 %collective-permute-start.5 = (bf16[128,256]{0,1:T(8,128)(2,1)S(1)}, bf16[128,256]{0,1:T(8,128)(2,1)S(1)}, u32[]{:S(2)}, u32[]{:S(2)}) collective-permute-start(bf16[128,256]{0,1:T(8,128)(2,1)S(1)} %bitcast.111), channel_id=1, source_target_pairs={{0,1},{1,0},{2,3},{3,2},{4,5},{5,4},{6,7},{7,6},{8,9},{9,8},{10,11... | collective-permute-start | bytes 196616 | tf_op jit(solution)/shard_map/ppermute | solution.py:23
  115.8 6.4 %copy-start.5 = (f32[128,1152]{0,1:T(8,128)}, f32[128,1152]{0,1:T(8,128)S(1)}, u32[]{:S(2)}) copy-start(f32[128,1152]{0,1:T(8,128)S(1)} %get-tuple-element.23) | copy-start | bytes 1769476
  115.8 71.1 %copy-start.13 = (f32[128]{0:T(128)}, f32[128]{0:T(128)S(1)}, u32[]{:S(2)}) copy-start(f32[128]{0:T(128)S(1)} %get-tuple-element.22) | copy-start | bytes 1540
  118.9 8.4 %collective-permute-start.6 = (bf16[128,512]{0,1:T(8,128)(2,1)S(1)}, bf16[128,512]{0,1:T(8,128)(2,1)S(1)}, u32[]{:S(2)}, u32[]{:S(2)}) collective-permute-start(bf16[128,512]{0,1:T(8,128)(2,1)S(1)} %maximum_select_fusion.4), channel_id=1, source_target_pairs={{0,2},{1,3},{2,0},{3,1},{4,6},{5,7},{6,4},{7,5},{8,10},{9,11},{10,... | collective-permute-start | bytes 393224 | tf_op jit(solution)/shard_map/ppermute | solution.py:23
  122.5 64.4 %copy-start.14 = (f32[128]{0:T(128)}, f32[128]{0:T(128)S(1)}, u32[]{:S(2)}) copy-start(f32[128]{0:T(128)S(1)} %fusion.32) | copy-start | bytes 1540
  127.3 8.6 %collective-permute-start.7 = (bf16[128,1024]{0,1:T(8,128)(2,1)S(1)}, bf16[128,1024]{0,1:T(8,128)(2,1)}, u32[]{:S(2)}, u32[]{:S(2)}) collective-permute-start(bf16[128,1024]{0,1:T(8,128)(2,1)S(1)} %maximum_select_fusion.3), channel_id=1, source_target_pairs={{0,4},{1,5},{2,6},{3,7},{4,0},{5,1},{6,2},{7,3},{8,12},{9,13},{10,... | collective-permute-start | bytes 786440 | tf_op jit(solution)/shard_map/ppermute | solution.py:23
  141.5 30.7 %copy-start.1 = (f32[128,2304]{1,0:T(8,128)S(1)}, f32[128,2304]{1,0:T(8,128)}, u32[]{:S(2)}) copy-start(f32[128,2304]{1,0:T(8,128)} %get-tuple-element.27) | copy-start | bytes 3538948
  141.5 14.4 %collective-permute-start.8 = (bf16[128,2304]{1,0:T(8,128)(2,1)}, bf16[128,2304]{1,0:T(8,128)(2,1)S(1)}, u32[]{:S(2)}, u32[]{:S(2)}) collective-permute-start(bf16[128,2304]{1,0:T(8,128)(2,1)} %get-tuple-element.26), channel_id=1, source_target_pairs={{0,1},{1,0},{2,3},{3,2},{4,5},{5,4},{6,7},{7,6},{8,9},{9,8},{10,11... | collective-permute-start | bytes 1769480 | tf_op jit(solution)/shard_map/ppermute | solution.py:23
  157.4 27.4 %copy-start.7 = (bf16[256,2304]{1,0:T(8,128)(2,1)S(1)}, bf16[256,2304]{1,0:T(8,128)(2,1)}, u32[]{:S(2)}) copy-start(bf16[256,2304]{1,0:T(8,128)(2,1)} %param.22) | copy-start | bytes 3538948
  157.4 14.8 %collective-permute-start.9 = (bf16[128,2304]{1,0:T(8,128)(2,1)S(1)}, bf16[128,2304]{1,0:T(8,128)(2,1)S(1)}, u32[]{:S(2)}, u32[]{:S(2)}) collective-permute-start(bf16[128,2304]{1,0:T(8,128)(2,1)S(1)} %fusion.11), channel_id=1, source_target_pairs={{0,2},{1,3},{2,0},{3,1},{4,6},{5,7},{6,4},{7,5},{8,10},{9,11},{10,... | collective-permute-start | bytes 1769480 | tf_op jit(solution)/shard_map/ppermute | solution.py:23
  172.4 12.9 %copy-start.6 = (f32[128,1152]{0,1:T(8,128)S(1)}, f32[128,1152]{0,1:T(8,128)}, u32[]{:S(2)}) copy-start(f32[128,1152]{0,1:T(8,128)} %copy-done.5) | copy-start | bytes 1769476
  172.4 12.4 %collective-permute-start.10 = (bf16[128,2304]{1,0:T(8,128)(2,1)S(1)}, bf16[128,2304]{1,0:T(8,128)(2,1)S(1)}, u32[]{:S(2)}, u32[]{:S(2)}) collective-permute-start(bf16[128,2304]{1,0:T(8,128)(2,1)S(1)} %fusion.30), channel_id=1, source_target_pairs={{0,4},{1,5},{2,6},{3,7},{4,0},{5,1},{6,2},{7,3},{8,12},{9,13},{10,... | collective-permute-start | bytes 1769480 | tf_op jit(solution)/shard_map/ppermute | solution.py:23
  195.9 4.9 %collective-permute-start.11 = (f32[4,256,256]{2,1,0:T(8,128)}, f32[4,256,256]{2,1,0:T(8,128)}, u32[]{:S(2)}, u32[]{:S(2)}) collective-permute-start(f32[4,256,256]{2,1,0:T(8,128)} %slice.69), channel_id=1, source_target_pairs={{0,8},{8,0},{16,24},{24,16},{32,40},{40,32},{48,56},{56,48},{64,72... | collective-permute-start | bytes 3145736 | tf_op jit(solution)/shard_map/ppermute | solution.py:23
  203.0 31.4 %copy-start.3 = (f32[5,256,256]{2,1,0:T(8,128)}, f32[5,256,256]{2,1,0:T(8,128)S(1)}, u32[]{:S(2)}) copy-start(f32[5,256,256]{2,1,0:T(8,128)S(1)} %select_add_fusion) | copy-start | bytes 3932164
  203.0 7.4 %collective-permute-start.12 = (bf16[256,256]{1,0:T(8,128)(2,1)S(1)}, bf16[256,256]{1,0:T(8,128)(2,1)S(1)}, u32[]{:S(2)}, u32[]{:S(2)}) collective-permute-start(bf16[256,256]{1,0:T(8,128)(2,1)S(1)} %fusion.43), channel_id=1, source_target_pairs={{16,0},{24,8},{32,16},{40,24},{48,32},{56,40},{64,48},{72,56},{80,... | collective-permute-start | bytes 393224 | tf_op jit(solution)/shard_map/ppermute | solution.py:18
  210.5 11.4 %collective-permute-start.13 = (bf16[256,256]{1,0:T(8,128)(2,1)S(1)}, bf16[256,256]{1,0:T(8,128)(2,1)S(1)}, u32[]{:S(2)}, u32[]{:S(2)}) collective-permute-start(bf16[256,256]{1,0:T(8,128)(2,1)S(1)} %fusion.34), channel_id=1, source_target_pairs={{16,0},{24,8},{32,16},{40,24},{48,32},{56,40},{64,48},{72,56},{80,... | collective-permute-start | bytes 393224 | tf_op jit(solution)/shard_map/ppermute | solution.py:18
  222.0 12.4 %collective-permute-start.14 = (bf16[256,256]{1,0:T(8,128)(2,1)S(1)}, bf16[256,256]{1,0:T(8,128)(2,1)S(1)}, u32[]{:S(2)}, u32[]{:S(2)}) collective-permute-start(bf16[256,256]{1,0:T(8,128)(2,1)S(1)} %fusion.36), channel_id=1, source_target_pairs={{16,0},{24,8},{32,16},{40,24},{48,32},{56,40},{64,48},{72,56},{80,... | collective-permute-start | bytes 393224 | tf_op jit(solution)/shard_map/ppermute | solution.py:18
  235.1 12.2 %collective-permute-start.15 = (bf16[256,256]{1,0:T(8,128)(2,1)}, bf16[256,256]{1,0:T(8,128)(2,1)}, u32[]{:S(2)}, u32[]{:S(2)}) collective-permute-start(bf16[256,256]{1,0:T(8,128)(2,1)} %fusion.38), channel_id=1, source_target_pairs={{16,0},{24,8},{32,16},{40,24},{48,32},{56,40},{64,48},{72,56},{80,... | collective-permute-start | bytes 393224 | tf_op jit(solution)/shard_map/ppermute | solution.py:18
  (10 other events, 29.0 us)

commit v4 on v3

--- a/solution.py
+++ b/solution.py
@@ -62,6 +62,59 @@
         value = value + swapped(value.astype(jnp.bfloat16), axis, bit).astype(jnp.float32)
         bit *= 2
     return value
+
+
+def swap_pieces(chain, steps, core):
+    partner = swapped(lax.dynamic_slice_in_dim(jnp.stack(chain), core, steps, 0), "seq", 1)
+    pieces = []
+    for k in range(steps, 0, -1):
+        pieces.append(chain[k])
+        pieces.append(partner[k - 1])
+    pieces.append(chain[0])
+    return pieces
+
+
+def relay(own, steps, core):
+    chain = [own]
+    for _ in range(steps):
+        chain.append(shifted(chain[-1], "seq", 2))
+    return swap_pieces(chain, steps, core)
+
+
+def gather_beside_relay(value, axis, along, own, steps):
+    size = lax.axis_size(axis)
+    me = lax.axis_index(axis)
+    own, value = lax.optimization_barrier((own, value))
+    chain = [own]
+    bit = 1
+    for _ in range(steps):
+        if bit < size:
+            incoming = swapped(value, axis, bit)
+        step = shifted(chain[-1], "seq", 2)
+        if bit < size:
+            upper = (me // bit) % 2 == 1
+            value = jnp.where(
+                upper,
+                jnp.concatenate([incoming, value], along),
+                jnp.concatenate([value, incoming], along),
+            )
+            bit *= 2
+        value, step = lax.optimization_barrier((value, step))
+        chain.append(step)
+    while bit < size:
+        incoming = swapped(value, axis, bit)
+        upper = (me // bit) % 2 == 1
+        value = jnp.where(
+            upper,
+            jnp.concatenate([incoming, value], along),
+            jnp.concatenate([value, incoming], along),
+        )
+        bit *= 2
+    return value, chain
+
+
+def joined(pieces, first, last):
+    return jnp.concatenate([piece[first:last] for piece in pieces], 0)
 
 
 def window_probs(queries, keys_all, marks_query, marks_all, heads, depth, scale, block_rows):
@@ -111,34 +164,26 @@
     student_scale = DH_S ** (-0.5)
     doc_marks = segment_ids + 1
     mark_rows = jnp.pad(doc_marks.astype(jnp.bfloat16), (0, 8 * width - rows)).reshape(8, width)
-    own = jnp.concatenate([teacher_key, teacher_value, student_key, student_value, mark_rows], 0)
-    chain = [own]
-    for _ in range(steps):
-        chain.append(shifted(chain[-1], "seq", 2))
     core = lax.axis_index("seq") % 2
-    stacked = jnp.stack(chain)
-    partner = swapped(lax.dynamic_slice_in_dim(stacked, core, steps, 0), "seq", 1)
-    pieces = []
-    for k in range(steps, 0, -1):
-        pieces.append(chain[k])
-        pieces.append(partner[k - 1])
-    pieces.append(own)
-    window = jnp.stack(pieces)
-    span = window.shape[0] * rows
-    keys_teacher = window[:, 0:rows].reshape(span, width)
-    values_teacher = window[:, rows : 2 * rows].reshape(span, width)
-    keys_student = window[:, 2 * rows : 3 * rows].reshape(span, width)
-    values_student = window[:, 3 * rows : 4 * rows].reshape(span, width)
-    marks_all = (
-        window[:, 4 * rows :].reshape(window.shape[0], 8 * width)[:, :rows].reshape(span)
+    own_teacher = jnp.concatenate([teacher_key, teacher_value, mark_rows], 0)
+    pieces_teacher = relay(own_teacher, steps, core)
+    keys_teacher = joined(pieces_teacher, 0, rows)
+    values_teacher = joined(pieces_teacher, rows, 2 * rows)
+    marks_all = jnp.concatenate(
+        [piece[2 * rows :].reshape(8 * width)[:rows] for piece in pieces_teacher], 0
     ).astype(jnp.int32)
 
     probability, _, _ = window_probs(
         teacher_query, keys_teacher, doc_marks, marks_all, heads_t, DH_T, teacher_scale, rows
     )
     teacher_mix, _, _ = mix_values(probability, values_teacher, rows, heads_t, DH_T)
+    own_student = jnp.concatenate([student_key, student_value], 0)
+    gathered, chain_student = gather_beside_relay(teacher_mix, "head", 1, own_student, steps)
+    pieces_student = swap_pieces(chain_student, steps, core)
+    keys_student = joined(pieces_student, 0, rows)
+    values_student = joined(pieces_student, rows, 2 * rows)
     target_cols = lax.dot_general(
-        gather_doubling(teacher_mix, "head", 1),
+        gathered,
         teacher_out_proj,
         (((1,), (1,)), ((), ())),
         preferred_element_type=jnp.float32,
@@ -179,7 +224,7 @@
         "hqk,qhd->khd", grad_scores, query_part, preferred_element_type=jnp.float32
     )
     grad_v = jnp.einsum("hqk,qhd->khd", rounded, grad_part, preferred_element_type=jnp.float32)
-    blocks = span // rows
+    blocks = keys_student.shape[0] // rows
     grads = jnp.concatenate(
         [grad_k.reshape(blocks, rows, width), grad_v.reshape(blocks, rows, width)], 1
     )

time: 250 us -> 316 us (1.26)
  the two profiles are of different devices: /device:TPU:46 before, /device:TPU:40 now
where the time goes in v4:
time: 316 us; the launch traced here: 314 us
  waiting for transfers between devices  155 us (49%)
  starting transfers between devices  73 us (23%)
  local copies, waits for them, and re-layouts  58.1 us (18%)
  matrix products  14.5 us (5%)
  other arithmetic  11.9 us (4%)
    ppermute x12, waiting for transfers between devices, shifted(): return lax.ppermute(value, axis, pairs)  98.8 us
    ppermute x9, waiting for transfers between devices, swapped(): return lax.ppermute(value, axis, [(i, i ^ bit) for i in range(length)])  56 us
    ppermute x12, starting transfers between devices, shifted(): return lax.ppermute(value, axis, pairs)  48.5 us
    unnamed x113, local copies, waits for them, and re-layouts  29.3 us
    ppermute x9, starting transfers between devices, swapped(): return lax.ppermute(value, axis, [(i, i ^ bit) for i in range(length)])  24.5 us
    concatenate x12, local copies, waits for them, and re-layouts, joined(): return jnp.concatenate([piece[first:last] for piece in pieces], 0)  9.96 us
    slice x9, local copies, waits for them, and re-layouts, joined(): return jnp.concatenate([piece[first:last] for piece in pieces], 0)  9.18 us
  transfers between devices with their start and end apart: 21, of which 20 were waited for; matrix products, arithmetic and copies ran while one was open for 4% of the time, Pallas kernels for 0%

profile of v4, /device:TPU:40, one launch (start us, length us, event | category | flops | bytes accessed | tf_op | source)
XLA Modules:
  0.0 313.7 jit_solution(6564716027354020787)
XLA Ops:
  3.6 4.3 %collective-permute-start = (bf16[264,256]{0,1:T(8,128)(2,1)S(1)}, bf16[264,256]{0,1:T(8,128)(2,1)S(1)}, u32[]{:S(2)}, u32[]{:S(2)}) collective-permute-start(bf16[264,256]{0,1:T(8,128)(2,1)S(1)} %pad_maximum_fusion.1), channel_id=1, source_target_pairs={{0,16},{8,24},{16,32},{24,40},{32,48},{40,56},{48,64},{56,72},{64,... | collective-permute-start | bytes 405512 | tf_op jit(solution)/shard_map/ppermute | solution.py:18
  10.8 20.8 %collective-permute-done = bf16[264,256]{0,1:T(8,128)(2,1)S(1)} collective-permute-done((bf16[264,256]{0,1:T(8,128)(2,1)S(1)}, bf16[264,256]{0,1:T(8,128)(2,1)S(1)}, u32[]{:S(2)}, u32[]{:S(2)}) %collective-permute-start) | collective-permute-done | bytes 135200 | tf_op jit(solution)/shard_map/ppermute | solution.py:18
  35.7 12.3 %collective-permute-done.1 = bf16[264,256]{0,1:T(8,128)(2,1)S(1)} collective-permute-done((bf16[264,256]{0,1:T(8,128)(2,1)S(1)}, bf16[264,256]{0,1:T(8,128)(2,1)S(1)}, u32[]{:S(2)}, u32[]{:S(2)}) %collective-permute-start.1) | collective-permute-done | bytes 135200 | tf_op jit(solution)/shard_map/ppermute | solution.py:18
  52.1 10.2 %collective-permute-done.2 = bf16[264,256]{0,1:T(8,128)(2,1)S(1)} collective-permute-done((bf16[264,256]{0,1:T(8,128)(2,1)S(1)}, bf16[264,256]{0,1:T(8,128)(2,1)S(1)}, u32[]{:S(2)}, u32[]{:S(2)}) %collective-permute-start.2) | collective-permute-done | bytes 135200 | tf_op jit(solution)/shard_map/ppermute | solution.py:18
  64.8 10.1 %collective-permute-done.3 = bf16[264,256]{0,1:T(8,128)(2,1)S(1)} collective-permute-done((bf16[264,256]{0,1:T(8,128)(2,1)S(1)}, bf16[264,256]{0,1:T(8,128)(2,1)S(1)}, u32[]{:S(2)}, u32[]{:S(2)}) %collective-permute-start.3) | collective-permute-done | bytes 135200 | tf_op jit(solution)/shard_map/ppermute | solution.py:18
  121.0 3.4 %collective-permute-start.5 = (bf16[128,256]{0,1:T(8,128)(2,1)S(1)}, bf16[128,256]{0,1:T(8,128)(2,1)S(1)}, u32[]{:S(2)}, u32[]{:S(2)}) collective-permute-start(bf16[128,256]{0,1:T(8,128)(2,1)S(1)} %bitcast.191), channel_id=1, source_target_pairs={{0,1},{1,0},{2,3},{3,2},{4,5},{5,4},{6,7},{7,6},{8,9},{9,8},{10,11... | collective-permute-start | bytes 196616 | tf_op jit(solution)/shard_map/ppermute | solution.py:23
  127.4 10.2 %collective-permute-done.6 = bf16[256,256]{1,0:T(8,128)(2,1)S(1)} collective-permute-done((bf16[256,256]{1,0:T(8,128)(2,1)S(1)}, bf16[256,256]{1,0:T(8,128)(2,1)S(1)}, u32[]{:S(2)}, u32[]{:S(2)}) %collective-permute-start.6) | collective-permute-done | bytes 131104 | tf_op jit(solution)/shard_map/ppermute | solution.py:18
  137.5 4.6 %collective-permute-start.7 = (bf16[128,512]{0,1:T(8,128)(2,1)S(1)}, bf16[128,512]{0,1:T(8,128)(2,1)S(1)}, u32[]{:S(2)}, u32[]{:S(2)}) collective-permute-start(bf16[128,512]{0,1:T(8,128)(2,1)S(1)} %maximum_select_fusion.2), channel_id=1, source_target_pairs={{0,2},{1,3},{2,0},{3,1},{4,6},{5,7},{6,4},{7,5},{8,10},{9,11},{10,... | collective-permute-start | bytes 393224 | tf_op jit(solution)/shard_map/ppermute | solution.py:23
  146.0 8.8 %collective-permute-done.8 = bf16[256,256]{1,0:T(8,128)(2,1)S(1)} collective-permute-done((bf16[256,256]{1,0:T(8,128)(2,1)S(1)}, bf16[256,256]{1,0:T(8,128)(2,1)S(1)}, u32[]{:S(2)}, u32[]{:S(2)}) %collective-permute-start.8) | collective-permute-done | bytes 131104 | tf_op jit(solution)/shard_map/ppermute | solution.py:18
  154.8 3.1 collective-permute-start.9
  159.9 5.0 %collective-permute-done.9 = bf16[128,1024]{0,1:T(8,128)(2,1)S(1)} collective-permute-done((bf16[128,1024]{0,1:T(8,128)(2,1)S(1)}, bf16[128,1024]{0,1:T(8,128)(2,1)S(1)}, u32[]{:S(2)}, u32[]{:S(2)}) %collective-permute-start.9) | collective-permute-done | bytes 262176 | tf_op jit(solution)/shard_map/ppermute | solution.py:23
  165.8 4.3 %collective-permute-done.10 = bf16[256,256]{1,0:T(8,128)(2,1)S(1)} collective-permute-done((bf16[256,256]{1,0:T(8,128)(2,1)S(1)}, bf16[256,256]{1,0:T(8,128)(2,1)S(1)}, u32[]{:S(2)}, u32[]{:S(2)}) %collective-permute-start.10) | collective-permute-done | bytes 131104 | tf_op jit(solution)/shard_map/ppermute | solution.py:18
  172.0 10.2 %collective-permute-done.11 = bf16[256,256]{1,0:T(8,128)(2,1)S(1)} collective-permute-done((bf16[256,256]{1,0:T(8,128)(2,1)S(1)}, bf16[256,256]{1,0:T(8,128)(2,1)S(1)}, u32[]{:S(2)}, u32[]{:S(2)}) %collective-permute-start.11) | collective-permute-done | bytes 131104 | tf_op jit(solution)/shard_map/ppermute | solution.py:18
  187.9 3.4 %fusion.10 = f32[128,2304]{1,0:T(8,128)} fusion(bf16[256,2304]{1,0:T(8,128)(2,1)} %param.22, bf16[1152,256]{1,0:T(8,128)(2,1)} %copy-done.22, f32[128,1152]{0,1:T(8,128)S(1)} %get-tuple-element.83, f32[128]{0:T(128)S(1)} %fusion.18, f32[128]{0:T(128)S(1)} %get-tuple-element.82, s32[128]{0:T(128)S(1)} %get-tuple-element.88, ...), kind=kOutput, calls=%fused_computation.27 | convolution fusion | flops 227852288 | bytes 3545600 | tf_op jit(solution)/shard_map/dot_general | solution.py:203
  191.3 5.6 %fusion.44 = (bf16[128,2304]{1,0:T(8,128)(2,1)}, f32[128,2304]{1,0:T(8,128)}) fusion(f32[128,2304]{1,0:T(8,128)} %fusion.10, bf16[576,2304]{1,0:T(8,128)(2,1)S(1)} %copy-done, bf16[576,2048]{1,0:T(8,128)(2,1)} %param.21, bf16[128,2048]{0,1:T(8,128)(2,1)} %maximum_select_fusion, f32[128]{0:T(128)S(1)} %select_reduce_fusion.2), kind=kOutput, calls=%fused_computation.138 | convolution fusion | flops 642686976 | bytes 8487424 | tf_op jit(solution)/shard_map/dot_general | solution.py:204
  199.1 15.3 %collective-permute-done.13 = bf16[128,2304]{1,0:T(8,128)(2,1)S(1)} collective-permute-done((bf16[128,2304]{1,0:T(8,128)(2,1)}, bf16[128,2304]{1,0:T(8,128)(2,1)S(1)}, u32[]{:S(2)}, u32[]{:S(2)}) %collective-permute-start.13) | collective-permute-done | bytes 589856 | tf_op jit(solution)/shard_map/ppermute | solution.py:23
  218.3 15.7 %collective-permute-done.14 = bf16[128,2304]{1,0:T(8,128)(2,1)S(1)} collective-permute-done((bf16[128,2304]{1,0:T(8,128)(2,1)S(1)}, bf16[128,2304]{1,0:T(8,128)(2,1)S(1)}, u32[]{:S(2)}, u32[]{:S(2)}) %collective-permute-start.14) | collective-permute-done | bytes 589856 | tf_op jit(solution)/shard_map/ppermute | solution.py:23
  234.1 3.1 collective-permute-start.15
  237.3 12.5 %collective-permute-done.15 = bf16[128,2304]{1,0:T(8,128)(2,1)S(1)} collective-permute-done((bf16[128,2304]{1,0:T(8,128)(2,1)S(1)}, bf16[128,2304]{1,0:T(8,128)(2,1)S(1)}, u32[]{:S(2)}, u32[]{:S(2)}) %collective-permute-start.15) | collective-permute-done | bytes 589856 | tf_op jit(solution)/shard_map/ppermute | solution.py:23
  262.7 3.0 collective-permute-done.16
  270.0 5.5 %collective-permute-done.17 = bf16[256,256]{1,0:T(8,128)(2,1)S(1)} collective-permute-done((bf16[256,256]{1,0:T(8,128)(2,1)S(1)}, bf16[256,256]{1,0:T(8,128)(2,1)S(1)}, u32[]{:S(2)}, u32[]{:S(2)}) %collective-permute-start.17) | collective-permute-done | bytes 131104 | tf_op jit(solution)/shard_map/ppermute | solution.py:18
  275.5 8.6 %collective-permute-start.18 = (bf16[256,256]{1,0:T(8,128)(2,1)S(1)}, bf16[256,256]{1,0:T(8,128)(2,1)S(1)}, u32[]{:S(2)}, u32[]{:S(2)}) collective-permute-start(bf16[256,256]{1,0:T(8,128)(2,1)S(1)} %fusion.20), channel_id=1, source_target_pairs={{16,0},{24,8},{32,16},{40,24},{48,32},{56,40},{64,48},{72,56},{80,... | collective-permute-start | bytes 393224 | tf_op jit(solution)/shard_map/ppermute | solution.py:18
  286.8 10.6 %collective-permute-start.19 = (bf16[256,256]{1,0:T(8,128)(2,1)S(1)}, bf16[256,256]{1,0:T(8,128)(2,1)S(1)}, u32[]{:S(2)}, u32[]{:S(2)}) collective-permute-start(bf16[256,256]{1,0:T(8,128)(2,1)S(1)} %fusion.22), channel_id=1, source_target_pairs={{16,0},{24,8},{32,16},{40,24},{48,32},{56,40},{64,48},{72,56},{80,... | collective-permute-start | bytes 393224 | tf_op jit(solution)/shard_map/ppermute | solution.py:18
  300.0 9.5 %collective-permute-start.20 = (bf16[256,256]{1,0:T(8,128)(2,1)S(1)}, bf16[256,256]{1,0:T(8,128)(2,1)S(1)}, u32[]{:S(2)}, u32[]{:S(2)}) collective-permute-start(bf16[256,256]{1,0:T(8,128)(2,1)S(1)} %fusion.24), channel_id=1, source_target_pairs={{16,0},{24,8},{32,16},{40,24},{48,32},{56,40},{64,48},{72,56},{80,... | collective-permute-start | bytes 393224 | tf_op jit(solution)/shard_map/ppermute | solution.py:18
  (213 shorter events, 112.2 us)
Async XLA Ops:
  0.6 190.7 %copy-start = (bf16[576,2304]{1,0:T(8,128)(2,1)S(1)}, bf16[576,2304]{1,0:T(8,128)(2,1)}, u32[]{:S(2)}) copy-start(bf16[576,2304]{1,0:T(8,128)(2,1)} %param.23) | copy-start | bytes 7962628
  3.6 28.1 %collective-permute-start = (bf16[264,256]{0,1:T(8,128)(2,1)S(1)}, bf16[264,256]{0,1:T(8,128)(2,1)S(1)}, u32[]{:S(2)}, u32[]{:S(2)}) collective-permute-start(bf16[264,256]{0,1:T(8,128)(2,1)S(1)} %pad_maximum_fusion.1), channel_id=1, source_target_pairs={{0,16},{8,24},{16,32},{24,40},{32,48},{40,56},{48,64},{56,72},{64,... | collective-permute-start | bytes 405512 | tf_op jit(solution)/shard_map/ppermute | solution.py:18
  33.1 14.9 %collective-permute-start.1 = (bf16[264,256]{0,1:T(8,128)(2,1)S(1)}, bf16[264,256]{0,1:T(8,128)(2,1)S(1)}, u32[]{:S(2)}, u32[]{:S(2)}) collective-permute-start(bf16[264,256]{0,1:T(8,128)(2,1)S(1)} %collective-permute-done), channel_id=1, source_target_pairs={{0,16},{8,24},{16,32},{24,40},{32,48},{40,56},{48,64},{56,72},{64,... | collective-permute-start | bytes 405512 | tf_op jit(solution)/shard_map/ppermute | solution.py:18
  49.4 12.8 %collective-permute-start.2 = (bf16[264,256]{0,1:T(8,128)(2,1)S(1)}, bf16[264,256]{0,1:T(8,128)(2,1)S(1)}, u32[]{:S(2)}, u32[]{:S(2)}) collective-permute-start(bf16[264,256]{0,1:T(8,128)(2,1)S(1)} %collective-permute-done.1), channel_id=1, source_target_pairs={{0,16},{8,24},{16,32},{24,40},{32,48},{40,56},{48,64},{56,72},{64,... | collective-permute-start | bytes 405512 | tf_op jit(solution)/shard_map/ppermute | solution.py:18
  62.2 12.7 %collective-permute-start.3 = (bf16[264,256]{0,1:T(8,128)(2,1)S(1)}, bf16[264,256]{0,1:T(8,128)(2,1)S(1)}, u32[]{:S(2)}, u32[]{:S(2)}) collective-permute-start(bf16[264,256]{0,1:T(8,128)(2,1)S(1)} %collective-permute-done.2), channel_id=1, source_target_pairs={{0,16},{8,24},{16,32},{24,40},{32,48},{40,56},{48,64},{56,72},{64,... | collective-permute-start | bytes 405512 | tf_op jit(solution)/shard_map/ppermute | solution.py:18
  78.6 8.0 %collective-permute-start.4 = (bf16[4,264,256]{2,1,0:T(8,128)(2,1)}, bf16[4,264,256]{2,1,0:T(8,128)(2,1)}, u32[]{:S(2)}, u32[]{:S(2)}) collective-permute-start(bf16[4,264,256]{2,1,0:T(8,128)(2,1)} %copy.113), channel_id=1, source_target_pairs={{0,8},{8,0},{16,24},{24,16},{32,40},{40,32},{48,56},{56,48},{64,72... | collective-permute-start | bytes 1622024 | tf_op jit(solution)/shard_map/ppermute | solution.py:23
  121.0 6.4 %collective-permute-start.5 = (bf16[128,256]{0,1:T(8,128)(2,1)S(1)}, bf16[128,256]{0,1:T(8,128)(2,1)S(1)}, u32[]{:S(2)}, u32[]{:S(2)}) collective-permute-start(bf16[128,256]{0,1:T(8,128)(2,1)S(1)} %bitcast.191), channel_id=1, source_target_pairs={{0,1},{1,0},{2,3},{3,2},{4,5},{5,4},{6,7},{7,6},{8,9},{9,8},{10,11... | collective-permute-start | bytes 196616 | tf_op jit(solution)/shard_map/ppermute | solution.py:23
  124.4 13.2 %collective-permute-start.6 = (bf16[256,256]{1,0:T(8,128)(2,1)S(1)}, bf16[256,256]{1,0:T(8,128)(2,1)S(1)}, u32[]{:S(2)}, u32[]{:S(2)}) collective-permute-start(bf16[256,256]{1,0:T(8,128)(2,1)S(1)} %copy-done.5), channel_id=1, source_target_pairs={{0,16},{8,24},{16,32},{24,40},{32,48},{40,56},{48,64},{56,72},{64,... | collective-permute-start | bytes 393224 | tf_op jit(solution)/shard_map/ppermute | solution.py:18
  137.5 8.4 %collective-permute-start.7 = (bf16[128,512]{0,1:T(8,128)(2,1)S(1)}, bf16[128,512]{0,1:T(8,128)(2,1)S(1)}, u32[]{:S(2)}, u32[]{:S(2)}) collective-permute-start(bf16[128,512]{0,1:T(8,128)(2,1)S(1)} %maximum_select_fusion.2), channel_id=1, source_target_pairs={{0,2},{1,3},{2,0},{3,1},{4,6},{5,7},{6,4},{7,5},{8,10},{9,11},{10,... | collective-permute-start | bytes 393224 | tf_op jit(solution)/shard_map/ppermute | solution.py:23
  142.2 12.6 %collective-permute-start.8 = (bf16[256,256]{1,0:T(8,128)(2,1)S(1)}, bf16[256,256]{1,0:T(8,128)(2,1)S(1)}, u32[]{:S(2)}, u32[]{:S(2)}) collective-permute-start(bf16[256,256]{1,0:T(8,128)(2,1)S(1)} %collective-permute-done.6), channel_id=1, source_target_pairs={{0,16},{8,24},{16,32},{24,40},{32,48},{40,56},{48,64},{56,72},{64,... | collective-permute-start | bytes 393224 | tf_op jit(solution)/shard_map/ppermute | solution.py:18
  154.8 10.1 %collective-permute-start.9 = (bf16[128,1024]{0,1:T(8,128)(2,1)S(1)}, bf16[128,1024]{0,1:T(8,128)(2,1)S(1)}, u32[]{:S(2)}, u32[]{:S(2)}) collective-permute-start(bf16[128,1024]{0,1:T(8,128)(2,1)S(1)} %maximum_select_fusion.1), channel_id=1, source_target_pairs={{0,4},{1,5},{2,6},{3,7},{4,0},{5,1},{6,2},{7,3},{8,12},{9,13},{10,... | collective-permute-start | bytes 786440 | tf_op jit(solution)/shard_map/ppermute | solution.py:23
  157.9 12.2 %collective-permute-start.10 = (bf16[256,256]{1,0:T(8,128)(2,1)S(1)}, bf16[256,256]{1,0:T(8,128)(2,1)S(1)}, u32[]{:S(2)}, u32[]{:S(2)}) collective-permute-start(bf16[256,256]{1,0:T(8,128)(2,1)S(1)} %collective-permute-done.8), channel_id=1, source_target_pairs={{0,16},{8,24},{16,32},{24,40},{32,48},{40,56},{48,64},{56,72},{64,... | collective-permute-start | bytes 393224 | tf_op jit(solution)/shard_map/ppermute | solution.py:18
  170.1 12.1 %collective-permute-start.11 = (bf16[256,256]{1,0:T(8,128)(2,1)S(1)}, bf16[256,256]{1,0:T(8,128)(2,1)S(1)}, u32[]{:S(2)}, u32[]{:S(2)}) collective-permute-start(bf16[256,256]{1,0:T(8,128)(2,1)S(1)} %collective-permute-done.10), channel_id=1, source_target_pairs={{0,16},{8,24},{16,32},{24,40},{32,48},{40,56},{48,64},{56,72},{64,... | collective-permute-start | bytes 393224 | tf_op jit(solution)/shard_map/ppermute | solution.py:18
  182.3 3.8 %collective-permute-start.12 = (bf16[4,256,256]{2,1,0:T(8,128)(2,1)S(1)}, bf16[4,256,256]{2,1,0:T(8,128)(2,1)S(1)}, u32[]{:S(2)}, u32[]{:S(2)}) collective-permute-start(bf16[4,256,256]{2,1,0:T(8,128)(2,1)S(1)} %constant_dynamic-slice_fusion), channel_id=1, source_target_pairs={{0,8},{8,0},{16,24},{24,16},{32,40},{40,32},{48,56},{56,48},{64,72... | collective-permute-start | bytes 1572872 | tf_op jit(solution)/shard_map/ppermute | solution.py:23
  187.4 64.6 %copy-start.24 = (f32[128]{0:T(128)}, f32[128]{0:T(128)S(1)}, u32[]{:S(2)}) copy-start(f32[128]{0:T(128)S(1)} %get-tuple-element.82) | copy-start | bytes 1540
  187.9 64.1 %copy-start.25 = (f32[128]{0:T(128)}, f32[128]{0:T(128)S(1)}, u32[]{:S(2)}) copy-start(f32[128]{0:T(128)S(1)} %fusion.18) | copy-start | bytes 1540
  196.9 17.5 %collective-permute-start.13 = (bf16[128,2304]{1,0:T(8,128)(2,1)}, bf16[128,2304]{1,0:T(8,128)(2,1)S(1)}, u32[]{:S(2)}, u32[]{:S(2)}) collective-permute-start(bf16[128,2304]{1,0:T(8,128)(2,1)} %get-tuple-element.84), channel_id=1, source_target_pairs={{0,1},{1,0},{2,3},{3,2},{4,5},{5,4},{6,7},{7,6},{8,9},{9,8},{10,11... | collective-permute-start | bytes 1769480 | tf_op jit(solution)/shard_map/ppermute | solution.py:23
  215.9 18.1 %collective-permute-start.14 = (bf16[128,2304]{1,0:T(8,128)(2,1)S(1)}, bf16[128,2304]{1,0:T(8,128)(2,1)S(1)}, u32[]{:S(2)}, u32[]{:S(2)}) collective-permute-start(bf16[128,2304]{1,0:T(8,128)(2,1)S(1)} %fusion.11), channel_id=1, source_target_pairs={{0,2},{1,3},{2,0},{3,1},{4,6},{5,7},{6,4},{7,5},{8,10},{9,11},{10,... | collective-permute-start | bytes 1769480 | tf_op jit(solution)/shard_map/ppermute | solution.py:23
  234.1 15.7 %collective-permute-start.15 = (bf16[128,2304]{1,0:T(8,128)(2,1)S(1)}, bf16[128,2304]{1,0:T(8,128)(2,1)S(1)}, u32[]{:S(2)}, u32[]{:S(2)}) collective-permute-start(bf16[128,2304]{1,0:T(8,128)(2,1)S(1)} %fusion.16), channel_id=1, source_target_pairs={{0,4},{1,5},{2,6},{3,7},{4,0},{5,1},{6,2},{7,3},{8,12},{9,13},{10,... | collective-permute-start | bytes 1769480 | tf_op jit(solution)/shard_map/ppermute | solution.py:23
  260.8 4.9 %collective-permute-start.16 = (f32[4,256,256]{2,1,0:T(8,128)}, f32[4,256,256]{2,1,0:T(8,128)}, u32[]{:S(2)}, u32[]{:S(2)}) collective-permute-start(f32[4,256,256]{2,1,0:T(8,128)} %slice.302), channel_id=1, source_target_pairs={{0,8},{8,0},{16,24},{24,16},{32,40},{40,32},{48,56},{56,48},{64,72... | collective-permute-start | bytes 3145736 | tf_op jit(solution)/shard_map/ppermute | solution.py:23
  267.9 7.6 %collective-permute-start.17 = (bf16[256,256]{1,0:T(8,128)(2,1)S(1)}, bf16[256,256]{1,0:T(8,128)(2,1)S(1)}, u32[]{:S(2)}, u32[]{:S(2)}) collective-permute-start(bf16[256,256]{1,0:T(8,128)(2,1)S(1)} %fusion.29), channel_id=1, source_target_pairs={{16,0},{24,8},{32,16},{40,24},{48,32},{56,40},{64,48},{72,56},{80,... | collective-permute-start | bytes 393224 | tf_op jit(solution)/shard_map/ppermute | solution.py:18
  275.5 11.3 %collective-permute-start.18 = (bf16[256,256]{1,0:T(8,128)(2,1)S(1)}, bf16[256,256]{1,0:T(8,128)(2,1)S(1)}, u32[]{:S(2)}, u32[]{:S(2)}) collective-permute-start(bf16[256,256]{1,0:T(8,128)(2,1)S(1)} %fusion.20), channel_id=1, source_target_pairs={{16,0},{24,8},{32,16},{40,24},{48,32},{56,40},{64,48},{72,56},{80,... | collective-permute-start | bytes 393224 | tf_op jit(solution)/shard_map/ppermute | solution.py:18
  286.8 13.1 %collective-permute-start.19 = (bf16[256,256]{1,0:T(8,128)(2,1)S(1)}, bf16[256,256]{1,0:T(8,128)(2,1)S(1)}, u32[]{:S(2)}, u32[]{:S(2)}) collective-permute-start(bf16[256,256]{1,0:T(8,128)(2,1)S(1)} %fusion.22), channel_id=1, source_target_pairs={{16,0},{24,8},{32,16},{40,24},{48,32},{56,40},{64,48},{72,56},{80,... | collective-permute-start | bytes 393224 | tf_op jit(solution)/shard_map/ppermute | solution.py:18
  300.0 12.0 %collective-permute-start.20 = (bf16[256,256]{1,0:T(8,128)(2,1)S(1)}, bf16[256,256]{1,0:T(8,128)(2,1)S(1)}, u32[]{:S(2)}, u32[]{:S(2)}) collective-permute-start(bf16[256,256]{1,0:T(8,128)(2,1)S(1)} %fusion.24), channel_id=1, source_target_pairs={{16,0},{24,8},{32,16},{40,24},{48,32},{56,40},{64,48},{72,56},{80,... | collective-permute-start | bytes 393224 | tf_op jit(solution)/shard_map/ppermute | solution.py:18
  (26 other events, 305.1 us)

commit v5 on v3

--- a/solution.py
+++ b/solution.py
@@ -55,13 +55,24 @@
     return value
 
 
-def reduce_doubling(value, axis):
+def reduce_in_halves(value, axis):
     size = lax.axis_size(axis)
+    me = lax.axis_index(axis)
+    top = size // 2
+    half = value.shape[0] // 2
+    upper = (me // top) % 2 == 1
+    send = jnp.where(upper, value[:half], value[half:])
+    keep = jnp.where(upper, value[half:], value[:half])
+    part = keep + swapped(send.astype(jnp.bfloat16), axis, top).astype(jnp.float32)
     bit = 1
-    while bit < size:
-        value = value + swapped(value.astype(jnp.bfloat16), axis, bit).astype(jnp.float32)
+    while bit < top:
+        part = part + swapped(part.astype(jnp.bfloat16), axis, bit).astype(jnp.float32)
         bit *= 2
-    return value
+    part = part.astype(jnp.bfloat16)
+    other = swapped(part, axis, top)
+    return jnp.where(
+        upper, jnp.concatenate([other, part], 0), jnp.concatenate([part, other], 0)
+    )
 
 
 def window_probs(queries, keys_all, marks_query, marks_all, heads, depth, scale, block_rows):
@@ -158,7 +169,7 @@
         jnp.dot(student_mix, student_out_proj, preferred_element_type=jnp.float32)
         - jnp.dot(target_cols, match_proj, preferred_element_type=jnp.float32)
     )
-    grad_mix = reduce_doubling(weighted, "head").astype(jnp.bfloat16)
+    grad_mix = reduce_in_halves(weighted, "head")
     grad_heads = lax.dot_general(
         grad_mix,
         student_out_proj,

time: 250 us -> 249 us (level)
  waiting for transfers between devices: 120 us -> 113 us
  starting transfers between devices: 64 us -> 68.7 us
    ppermute x8 -> x9, waiting for transfers between devices: 45.7 us -> 38.5 us  [swapped(): return lax.ppermute(value, axis, [(i, i ^ bit) for i in range(length)])]
    ppermute x8 -> x9, starting transfers between devices: 23.8 us -> 27.2 us  [swapped(): return lax.ppermute(value, axis, [(i, i ^ bit) for i in range(length)])]
    unnamed x54 -> x52, local copies, waits for them, and re-layouts: 20.5 us -> 20.5 us
  transfers between devices with their start and end apart: 16 -> 17, of which waited for: 16 -> 17; matrix products, arithmetic and copies ran while one was open for 5% -> 5% of each run, Pallas kernels for 0% -> 0%
where the time goes in v5:
time: 249 us; the launch traced here: 247 us
  waiting for transfers between devices  113 us (45%)
  starting transfers between devices  68.7 us (28%)
  local copies, waits for them, and re-layouts  37.5 us (15%)
  matrix products  16.2 us (7%)
  other arithmetic  11.1 us (4%)
    ppermute x8, waiting for transfers between devices, shifted(): return lax.ppermute(value, axis, pairs)  74.4 us
    ppermute x8, starting transfers between devices, shifted(): return lax.ppermute(value, axis, pairs)  41.5 us
    ppermute x9, waiting for transfers between devices, swapped(): return lax.ppermute(value, axis, [(i, i ^ bit) for i in range(length)])  38.5 us
    ppermute x9, starting transfers between devices, swapped(): return lax.ppermute(value, axis, [(i, i ^ bit) for i in range(length)])  27.2 us
    unnamed x52, local copies, waits for them, and re-layouts  20.5 us
    dot_general x1, matrix products, shards(): jnp.dot(target_cols, match_proj, preferred_element_type=jnp.float32)  5.38 us
  transfers between devices with their start and end apart: 17, of which 17 were waited for; matrix products, arithmetic and copies ran while one was open for 5% of the time, Pallas kernels for 0%

profile of v5, /device:TPU:46, one launch (start us, length us, event | category | flops | bytes accessed | tf_op | source)
XLA Modules:
  0.0 247.5 jit_solution(2427195464609588767)
XLA Ops:
  4.9 4.3 %collective-permute-start = (bf16[520,256]{1,0:T(8,128)(2,1)S(1)}, bf16[520,256]{1,0:T(8,128)(2,1)S(1)}, u32[]{:S(2)}, u32[]{:S(2)}) collective-permute-start(bf16[520,256]{1,0:T(8,128)(2,1)S(1)} %constant_dynamic-update-slice_fusion), channel_id=1, source_target_pairs={{0,16},{8,24},{16,32},{24,40},{32,48},{40,56},{48,64},{56,72},{64,... | collective-permute-start | bytes 798728 | tf_op jit(solution)/shard_map/ppermute | solution.py:18
  9.1 26.8 %collective-permute-done = bf16[520,256]{1,0:T(8,128)(2,1)S(1)} collective-permute-done((bf16[520,256]{1,0:T(8,128)(2,1)S(1)}, bf16[520,256]{1,0:T(8,128)(2,1)S(1)}, u32[]{:S(2)}, u32[]{:S(2)}) %collective-permute-start) | collective-permute-done | bytes 266272 | tf_op jit(solution)/shard_map/ppermute | solution.py:18
  37.8 15.9 %collective-permute-done.1 = bf16[520,256]{1,0:T(8,128)(2,1)S(1)} collective-permute-done((bf16[520,256]{1,0:T(8,128)(2,1)S(1)}, bf16[520,256]{1,0:T(8,128)(2,1)S(1)}, u32[]{:S(2)}, u32[]{:S(2)}) %collective-permute-start.1) | collective-permute-done | bytes 266272 | tf_op jit(solution)/shard_map/ppermute | solution.py:18
  57.1 11.5 %collective-permute-done.2 = bf16[520,256]{1,0:T(8,128)(2,1)} collective-permute-done((bf16[520,256]{1,0:T(8,128)(2,1)S(1)}, bf16[520,256]{1,0:T(8,128)(2,1)}, u32[]{:S(2)}, u32[]{:S(2)}) %collective-permute-start.2) | collective-permute-done | bytes 266272 | tf_op jit(solution)/shard_map/ppermute | solution.py:18
  73.0 9.5 %collective-permute-done.3 = bf16[520,256]{1,0:T(8,128)(2,1)S(1)} collective-permute-done((bf16[520,256]{1,0:T(8,128)(2,1)}, bf16[520,256]{1,0:T(8,128)(2,1)S(1)}, u32[]{:S(2)}, u32[]{:S(2)}) %collective-permute-start.3) | collective-permute-done | bytes 266272 | tf_op jit(solution)/shard_map/ppermute | solution.py:18
  101.1 2.8 %fusion.61 = (bf16[9,128,256]{2,1,0:T(8,128)(2,1)}, bf16[9,128,256]{2,1,0:T(8,128)(2,1)}, bf16[9,128,256]{2,1,0:T(8,128)(2,1)}, bf16[9,128,256]{2,1,0:T(8,128)(2,1)S(1)}) fusion(bf16[9,520,256]{2,1,0:T(8,128)(2,1)} %bitcast_dynamic-update-slice_fusion.6), kind=kLoop, calls=%fused_computation.108 | loop fusion | bytes 4718592 | tf_op jit(solution)/shard_map/slice | solution.py:139
  115.8 3.0 %collective-permute-done.5 = bf16[128,256]{0,1:T(8,128)(2,1)S(1)} collective-permute-done((bf16[128,256]{0,1:T(8,128)(2,1)S(1)}, bf16[128,256]{0,1:T(8,128)(2,1)S(1)}, u32[]{:S(2)}, u32[]{:S(2)}) %collective-permute-start.5) | collective-permute-done | bytes 65568 | tf_op jit(solution)/shard_map/ppermute | solution.py:23
  118.9 3.3 %collective-permute-start.6 = (bf16[128,512]{0,1:T(8,128)(2,1)S(1)}, bf16[128,512]{0,1:T(8,128)(2,1)S(1)}, u32[]{:S(2)}, u32[]{:S(2)}) collective-permute-start(bf16[128,512]{0,1:T(8,128)(2,1)S(1)} %maximum_select_fusion.6), channel_id=1, source_target_pairs={{0,2},{1,3},{2,0},{3,1},{4,6},{5,7},{6,4},{7,5},{8,10},{9,11},{10,... | collective-permute-start | bytes 393224 | tf_op jit(solution)/shard_map/ppermute | solution.py:23
  122.5 4.8 %collective-permute-done.6 = bf16[128,512]{0,1:T(8,128)(2,1)S(1)} collective-permute-done((bf16[128,512]{0,1:T(8,128)(2,1)S(1)}, bf16[128,512]{0,1:T(8,128)(2,1)S(1)}, u32[]{:S(2)}, u32[]{:S(2)}) %collective-permute-start.6) | collective-permute-done | bytes 131104 | tf_op jit(solution)/shard_map/ppermute | solution.py:23
  127.3 4.2 %collective-permute-start.7 = (bf16[128,1024]{0,1:T(8,128)(2,1)S(1)}, bf16[128,1024]{0,1:T(8,128)(2,1)}, u32[]{:S(2)}, u32[]{:S(2)}) collective-permute-start(bf16[128,1024]{0,1:T(8,128)(2,1)S(1)} %maximum_select_fusion.5), channel_id=1, source_target_pairs={{0,4},{1,5},{2,6},{3,7},{4,0},{5,1},{6,2},{7,3},{8,12},{9,13},{10,... | collective-permute-start | bytes 786440 | tf_op jit(solution)/shard_map/ppermute | solution.py:23
  131.5 3.6 %fusion.10 = f32[128,2304]{1,0:T(8,128)} fusion(bf16[256,2304]{1,0:T(8,128)(2,1)} %param.22, bf16[1152,256]{1,0:T(8,128)(2,1)} %bitcast.107, f32[128,1152]{0,1:T(8,128)} %copy-done.4, f32[128]{0:T(128)S(1)} %fusion.36, f32[128]{0:T(128)S(1)} %get-tuple-element.24, s32[128]{0:T(128)S(1)} %get-tuple-element.30, s32[1152]{0:T(1024)S(1)} %fusion.51, ...), kind=kOutput, calls=%fused_computation.24 | convolution fusion | flops 227852288 | bytes 3545600 | tf_op jit(solution)/shard_map/dot_general | solution.py:169
  136.0 5.4 %fusion.1 = f32[128,2304]{1,0:T(8,128)} fusion(f32[128,2304]{1,0:T(8,128)} %fusion.10, bf16[576,2304]{1,0:T(8,128)(2,1)S(1)} %copy-done, bf16[576,2048]{1,0:T(8,128)(2,1)} %param.21, f32[128]{0:T(128)S(1)} %copy-done.13, bf16[128,1024]{0,1:T(8,128)(2,1)S(1)} %maximum_select_fusion.5, bf16[128,1024]{0,1:T(8,128)(2,1)} %collective-permute-done.7, pred[]{:T(512)S(6)} %eq.54), kind=kOutput, calls=%fused_computation.2 | convolution fusion | flops 644751360 | bytes 7897601 | tf_op jit(solution)/shard_map/dot_general | solution.py:170
  142.6 3.9 %collective-permute-start.8 = (bf16[64,2304]{1,0:T(8,128)(2,1)S(1)}, bf16[64,2304]{1,0:T(8,128)(2,1)S(1)}, u32[]{:S(2)}, u32[]{:S(2)}) collective-permute-start(bf16[64,2304]{1,0:T(8,128)(2,1)S(1)} %select_convert_fusion), channel_id=1, source_target_pairs={{0,4},{1,5},{2,6},{3,7},{4,0},{5,1},{6,2},{7,3},{8,12},{9,13},{10,... | collective-permute-start | bytes 884744 | tf_op jit(solution)/shard_map/ppermute | solution.py:23
  146.6 4.7 %collective-permute-done.8 = bf16[64,2304]{1,0:T(8,128)(2,1)S(1)} collective-permute-done((bf16[64,2304]{1,0:T(8,128)(2,1)S(1)}, bf16[64,2304]{1,0:T(8,128)(2,1)S(1)}, u32[]{:S(2)}, u32[]{:S(2)}) %collective-permute-start.8) | collective-permute-done | bytes 294944 | tf_op jit(solution)/shard_map/ppermute | solution.py:23
  152.6 2.7 %collective-permute-start.9 = (bf16[64,2304]{1,0:T(8,128)(2,1)S(1)}, bf16[64,2304]{1,0:T(8,128)(2,1)S(1)}, u32[]{:S(2)}, u32[]{:S(2)}) collective-permute-start(bf16[64,2304]{1,0:T(8,128)(2,1)S(1)} %get-tuple-element.12), channel_id=1, source_target_pairs={{0,1},{1,0},{2,3},{3,2},{4,5},{5,4},{6,7},{7,6},{8,9},{9,8},{10,11... | collective-permute-start | bytes 884744 | tf_op jit(solution)/shard_map/ppermute | solution.py:23
  155.3 7.1 %collective-permute-done.9 = bf16[64,2304]{1,0:T(8,128)(2,1)S(1)} collective-permute-done((bf16[64,2304]{1,0:T(8,128)(2,1)S(1)}, bf16[64,2304]{1,0:T(8,128)(2,1)S(1)}, u32[]{:S(2)}, u32[]{:S(2)}) %collective-permute-start.9) | collective-permute-done | bytes 294944 | tf_op jit(solution)/shard_map/ppermute | solution.py:23
  164.7 8.1 %collective-permute-done.10 = bf16[64,2304]{1,0:T(8,128)(2,1)S(1)} collective-permute-done((bf16[64,2304]{1,0:T(8,128)(2,1)S(1)}, bf16[64,2304]{1,0:T(8,128)(2,1)S(1)}, u32[]{:S(2)}, u32[]{:S(2)}) %collective-permute-start.10) | collective-permute-done | bytes 294944 | tf_op jit(solution)/shard_map/ppermute | solution.py:23
  172.9 4.3 %collective-permute-start.11 = (bf16[64,2304]{1,0:T(8,128)(2,1)S(1)}, bf16[64,2304]{1,0:T(8,128)(2,1)S(1)}, u32[]{:S(2)}, u32[]{:S(2)}) collective-permute-start(bf16[64,2304]{1,0:T(8,128)(2,1)S(1)} %add_convert_fusion), channel_id=1, source_target_pairs={{0,4},{1,5},{2,6},{3,7},{4,0},{5,1},{6,2},{7,3},{8,12},{9,13},{10,... | collective-permute-start | bytes 884744 | tf_op jit(solution)/shard_map/ppermute | solution.py:23
  177.2 4.7 %collective-permute-done.11 = bf16[64,2304]{1,0:T(8,128)(2,1)S(1)} collective-permute-done((bf16[64,2304]{1,0:T(8,128)(2,1)S(1)}, bf16[64,2304]{1,0:T(8,128)(2,1)S(1)}, u32[]{:S(2)}, u32[]{:S(2)}) %collective-permute-start.11) | collective-permute-done | bytes 294944 | tf_op jit(solution)/shard_map/ppermute | solution.py:23
  195.0 3.0 %collective-permute-done.12 = f32[4,256,256]{2,1,0:T(8,128)} collective-permute-done((f32[4,256,256]{2,1,0:T(8,128)}, f32[4,256,256]{2,1,0:T(8,128)}, u32[]{:S(2)}, u32[]{:S(2)}) %collective-permute-start.12) | collective-permute-done | bytes 1048608 | tf_op jit(solution)/shard_map/ppermute | solution.py:23
  202.1 5.5 %collective-permute-done.13 = bf16[256,256]{1,0:T(8,128)(2,1)S(1)} collective-permute-done((bf16[256,256]{1,0:T(8,128)(2,1)S(1)}, bf16[256,256]{1,0:T(8,128)(2,1)S(1)}, u32[]{:S(2)}, u32[]{:S(2)}) %collective-permute-start.13) | collective-permute-done | bytes 131104 | tf_op jit(solution)/shard_map/ppermute | solution.py:18
  207.7 9.6 %collective-permute-start.14 = (bf16[256,256]{1,0:T(8,128)(2,1)S(1)}, bf16[256,256]{1,0:T(8,128)(2,1)S(1)}, u32[]{:S(2)}, u32[]{:S(2)}) collective-permute-start(bf16[256,256]{1,0:T(8,128)(2,1)S(1)} %fusion.39), channel_id=1, source_target_pairs={{16,0},{24,8},{32,16},{40,24},{48,32},{56,40},{64,48},{72,56},{80,... | collective-permute-start | bytes 393224 | tf_op jit(solution)/shard_map/ppermute | solution.py:18
  219.8 10.5 %collective-permute-start.15 = (bf16[256,256]{1,0:T(8,128)(2,1)S(1)}, bf16[256,256]{1,0:T(8,128)(2,1)S(1)}, u32[]{:S(2)}, u32[]{:S(2)}) collective-permute-start(bf16[256,256]{1,0:T(8,128)(2,1)S(1)} %fusion.41), channel_id=1, source_target_pairs={{16,0},{24,8},{32,16},{40,24},{48,32},{56,40},{64,48},{72,56},{80,... | collective-permute-start | bytes 393224 | tf_op jit(solution)/shard_map/ppermute | solution.py:18
  233.5 9.5 %collective-permute-start.16 = (bf16[256,256]{1,0:T(8,128)(2,1)}, bf16[256,256]{1,0:T(8,128)(2,1)}, u32[]{:S(2)}, u32[]{:S(2)}) collective-permute-start(bf16[256,256]{1,0:T(8,128)(2,1)} %fusion.43), channel_id=1, source_target_pairs={{16,0},{24,8},{32,16},{40,24},{48,32},{56,40},{64,48},{72,56},{80,... | collective-permute-start | bytes 393224 | tf_op jit(solution)/shard_map/ppermute | solution.py:18
  (105 shorter events, 77.8 us)
Async XLA Ops:
  0.6 135.3 %copy-start = (bf16[576,2304]{1,0:T(8,128)(2,1)S(1)}, bf16[576,2304]{1,0:T(8,128)(2,1)}, u32[]{:S(2)}) copy-start(bf16[576,2304]{1,0:T(8,128)(2,1)} %param.23) | copy-start | bytes 7962628
  4.9 31.0 %collective-permute-start = (bf16[520,256]{1,0:T(8,128)(2,1)S(1)}, bf16[520,256]{1,0:T(8,128)(2,1)S(1)}, u32[]{:S(2)}, u32[]{:S(2)}) collective-permute-start(bf16[520,256]{1,0:T(8,128)(2,1)S(1)} %constant_dynamic-update-slice_fusion), channel_id=1, source_target_pairs={{0,16},{8,24},{16,32},{24,40},{32,48},{40,56},{48,64},{56,72},{64,... | collective-permute-start | bytes 798728 | tf_op jit(solution)/shard_map/ppermute | solution.py:18
  35.9 17.9 %collective-permute-start.1 = (bf16[520,256]{1,0:T(8,128)(2,1)S(1)}, bf16[520,256]{1,0:T(8,128)(2,1)S(1)}, u32[]{:S(2)}, u32[]{:S(2)}) collective-permute-start(bf16[520,256]{1,0:T(8,128)(2,1)S(1)} %collective-permute-done), channel_id=1, source_target_pairs={{0,16},{8,24},{16,32},{24,40},{32,48},{40,56},{48,64},{56,72},{64,... | collective-permute-start | bytes 798728 | tf_op jit(solution)/shard_map/ppermute | solution.py:18
  53.8 14.9 %collective-permute-start.2 = (bf16[520,256]{1,0:T(8,128)(2,1)S(1)}, bf16[520,256]{1,0:T(8,128)(2,1)}, u32[]{:S(2)}, u32[]{:S(2)}) collective-permute-start(bf16[520,256]{1,0:T(8,128)(2,1)S(1)} %collective-permute-done.1), channel_id=1, source_target_pairs={{0,16},{8,24},{16,32},{24,40},{32,48},{40,56},{48,64},{56,72},{64,... | collective-permute-start | bytes 798728 | tf_op jit(solution)/shard_map/ppermute | solution.py:18
  68.7 13.9 %collective-permute-start.3 = (bf16[520,256]{1,0:T(8,128)(2,1)}, bf16[520,256]{1,0:T(8,128)(2,1)S(1)}, u32[]{:S(2)}, u32[]{:S(2)}) collective-permute-start(bf16[520,256]{1,0:T(8,128)(2,1)} %collective-permute-done.2), channel_id=1, source_target_pairs={{0,16},{8,24},{16,32},{24,40},{32,48},{40,56},{48,64},{56,72},{64,... | collective-permute-start | bytes 798728 | tf_op jit(solution)/shard_map/ppermute | solution.py:18
  85.7 4.9 %collective-permute-start.4 = (bf16[4,520,256]{2,1,0:T(8,128)(2,1)}, bf16[4,520,256]{2,1,0:T(8,128)(2,1)}, u32[]{:S(2)}, u32[]{:S(2)}) collective-permute-start(bf16[4,520,256]{2,1,0:T(8,128)(2,1)} %constant_dynamic-slice_fusion), channel_id=1, source_target_pairs={{0,8},{8,0},{16,24},{24,16},{32,40},{40,32},{48,56},{56,48},{64,72... | collective-permute-start | bytes 3194888 | tf_op jit(solution)/shard_map/ppermute | solution.py:23
  112.7 6.2 %collective-permute-start.5 = (bf16[128,256]{0,1:T(8,128)(2,1)S(1)}, bf16[128,256]{0,1:T(8,128)(2,1)S(1)}, u32[]{:S(2)}, u32[]{:S(2)}) collective-permute-start(bf16[128,256]{0,1:T(8,128)(2,1)S(1)} %bitcast.111), channel_id=1, source_target_pairs={{0,1},{1,0},{2,3},{3,2},{4,5},{5,4},{6,7},{7,6},{8,9},{9,8},{10,11... | collective-permute-start | bytes 196616 | tf_op jit(solution)/shard_map/ppermute | solution.py:23
  115.8 6.4 %copy-start.4 = (f32[128,1152]{0,1:T(8,128)}, f32[128,1152]{0,1:T(8,128)S(1)}, u32[]{:S(2)}) copy-start(f32[128,1152]{0,1:T(8,128)S(1)} %get-tuple-element.25) | copy-start | bytes 1769476
  115.8 68.2 %copy-start.11 = (f32[128]{0:T(128)}, f32[128]{0:T(128)S(1)}, u32[]{:S(2)}) copy-start(f32[128]{0:T(128)S(1)} %get-tuple-element.24) | copy-start | bytes 1540
  118.9 8.4 %collective-permute-start.6 = (bf16[128,512]{0,1:T(8,128)(2,1)S(1)}, bf16[128,512]{0,1:T(8,128)(2,1)S(1)}, u32[]{:S(2)}, u32[]{:S(2)}) collective-permute-start(bf16[128,512]{0,1:T(8,128)(2,1)S(1)} %maximum_select_fusion.6), channel_id=1, source_target_pairs={{0,2},{1,3},{2,0},{3,1},{4,6},{5,7},{6,4},{7,5},{8,10},{9,11},{10,... | collective-permute-start | bytes 393224 | tf_op jit(solution)/shard_map/ppermute | solution.py:23
  122.5 61.6 %copy-start.12 = (f32[128]{0:T(128)}, f32[128]{0:T(128)S(1)}, u32[]{:S(2)}) copy-start(f32[128]{0:T(128)S(1)} %fusion.36) | copy-start | bytes 1540
  127.3 8.6 %collective-permute-start.7 = (bf16[128,1024]{0,1:T(8,128)(2,1)S(1)}, bf16[128,1024]{0,1:T(8,128)(2,1)}, u32[]{:S(2)}, u32[]{:S(2)}) collective-permute-start(bf16[128,1024]{0,1:T(8,128)(2,1)S(1)} %maximum_select_fusion.5), channel_id=1, source_target_pairs={{0,4},{1,5},{2,6},{3,7},{4,0},{5,1},{6,2},{7,3},{8,12},{9,13},{10,... | collective-permute-start | bytes 786440 | tf_op jit(solution)/shard_map/ppermute | solution.py:23
  142.6 8.6 %collective-permute-start.8 = (bf16[64,2304]{1,0:T(8,128)(2,1)S(1)}, bf16[64,2304]{1,0:T(8,128)(2,1)S(1)}, u32[]{:S(2)}, u32[]{:S(2)}) collective-permute-start(bf16[64,2304]{1,0:T(8,128)(2,1)S(1)} %select_convert_fusion), channel_id=1, source_target_pairs={{0,4},{1,5},{2,6},{3,7},{4,0},{5,1},{6,2},{7,3},{8,12},{9,13},{10,... | collective-permute-start | bytes 884744 | tf_op jit(solution)/shard_map/ppermute | solution.py:23
  152.6 9.9 %collective-permute-start.9 = (bf16[64,2304]{1,0:T(8,128)(2,1)S(1)}, bf16[64,2304]{1,0:T(8,128)(2,1)S(1)}, u32[]{:S(2)}, u32[]{:S(2)}) collective-permute-start(bf16[64,2304]{1,0:T(8,128)(2,1)S(1)} %get-tuple-element.12), channel_id=1, source_target_pairs={{0,1},{1,0},{2,3},{3,2},{4,5},{5,4},{6,7},{7,6},{8,9},{9,8},{10,11... | collective-permute-start | bytes 884744 | tf_op jit(solution)/shard_map/ppermute | solution.py:23
  162.5 19.4 %copy-start.14 = (bf16[256,2304]{1,0:T(8,128)(2,1)S(1)}, bf16[256,2304]{1,0:T(8,128)(2,1)}, u32[]{:S(2)}) copy-start(bf16[256,2304]{1,0:T(8,128)(2,1)} %param.22) | copy-start | bytes 3538948
  162.5 10.3 %collective-permute-start.10 = (bf16[64,2304]{1,0:T(8,128)(2,1)S(1)}, bf16[64,2304]{1,0:T(8,128)(2,1)S(1)}, u32[]{:S(2)}, u32[]{:S(2)}) collective-permute-start(bf16[64,2304]{1,0:T(8,128)(2,1)S(1)} %fusion.37), channel_id=1, source_target_pairs={{0,2},{1,3},{2,0},{3,1},{4,6},{5,7},{6,4},{7,5},{8,10},{9,11},{10,... | collective-permute-start | bytes 884744 | tf_op jit(solution)/shard_map/ppermute | solution.py:23
  172.9 9.6 %copy-start.5 = (f32[128,1152]{0,1:T(8,128)S(1)}, f32[128,1152]{0,1:T(8,128)}, u32[]{:S(2)}) copy-start(f32[128,1152]{0,1:T(8,128)} %copy-done.4) | copy-start | bytes 1769476
  172.9 9.0 %collective-permute-start.11 = (bf16[64,2304]{1,0:T(8,128)(2,1)S(1)}, bf16[64,2304]{1,0:T(8,128)(2,1)S(1)}, u32[]{:S(2)}, u32[]{:S(2)}) collective-permute-start(bf16[64,2304]{1,0:T(8,128)(2,1)S(1)} %add_convert_fusion), channel_id=1, source_target_pairs={{0,4},{1,5},{2,6},{3,7},{4,0},{5,1},{6,2},{7,3},{8,12},{9,13},{10,... | collective-permute-start | bytes 884744 | tf_op jit(solution)/shard_map/ppermute | solution.py:23
  193.1 4.9 %collective-permute-start.12 = (f32[4,256,256]{2,1,0:T(8,128)}, f32[4,256,256]{2,1,0:T(8,128)}, u32[]{:S(2)}, u32[]{:S(2)}) collective-permute-start(f32[4,256,256]{2,1,0:T(8,128)} %slice.79), channel_id=1, source_target_pairs={{0,8},{8,0},{16,24},{24,16},{32,40},{40,32},{48,56},{56,48},{64,72... | collective-permute-start | bytes 3145736 | tf_op jit(solution)/shard_map/ppermute | solution.py:23
  200.2 32.6 %copy-start.2 = (f32[5,256,256]{2,1,0:T(8,128)}, f32[5,256,256]{2,1,0:T(8,128)S(1)}, u32[]{:S(2)}) copy-start(f32[5,256,256]{2,1,0:T(8,128)S(1)} %select_add_fusion) | copy-start | bytes 3932164
  200.2 7.4 %collective-permute-start.13 = (bf16[256,256]{1,0:T(8,128)(2,1)S(1)}, bf16[256,256]{1,0:T(8,128)(2,1)S(1)}, u32[]{:S(2)}, u32[]{:S(2)}) collective-permute-start(bf16[256,256]{1,0:T(8,128)(2,1)S(1)} %fusion.48), channel_id=1, source_target_pairs={{16,0},{24,8},{32,16},{40,24},{48,32},{56,40},{64,48},{72,56},{80,... | collective-permute-start | bytes 393224 | tf_op jit(solution)/shard_map/ppermute | solution.py:18
  207.7 12.1 %collective-permute-start.14 = (bf16[256,256]{1,0:T(8,128)(2,1)S(1)}, bf16[256,256]{1,0:T(8,128)(2,1)S(1)}, u32[]{:S(2)}, u32[]{:S(2)}) collective-permute-start(bf16[256,256]{1,0:T(8,128)(2,1)S(1)} %fusion.39), channel_id=1, source_target_pairs={{16,0},{24,8},{32,16},{40,24},{48,32},{56,40},{64,48},{72,56},{80,... | collective-permute-start | bytes 393224 | tf_op jit(solution)/shard_map/ppermute | solution.py:18
  219.8 13.0 %collective-permute-start.15 = (bf16[256,256]{1,0:T(8,128)(2,1)S(1)}, bf16[256,256]{1,0:T(8,128)(2,1)S(1)}, u32[]{:S(2)}, u32[]{:S(2)}) collective-permute-start(bf16[256,256]{1,0:T(8,128)(2,1)S(1)} %fusion.41), channel_id=1, source_target_pairs={{16,0},{24,8},{32,16},{40,24},{48,32},{56,40},{64,48},{72,56},{80,... | collective-permute-start | bytes 393224 | tf_op jit(solution)/shard_map/ppermute | solution.py:18
  233.5 12.3 %collective-permute-start.16 = (bf16[256,256]{1,0:T(8,128)(2,1)}, bf16[256,256]{1,0:T(8,128)(2,1)}, u32[]{:S(2)}, u32[]{:S(2)}) collective-permute-start(bf16[256,256]{1,0:T(8,128)(2,1)} %fusion.43), channel_id=1, source_target_pairs={{16,0},{24,8},{32,16},{40,24},{48,32},{56,40},{64,48},{72,56},{80,... | collective-permute-start | bytes 393224 | tf_op jit(solution)/shard_map/ppermute | solution.py:18
  (10 other events, 29.0 us)

commit v6 on v5

--- a/solution.py
+++ b/solution.py
@@ -75,28 +75,36 @@
     )
 
 
-def window_probs(queries, keys_all, marks_query, marks_all, heads, depth, scale, block_rows):
-    query_part = queries.reshape(block_rows, heads, depth)
-    key_part = keys_all.reshape(block_rows + WINDOW, heads, depth)
-    scores = (
-        jnp.einsum("qhd,khd->hqk", query_part, key_part, preferred_element_type=jnp.float32) * scale
-    )
+def columns(value, head, depth):
+    return value[:, head * depth : (head + 1) * depth]
+
+
+def trans_dot(left, right):
+    return lax.dot_general(left, right, (((1,), (1,)), ((), ())), preferred_element_type=jnp.float32)
+
+
+def window_probs(queries, keys_all, marks_query, marks_all, depth, scale, block_rows):
     row_index = lax.broadcasted_iota(jnp.int32, (block_rows, block_rows + WINDOW), 0)
     col_index = lax.broadcasted_iota(jnp.int32, (block_rows, block_rows + WINDOW), 1)
     same_doc = marks_query[:, None] == marks_all[None, :]
     allowed = same_doc & (col_index > row_index) & (col_index <= row_index + WINDOW)
-    highest = jnp.max(jnp.where(allowed[None], scores, negative), axis=-1, keepdims=True)
-    weights = jnp.where(allowed[None], jnp.exp(scores - highest), 0.0)
-    totals = jnp.sum(weights, axis=-1, keepdims=True)
-    probability = weights / totals
-    return (probability, query_part, key_part)
-
-
-def mix_values(probability, values_all, block_rows, heads, depth):
-    value_part = values_all.reshape(block_rows + WINDOW, heads, depth)
-    rounded = probability.astype(jnp.bfloat16)
-    mixed = jnp.einsum("hqk,khd->qhd", rounded, value_part, preferred_element_type=jnp.float32)
-    return (mixed.astype(jnp.bfloat16).reshape(block_rows, heads * depth), rounded, value_part)
+    result = []
+    for head in range(queries.shape[1] // depth):
+        scores = trans_dot(columns(queries, head, depth), columns(keys_all, head, depth)) * scale
+        highest = jnp.max(jnp.where(allowed, scores, negative), axis=-1, keepdims=True)
+        weights = jnp.where(allowed, jnp.exp(scores - highest), 0.0)
+        totals = jnp.sum(weights, axis=-1, keepdims=True)
+        result.append(weights / totals)
+    return result
+
+
+def mix_values(probability, values_all, depth):
+    rounded = [part.astype(jnp.bfloat16) for part in probability]
+    mixed = [
+        jnp.dot(part, columns(values_all, head, depth), preferred_element_type=jnp.float32)
+        for head, part in enumerate(rounded)
+    ]
+    return jnp.concatenate(mixed, 1).astype(jnp.bfloat16), rounded
 
 
 def shards(
@@ -144,10 +152,10 @@
         window[:, 4 * rows :].reshape(window.shape[0], 8 * width)[:, :rows].reshape(span)
     ).astype(jnp.int32)
 
-    probability, _, _ = window_probs(
-        teacher_query, keys_teacher, doc_marks, marks_all, heads_t, DH_T, teacher_scale, rows
-    )
-    teacher_mix, _, _ = mix_values(probability, values_teacher, rows, heads_t, DH_T)
+    probability = window_probs(
+        teacher_query, keys_teacher, doc_marks, marks_all, DH_T, teacher_scale, rows
+    )
+    teacher_mix, _ = mix_values(probability, values_teacher, DH_T)
     target_cols = lax.dot_general(
         gather_doubling(teacher_mix, "head", 1),
         teacher_out_proj,
@@ -155,12 +163,10 @@
         preferred_element_type=jnp.float32,
     ).astype(jnp.bfloat16)
 
-    probability, query_part, key_part = window_probs(
-        student_query, keys_student, doc_marks, marks_all, heads_s, DH_S, student_scale, rows
-    )
-    student_mix, rounded, value_part = mix_values(
-        probability, values_student, rows, heads_s, DH_S
-    )
+    probability = window_probs(
+        student_query, keys_student, doc_marks, marks_all, DH_S, student_scale, rows
+    )
+    student_mix, rounded = mix_values(probability, values_student, DH_S)
     lang_table = lax.broadcasted_iota(jnp.int32, (rows, language_weight.shape[0]), 1)
     token_weight = jnp.sum(
         jnp.where(language_ids[:, None] == lang_table, language_weight[None, :], 0.0), axis=1
@@ -177,19 +183,24 @@
         preferred_element_type=jnp.float32,
     ).astype(jnp.bfloat16)
 
-    grad_part = grad_heads.reshape(rows, heads_s, DH_S)
-    grad_probs = jnp.einsum(
-        "qhd,khd->hqk", grad_part, value_part, preferred_element_type=jnp.float32
-    )
-    inner = jnp.sum(probability * grad_probs, axis=-1, keepdims=True)
-    grad_scores = (probability * (grad_probs - inner)).astype(jnp.bfloat16)
-    grad_q = student_scale * jnp.einsum(
-        "hqk,khd->qhd", grad_scores, key_part, preferred_element_type=jnp.float32
-    )
-    grad_k = student_scale * jnp.einsum(
-        "hqk,qhd->khd", grad_scores, query_part, preferred_element_type=jnp.float32
-    )
-    grad_v = jnp.einsum("hqk,qhd->khd", rounded, grad_part, preferred_element_type=jnp.float32)
+    grad_q, grad_k, grad_v = [], [], []
+    for head, (part, low) in enumerate(zip(probability, rounded)):
+        grad_here = columns(grad_heads, head, DH_S)
+        grad_probs = trans_dot(grad_here, columns(values_student, head, DH_S))
+        inner = jnp.sum(part * grad_probs, axis=-1, keepdims=True)
+        grad_scores = (part * (grad_probs - inner)).astype(jnp.bfloat16)
+        grad_q.append(
+            student_scale
+            * jnp.dot(grad_scores, columns(keys_student, head, DH_S), preferred_element_type=jnp.float32)
+        )
+        grad_k.append(
+            student_scale
+            * jnp.dot(grad_scores.T, columns(student_query, head, DH_S), preferred_element_type=jnp.float32)
+        )
+        grad_v.append(jnp.dot(low.T, grad_here, preferred_element_type=jnp.float32))
+    grad_q = jnp.concatenate(grad_q, 1)
+    grad_k = jnp.concatenate(grad_k, 1)
+    grad_v = jnp.concatenate(grad_v, 1)
     blocks = span // rows
     grads = jnp.concatenate(
         [grad_k.reshape(blocks, rows, width), grad_v.reshape(blocks, rows, width)], 1
@@ -205,7 +216,7 @@
     total = even[0]
     for k in range(1, steps + 1):
         total = even[k] + shifted(total.astype(jnp.bfloat16), "seq", -2).astype(jnp.float32)
-    return (grad_q.reshape(rows, width), total[:rows], total[rows:])
+    return (grad_q, total[:rows], total[rows:])
 
 
 def solution(mesh):

time: 249 us -> 225 us (0.904)
  local copies, waits for them, and re-layouts: 37.5 us -> 15.8 us
  waiting for transfers between devices: 113 us -> 116 us
  matrix products: 16.2 us -> 13.4 us
    unnamed x52 -> x45, local copies, waits for them, and re-layouts: 20.5 us -> 10.9 us
    another operation x2 -> x0, local copies, waits for them, and re-layouts: 5.03 us -> none  [the longest x1 2.52 us: window_probs(): key_part = keys_all.reshape(block_rows + WINDOW, heads, depth)]
    transpose x1 -> x0, local copies, waits for them, and re-layouts: 2.66 us -> none  [shards(): jnp.einsum('hqk,qhd->khd', rounded, grad_part, preferred_element_type=jnp...]
    dot_general x7 -> x9, matrix products: 6.74 us -> 4.3 us  [the longest x4 1.61 us: trans_dot(): lax.dot_general(left, right, (((1,), (1,)), ((), ())), preferred_element_...]
  transfers between devices with their start and end apart: 17 -> 17, of which waited for: 17 -> 17; matrix products, arithmetic and copies ran while one was open for 5% -> 4% of each run, Pallas kernels for 0% -> 0%
where the time goes in v6:
time: 225 us; the launch traced here: 224 us
  waiting for transfers between devices  116 us (52%)
  starting transfers between devices  68.6 us (30%)
  local copies, waits for them, and re-layouts  15.8 us (7%)
  matrix products  13.4 us (6%)
  other arithmetic  9.56 us (4%)
    ppermute x8, waiting for transfers between devices, shifted(): return lax.ppermute(value, axis, pairs)  75.9 us
    ppermute x8, starting transfers between devices, shifted(): return lax.ppermute(value, axis, pairs)  41.5 us
    ppermute x9, waiting for transfers between devices, swapped(): return lax.ppermute(value, axis, [(i, i ^ bit) for i in range(length)])  39.8 us
    ppermute x9, starting transfers between devices, swapped(): return lax.ppermute(value, axis, [(i, i ^ bit) for i in range(length)])  27.1 us
    unnamed x45, local copies, waits for them, and re-layouts  10.9 us
    dot_general x1, matrix products, shards(): jnp.dot(target_cols, match_proj, preferred_element_type=jnp.float32)  4.89 us
  transfers between devices with their start and end apart: 17, of which 17 were waited for; matrix products, arithmetic and copies ran while one was open for 4% of the time, Pallas kernels for 0%

profile of v6, /device:TPU:46, one launch (start us, length us, event | category | flops | bytes accessed | tf_op | source)
XLA Modules:
  0.0 224.2 jit_solution(2841319018721564450)
XLA Ops:
  4.9 4.3 %collective-permute-start = (bf16[520,256]{1,0:T(8,128)(2,1)S(1)}, bf16[520,256]{1,0:T(8,128)(2,1)S(1)}, u32[]{:S(2)}, u32[]{:S(2)}) collective-permute-start(bf16[520,256]{1,0:T(8,128)(2,1)S(1)} %constant_dynamic-update-slice_fusion), channel_id=1, source_target_pairs={{0,16},{8,24},{16,32},{24,40},{32,48},{40,56},{48,64},{56,72},{64,... | collective-permute-start | bytes 798728 | tf_op jit(solution)/shard_map/ppermute | solution.py:18
  9.1 26.8 %collective-permute-done = bf16[520,256]{1,0:T(8,128)(2,1)S(1)} collective-permute-done((bf16[520,256]{1,0:T(8,128)(2,1)S(1)}, bf16[520,256]{1,0:T(8,128)(2,1)S(1)}, u32[]{:S(2)}, u32[]{:S(2)}) %collective-permute-start) | collective-permute-done | bytes 266272 | tf_op jit(solution)/shard_map/ppermute | solution.py:18
  37.8 15.9 %collective-permute-done.1 = bf16[520,256]{1,0:T(8,128)(2,1)S(1)} collective-permute-done((bf16[520,256]{1,0:T(8,128)(2,1)S(1)}, bf16[520,256]{1,0:T(8,128)(2,1)S(1)}, u32[]{:S(2)}, u32[]{:S(2)}) %collective-permute-start.1) | collective-permute-done | bytes 266272 | tf_op jit(solution)/shard_map/ppermute | solution.py:18
  57.1 11.6 %collective-permute-done.2 = bf16[520,256]{1,0:T(8,128)(2,1)} collective-permute-done((bf16[520,256]{1,0:T(8,128)(2,1)S(1)}, bf16[520,256]{1,0:T(8,128)(2,1)}, u32[]{:S(2)}, u32[]{:S(2)}) %collective-permute-start.2) | collective-permute-done | bytes 266272 | tf_op jit(solution)/shard_map/ppermute | solution.py:18
  73.0 9.5 %collective-permute-done.3 = bf16[520,256]{1,0:T(8,128)(2,1)S(1)} collective-permute-done((bf16[520,256]{1,0:T(8,128)(2,1)}, bf16[520,256]{1,0:T(8,128)(2,1)S(1)}, u32[]{:S(2)}, u32[]{:S(2)}) %collective-permute-start.3) | collective-permute-done | bytes 266272 | tf_op jit(solution)/shard_map/ppermute | solution.py:18
  94.5 2.7 %collective-permute-start.5 = (bf16[128,256]{0,1:T(8,128)(2,1)S(1)}, bf16[128,256]{0,1:T(8,128)(2,1)}, u32[]{:S(2)}, u32[]{:S(2)}) collective-permute-start(bf16[128,256]{0,1:T(8,128)(2,1)S(1)} %pad_maximum_fusion.1), channel_id=1, source_target_pairs={{0,1},{1,0},{2,3},{3,2},{4,5},{5,4},{6,7},{7,6},{8,9},{9,8},{10,11... | collective-permute-start | bytes 196616 | tf_op jit(solution)/shard_map/ppermute | solution.py:23
  97.3 3.5 %collective-permute-done.5 = bf16[128,256]{0,1:T(8,128)(2,1)} collective-permute-done((bf16[128,256]{0,1:T(8,128)(2,1)S(1)}, bf16[128,256]{0,1:T(8,128)(2,1)}, u32[]{:S(2)}, u32[]{:S(2)}) %collective-permute-start.5) | collective-permute-done | bytes 65568 | tf_op jit(solution)/shard_map/ppermute | solution.py:23
  101.7 3.3 %collective-permute-start.6 = (bf16[128,512]{0,1:T(8,128)(2,1)S(1)}, bf16[128,512]{0,1:T(8,128)(2,1)}, u32[]{:S(2)}, u32[]{:S(2)}) collective-permute-start(bf16[128,512]{0,1:T(8,128)(2,1)S(1)} %maximum_select_fusion.6), channel_id=1, source_target_pairs={{0,2},{1,3},{2,0},{3,1},{4,6},{5,7},{6,4},{7,5},{8,10},{9,11},{10,... | collective-permute-start | bytes 393224 | tf_op jit(solution)/shard_map/ppermute | solution.py:23
  105.2 5.0 %collective-permute-done.6 = bf16[128,512]{0,1:T(8,128)(2,1)} collective-permute-done((bf16[128,512]{0,1:T(8,128)(2,1)S(1)}, bf16[128,512]{0,1:T(8,128)(2,1)}, u32[]{:S(2)}, u32[]{:S(2)}) %collective-permute-start.6) | collective-permute-done | bytes 131104 | tf_op jit(solution)/shard_map/ppermute | solution.py:23
  111.4 4.2 %collective-permute-start.7 = (bf16[128,1024]{0,1:T(8,128)(2,1)S(1)}, bf16[128,1024]{0,1:T(8,128)(2,1)}, u32[]{:S(2)}, u32[]{:S(2)}) collective-permute-start(bf16[128,1024]{0,1:T(8,128)(2,1)S(1)} %maximum_select_fusion.5), channel_id=1, source_target_pairs={{0,4},{1,5},{2,6},{3,7},{4,0},{5,1},{6,2},{7,3},{8,12},{9,13},{10,... | collective-permute-start | bytes 786440 | tf_op jit(solution)/shard_map/ppermute | solution.py:23
  115.6 3.7 %fusion.4 = f32[128,2304]{1,0:T(8,128)} fusion(bf16[256,2304]{1,0:T(8,128)(2,1)} %param.22, bf16[1152,256]{1,0:T(8,128)(2,1)} %bitcast.77, f32[128,1152]{0,1:T(8,128)} %copy-done.2, f32[128]{0:T(128)S(1)} %get-tuple-element.4, f32[128]{0:T(128)S(1)} %get-tuple-element.7, s32[128]{0:T(128)S(1)} %get-tuple-element.24, s32[128]{0:T(128)S(1)} %get-tuple-element.18, ...), kind=kOutput, calls=%fused_computation.15 | convolution fusion | flops 227852288 | bytes 3545600 | tf_op jit(solution)/shard_map/dot_general | solution.py:175
  120.0 4.9 %fusion = f32[128,2304]{1,0:T(8,128)} fusion(f32[128,2304]{1,0:T(8,128)} %fusion.4, bf16[576,2304]{1,0:T(8,128)(2,1)S(1)} %copy-done, bf16[576,2048]{1,0:T(8,128)(2,1)} %param.21, f32[128]{0:T(128)S(1)} %select_reduce_fusion.3, bf16[128,1024]{0,1:T(8,128)(2,1)S(1)} %maximum_select_fusion.5, bf16[128,1024]{0,1:T(8,128)(2,1)} %collective-permute-done.7, ...), kind=kOutput, calls=%fused_computation.1 | convolution fusion | flops 644751360 | bytes 7897601 | tf_op jit(solution)/shard_map/dot_general | solution.py:176
  126.2 3.9 %collective-permute-start.8 = (bf16[64,2304]{1,0:T(8,128)(2,1)S(1)}, bf16[64,2304]{1,0:T(8,128)(2,1)S(1)}, u32[]{:S(2)}, u32[]{:S(2)}) collective-permute-start(bf16[64,2304]{1,0:T(8,128)(2,1)S(1)} %select_convert_fusion), channel_id=1, source_target_pairs={{0,4},{1,5},{2,6},{3,7},{4,0},{5,1},{6,2},{7,3},{8,12},{9,13},{10,... | collective-permute-start | bytes 884744 | tf_op jit(solution)/shard_map/ppermute | solution.py:23
  130.1 4.7 %collective-permute-done.8 = bf16[64,2304]{1,0:T(8,128)(2,1)S(1)} collective-permute-done((bf16[64,2304]{1,0:T(8,128)(2,1)S(1)}, bf16[64,2304]{1,0:T(8,128)(2,1)S(1)}, u32[]{:S(2)}, u32[]{:S(2)}) %collective-permute-start.8) | collective-permute-done | bytes 294944 | tf_op jit(solution)/shard_map/ppermute | solution.py:23
  136.2 2.9 %collective-permute-start.9 = (bf16[64,2304]{1,0:T(8,128)(2,1)S(1)}, bf16[64,2304]{1,0:T(8,128)(2,1)S(1)}, u32[]{:S(2)}, u32[]{:S(2)}) collective-permute-start(bf16[64,2304]{1,0:T(8,128)(2,1)S(1)} %get-tuple-element.8), channel_id=1, source_target_pairs={{0,1},{1,0},{2,3},{3,2},{4,5},{5,4},{6,7},{7,6},{8,9},{9,8},{10,11... | collective-permute-start | bytes 884744 | tf_op jit(solution)/shard_map/ppermute | solution.py:23
  139.0 7.3 %collective-permute-done.9 = bf16[64,2304]{1,0:T(8,128)(2,1)S(1)} collective-permute-done((bf16[64,2304]{1,0:T(8,128)(2,1)S(1)}, bf16[64,2304]{1,0:T(8,128)(2,1)S(1)}, u32[]{:S(2)}, u32[]{:S(2)}) %collective-permute-start.9) | collective-permute-done | bytes 294944 | tf_op jit(solution)/shard_map/ppermute | solution.py:23
  148.3 8.2 %collective-permute-done.10 = bf16[64,2304]{1,0:T(8,128)(2,1)S(1)} collective-permute-done((bf16[64,2304]{1,0:T(8,128)(2,1)S(1)}, bf16[64,2304]{1,0:T(8,128)(2,1)S(1)}, u32[]{:S(2)}, u32[]{:S(2)}) %collective-permute-start.10) | collective-permute-done | bytes 294944 | tf_op jit(solution)/shard_map/ppermute | solution.py:23
  156.6 4.3 %collective-permute-start.11 = (bf16[64,2304]{1,0:T(8,128)(2,1)S(1)}, bf16[64,2304]{1,0:T(8,128)(2,1)S(1)}, u32[]{:S(2)}, u32[]{:S(2)}) collective-permute-start(bf16[64,2304]{1,0:T(8,128)(2,1)S(1)} %add_convert_fusion), channel_id=1, source_target_pairs={{0,4},{1,5},{2,6},{3,7},{4,0},{5,1},{6,2},{7,3},{8,12},{9,13},{10,... | collective-permute-start | bytes 884744 | tf_op jit(solution)/shard_map/ppermute | solution.py:23
  161.0 4.7 %collective-permute-done.11 = bf16[64,2304]{1,0:T(8,128)(2,1)S(1)} collective-permute-done((bf16[64,2304]{1,0:T(8,128)(2,1)S(1)}, bf16[64,2304]{1,0:T(8,128)(2,1)S(1)}, u32[]{:S(2)}, u32[]{:S(2)}) %collective-permute-start.11) | collective-permute-done | bytes 294944 | tf_op jit(solution)/shard_map/ppermute | solution.py:23
  173.6 3.0 %collective-permute-done.12 = f32[4,256,256]{2,1,0:T(8,128)} collective-permute-done((f32[4,256,256]{2,1,0:T(8,128)}, f32[4,256,256]{2,1,0:T(8,128)}, u32[]{:S(2)}, u32[]{:S(2)}) %collective-permute-start.12) | collective-permute-done | bytes 1048608 | tf_op jit(solution)/shard_map/ppermute | solution.py:23
  180.7 5.5 %collective-permute-done.13 = bf16[256,256]{1,0:T(8,128)(2,1)S(1)} collective-permute-done((bf16[256,256]{1,0:T(8,128)(2,1)S(1)}, bf16[256,256]{1,0:T(8,128)(2,1)S(1)}, u32[]{:S(2)}, u32[]{:S(2)}) %collective-permute-start.13) | collective-permute-done | bytes 131104 | tf_op jit(solution)/shard_map/ppermute | solution.py:18
  186.2 9.6 %collective-permute-start.14 = (bf16[256,256]{1,0:T(8,128)(2,1)S(1)}, bf16[256,256]{1,0:T(8,128)(2,1)S(1)}, u32[]{:S(2)}, u32[]{:S(2)}) collective-permute-start(bf16[256,256]{1,0:T(8,128)(2,1)S(1)} %fusion.35), channel_id=1, source_target_pairs={{16,0},{24,8},{32,16},{40,24},{48,32},{56,40},{64,48},{72,56},{80,... | collective-permute-start | bytes 393224 | tf_op jit(solution)/shard_map/ppermute | solution.py:18
  198.3 10.5 %collective-permute-start.15 = (bf16[256,256]{1,0:T(8,128)(2,1)S(1)}, bf16[256,256]{1,0:T(8,128)(2,1)S(1)}, u32[]{:S(2)}, u32[]{:S(2)}) collective-permute-start(bf16[256,256]{1,0:T(8,128)(2,1)S(1)} %fusion.37), channel_id=1, source_target_pairs={{16,0},{24,8},{32,16},{40,24},{48,32},{56,40},{64,48},{72,56},{80,... | collective-permute-start | bytes 393224 | tf_op jit(solution)/shard_map/ppermute | solution.py:18
  211.4 9.6 %collective-permute-start.16 = (bf16[256,256]{1,0:T(8,128)(2,1)S(1)}, bf16[256,256]{1,0:T(8,128)(2,1)S(1)}, u32[]{:S(2)}, u32[]{:S(2)}) collective-permute-start(bf16[256,256]{1,0:T(8,128)(2,1)S(1)} %fusion.39), channel_id=1, source_target_pairs={{16,0},{24,8},{32,16},{40,24},{48,32},{56,40},{64,48},{72,56},{80,... | collective-permute-start | bytes 393224 | tf_op jit(solution)/shard_map/ppermute | solution.py:18
  (96 shorter events, 53.6 us)
Async XLA Ops:
  0.6 119.4 %copy-start = (bf16[576,2304]{1,0:T(8,128)(2,1)S(1)}, bf16[576,2304]{1,0:T(8,128)(2,1)}, u32[]{:S(2)}) copy-start(bf16[576,2304]{1,0:T(8,128)(2,1)} %param.23) | copy-start | bytes 7962628
  4.9 31.0 %collective-permute-start = (bf16[520,256]{1,0:T(8,128)(2,1)S(1)}, bf16[520,256]{1,0:T(8,128)(2,1)S(1)}, u32[]{:S(2)}, u32[]{:S(2)}) collective-permute-start(bf16[520,256]{1,0:T(8,128)(2,1)S(1)} %constant_dynamic-update-slice_fusion), channel_id=1, source_target_pairs={{0,16},{8,24},{16,32},{24,40},{32,48},{40,56},{48,64},{56,72},{64,... | collective-permute-start | bytes 798728 | tf_op jit(solution)/shard_map/ppermute | solution.py:18
  35.9 17.9 %collective-permute-start.1 = (bf16[520,256]{1,0:T(8,128)(2,1)S(1)}, bf16[520,256]{1,0:T(8,128)(2,1)S(1)}, u32[]{:S(2)}, u32[]{:S(2)}) collective-permute-start(bf16[520,256]{1,0:T(8,128)(2,1)S(1)} %collective-permute-done), channel_id=1, source_target_pairs={{0,16},{8,24},{16,32},{24,40},{32,48},{40,56},{48,64},{56,72},{64,... | collective-permute-start | bytes 798728 | tf_op jit(solution)/shard_map/ppermute | solution.py:18
  53.8 14.9 %collective-permute-start.2 = (bf16[520,256]{1,0:T(8,128)(2,1)S(1)}, bf16[520,256]{1,0:T(8,128)(2,1)}, u32[]{:S(2)}, u32[]{:S(2)}) collective-permute-start(bf16[520,256]{1,0:T(8,128)(2,1)S(1)} %collective-permute-done.1), channel_id=1, source_target_pairs={{0,16},{8,24},{16,32},{24,40},{32,48},{40,56},{48,64},{56,72},{64,... | collective-permute-start | bytes 798728 | tf_op jit(solution)/shard_map/ppermute | solution.py:18
  68.7 13.9 %collective-permute-start.3 = (bf16[520,256]{1,0:T(8,128)(2,1)}, bf16[520,256]{1,0:T(8,128)(2,1)S(1)}, u32[]{:S(2)}, u32[]{:S(2)}) collective-permute-start(bf16[520,256]{1,0:T(8,128)(2,1)} %collective-permute-done.2), channel_id=1, source_target_pairs={{0,16},{8,24},{16,32},{24,40},{32,48},{40,56},{48,64},{56,72},{64,... | collective-permute-start | bytes 798728 | tf_op jit(solution)/shard_map/ppermute | solution.py:18
  84.6 4.6 %collective-permute-start.4 = (bf16[4,520,256]{2,1,0:T(8,128)(2,1)S(1)}, bf16[4,520,256]{2,1,0:T(8,128)(2,1)S(1)}, u32[]{:S(2)}, u32[]{:S(2)}) collective-permute-start(bf16[4,520,256]{2,1,0:T(8,128)(2,1)S(1)} %constant_dynamic-slice_fusion), channel_id=1, source_target_pairs={{0,8},{8,0},{16,24},{24,16},{32,40},{40,32},{48,56},{56,48},{64,72... | collective-permute-start | bytes 3194888 | tf_op jit(solution)/shard_map/ppermute | solution.py:23
  92.6 74.0 %copy-start.8 = (f32[128]{0:T(128)}, f32[128]{0:T(128)S(1)}, u32[]{:S(2)}) copy-start(f32[128]{0:T(128)S(1)} %get-tuple-element.7) | copy-start | bytes 1540
  93.1 73.5 %copy-start.9 = (f32[128]{0:T(128)}, f32[128]{0:T(128)S(1)}, u32[]{:S(2)}) copy-start(f32[128]{0:T(128)S(1)} %get-tuple-element.4) | copy-start | bytes 1540
  94.0 11.2 %copy-start.12 = (f32[16]{0:T(128)S(1)}, f32[16]{0:T(128)}, u32[]{:S(2)}) copy-start(f32[16]{0:T(128)} %param.20) | copy-start | bytes 196
  94.0 11.2 %copy-start.13 = (s32[128]{0:T(128)S(1)}, s32[128]{0:T(128)}, u32[]{:S(2)}) copy-start(s32[128]{0:T(128)} %param.19) | copy-start | bytes 1540
  94.5 6.3 %collective-permute-start.5 = (bf16[128,256]{0,1:T(8,128)(2,1)S(1)}, bf16[128,256]{0,1:T(8,128)(2,1)}, u32[]{:S(2)}, u32[]{:S(2)}) collective-permute-start(bf16[128,256]{0,1:T(8,128)(2,1)S(1)} %pad_maximum_fusion.1), channel_id=1, source_target_pairs={{0,1},{1,0},{2,3},{3,2},{4,5},{5,4},{6,7},{7,6},{8,9},{9,8},{10,11... | collective-permute-start | bytes 196616 | tf_op jit(solution)/shard_map/ppermute | solution.py:23
  101.7 8.5 %collective-permute-start.6 = (bf16[128,512]{0,1:T(8,128)(2,1)S(1)}, bf16[128,512]{0,1:T(8,128)(2,1)}, u32[]{:S(2)}, u32[]{:S(2)}) collective-permute-start(bf16[128,512]{0,1:T(8,128)(2,1)S(1)} %maximum_select_fusion.6), channel_id=1, source_target_pairs={{0,2},{1,3},{2,0},{3,1},{4,6},{5,7},{6,4},{7,5},{8,10},{9,11},{10,... | collective-permute-start | bytes 393224 | tf_op jit(solution)/shard_map/ppermute | solution.py:23
  111.4 8.6 %collective-permute-start.7 = (bf16[128,1024]{0,1:T(8,128)(2,1)S(1)}, bf16[128,1024]{0,1:T(8,128)(2,1)}, u32[]{:S(2)}, u32[]{:S(2)}) collective-permute-start(bf16[128,1024]{0,1:T(8,128)(2,1)S(1)} %maximum_select_fusion.5), channel_id=1, source_target_pairs={{0,4},{1,5},{2,6},{3,7},{4,0},{5,1},{6,2},{7,3},{8,12},{9,13},{10,... | collective-permute-start | bytes 786440 | tf_op jit(solution)/shard_map/ppermute | solution.py:23
  126.2 8.6 %collective-permute-start.8 = (bf16[64,2304]{1,0:T(8,128)(2,1)S(1)}, bf16[64,2304]{1,0:T(8,128)(2,1)S(1)}, u32[]{:S(2)}, u32[]{:S(2)}) collective-permute-start(bf16[64,2304]{1,0:T(8,128)(2,1)S(1)} %select_convert_fusion), channel_id=1, source_target_pairs={{0,4},{1,5},{2,6},{3,7},{4,0},{5,1},{6,2},{7,3},{8,12},{9,13},{10,... | collective-permute-start | bytes 884744 | tf_op jit(solution)/shard_map/ppermute | solution.py:23
  136.2 29.5 %copy-start.10 = (bf16[256,2304]{1,0:T(8,128)(2,1)S(1)}, bf16[256,2304]{1,0:T(8,128)(2,1)}, u32[]{:S(2)}) copy-start(bf16[256,2304]{1,0:T(8,128)(2,1)} %param.22) | copy-start | bytes 3538948
  136.2 10.2 %collective-permute-start.9 = (bf16[64,2304]{1,0:T(8,128)(2,1)S(1)}, bf16[64,2304]{1,0:T(8,128)(2,1)S(1)}, u32[]{:S(2)}, u32[]{:S(2)}) collective-permute-start(bf16[64,2304]{1,0:T(8,128)(2,1)S(1)} %get-tuple-element.8), channel_id=1, source_target_pairs={{0,1},{1,0},{2,3},{3,2},{4,5},{5,4},{6,7},{7,6},{8,9},{9,8},{10,11... | collective-permute-start | bytes 884744 | tf_op jit(solution)/shard_map/ppermute | solution.py:23
  146.4 10.1 %collective-permute-start.10 = (bf16[64,2304]{1,0:T(8,128)(2,1)S(1)}, bf16[64,2304]{1,0:T(8,128)(2,1)S(1)}, u32[]{:S(2)}, u32[]{:S(2)}) collective-permute-start(bf16[64,2304]{1,0:T(8,128)(2,1)S(1)} %fusion.29), channel_id=1, source_target_pairs={{0,2},{1,3},{2,0},{3,1},{4,6},{5,7},{6,4},{7,5},{8,10},{9,11},{10,... | collective-permute-start | bytes 884744 | tf_op jit(solution)/shard_map/ppermute | solution.py:23
  156.6 9.6 %copy-start.3 = (f32[128,1152]{0,1:T(8,128)S(1)}, f32[128,1152]{0,1:T(8,128)}, u32[]{:S(2)}) copy-start(f32[128,1152]{0,1:T(8,128)} %copy-done.2) | copy-start | bytes 1769476
  156.6 9.0 %collective-permute-start.11 = (bf16[64,2304]{1,0:T(8,128)(2,1)S(1)}, bf16[64,2304]{1,0:T(8,128)(2,1)S(1)}, u32[]{:S(2)}, u32[]{:S(2)}) collective-permute-start(bf16[64,2304]{1,0:T(8,128)(2,1)S(1)} %add_convert_fusion), channel_id=1, source_target_pairs={{0,4},{1,5},{2,6},{3,7},{4,0},{5,1},{6,2},{7,3},{8,12},{9,13},{10,... | collective-permute-start | bytes 884744 | tf_op jit(solution)/shard_map/ppermute | solution.py:23
  171.7 4.9 %collective-permute-start.12 = (f32[4,256,256]{2,1,0:T(8,128)}, f32[4,256,256]{2,1,0:T(8,128)}, u32[]{:S(2)}, u32[]{:S(2)}) collective-permute-start(f32[4,256,256]{2,1,0:T(8,128)} %slice.103), channel_id=1, source_target_pairs={{0,8},{8,0},{16,24},{24,16},{32,40},{40,32},{48,56},{56,48},{64,72... | collective-permute-start | bytes 3145736 | tf_op jit(solution)/shard_map/ppermute | solution.py:23
  178.8 7.4 %collective-permute-start.13 = (bf16[256,256]{1,0:T(8,128)(2,1)S(1)}, bf16[256,256]{1,0:T(8,128)(2,1)S(1)}, u32[]{:S(2)}, u32[]{:S(2)}) collective-permute-start(bf16[256,256]{1,0:T(8,128)(2,1)S(1)} %fusion.45), channel_id=1, source_target_pairs={{16,0},{24,8},{32,16},{40,24},{48,32},{56,40},{64,48},{72,56},{80,... | collective-permute-start | bytes 393224 | tf_op jit(solution)/shard_map/ppermute | solution.py:18
  186.2 12.1 %collective-permute-start.14 = (bf16[256,256]{1,0:T(8,128)(2,1)S(1)}, bf16[256,256]{1,0:T(8,128)(2,1)S(1)}, u32[]{:S(2)}, u32[]{:S(2)}) collective-permute-start(bf16[256,256]{1,0:T(8,128)(2,1)S(1)} %fusion.35), channel_id=1, source_target_pairs={{16,0},{24,8},{32,16},{40,24},{48,32},{56,40},{64,48},{72,56},{80,... | collective-permute-start | bytes 393224 | tf_op jit(solution)/shard_map/ppermute | solution.py:18
  198.3 13.0 %collective-permute-start.15 = (bf16[256,256]{1,0:T(8,128)(2,1)S(1)}, bf16[256,256]{1,0:T(8,128)(2,1)S(1)}, u32[]{:S(2)}, u32[]{:S(2)}) collective-permute-start(bf16[256,256]{1,0:T(8,128)(2,1)S(1)} %fusion.37), channel_id=1, source_target_pairs={{16,0},{24,8},{32,16},{40,24},{48,32},{56,40},{64,48},{72,56},{80,... | collective-permute-start | bytes 393224 | tf_op jit(solution)/shard_map/ppermute | solution.py:18
  211.4 12.1 %collective-permute-start.16 = (bf16[256,256]{1,0:T(8,128)(2,1)S(1)}, bf16[256,256]{1,0:T(8,128)(2,1)S(1)}, u32[]{:S(2)}, u32[]{:S(2)}) collective-permute-start(bf16[256,256]{1,0:T(8,128)(2,1)S(1)} %fusion.39), channel_id=1, source_target_pairs={{16,0},{24,8},{32,16},{40,24},{48,32},{56,40},{64,48},{72,56},{80,... | collective-permute-start | bytes 393224 | tf_op jit(solution)/shard_map/ppermute | solution.py:18
  (7 other events, 10.3 us)

commit v7 on v6

--- a/solution.py
+++ b/solution.py
@@ -131,12 +131,18 @@
     doc_marks = segment_ids + 1
     mark_rows = jnp.pad(doc_marks.astype(jnp.bfloat16), (0, 8 * width - rows)).reshape(8, width)
     own = jnp.concatenate([teacher_key, teacher_value, student_key, student_value, mark_rows], 0)
+    core = lax.axis_index("seq") % 2
     chain = [own]
+    partner = []
+    pending = None
     for _ in range(steps):
-        chain.append(shifted(chain[-1], "seq", 2))
-    core = lax.axis_index("seq") % 2
-    stacked = jnp.stack(chain)
-    partner = swapped(lax.dynamic_slice_in_dim(stacked, core, steps, 0), "seq", 1)
+        step = shifted(chain[-1], "seq", 2)
+        if pending is not None:
+            step, pending = lax.optimization_barrier((step, pending))
+            partner.append(pending)
+        chain.append(step)
+        pending = swapped(jnp.where(core == 0, chain[-2], chain[-1]), "seq", 1)
+    partner.append(pending)
     pieces = []
     for k in range(steps, 0, -1):
         pieces.append(chain[k])
@@ -205,7 +211,7 @@
     grads = jnp.concatenate(
         [grad_k.reshape(blocks, rows, width), grad_v.reshape(blocks, rows, width)], 1
     )
-    from_partner = swapped(grads[1::2], "seq", 1)
+    from_partner = swapped(grads[1::2].astype(jnp.bfloat16), "seq", 1).astype(jnp.float32)
     nothing = jnp.zeros_like(from_partner[:1])
     added = jnp.where(
         core == 1,

time: 225 us -> 236 us (1.049)
  waiting for transfers between devices: 116 us -> 127 us
  local copies, waits for them, and re-layouts: 15.8 us -> 8.23 us
  starting transfers between devices: 68.6 us -> 75 us
    ppermute x8, waiting for transfers between devices: 75.9 us -> 90.9 us  [shifted(): return lax.ppermute(value, axis, pairs)]
    ppermute x9 -> x12, starting transfers between devices: 27.1 us -> 33.3 us  [swapped(): return lax.ppermute(value, axis, [(i, i ^ bit) for i in range(length)])]
    unnamed x45 -> x44, local copies, waits for them, and re-layouts: 10.9 us -> 5.57 us
    ppermute x9 -> x12, waiting for transfers between devices: 39.8 us -> 35.7 us  [swapped(): return lax.ppermute(value, axis, [(i, i ^ bit) for i in range(length)])]
  transfers between devices with their start and end apart: 17 -> 20, of which waited for: 17 -> 17; matrix products, arithmetic and copies ran while one was open for 4% -> 3% of each run, Pallas kernels for 0% -> 0%
where the time goes in v7:
time: 236 us; the launch traced here: 235 us
  waiting for transfers between devices  127 us (54%)
  starting transfers between devices  75 us (32%)
  matrix products  13.4 us (6%)
  other arithmetic  10.6 us (4%)
  local copies, waits for them, and re-layouts  8.23 us (3%)
    ppermute x8, waiting for transfers between devices, shifted(): return lax.ppermute(value, axis, pairs)  90.9 us
    ppermute x8, starting transfers between devices, shifted(): return lax.ppermute(value, axis, pairs)  41.7 us
    ppermute x12, waiting for transfers between devices, swapped(): return lax.ppermute(value, axis, [(i, i ^ bit) for i in range(length)])  35.7 us
    ppermute x12, starting transfers between devices, swapped(): return lax.ppermute(value, axis, [(i, i ^ bit) for i in range(length)])  33.3 us
    unnamed x44, local copies, waits for them, and re-layouts  5.57 us
    dot_general x1, matrix products, shards(): jnp.dot(target_cols, match_proj, preferred_element_type=jnp.float32)  4.91 us
  transfers between devices with their start and end apart: 20, of which 17 were waited for; matrix products, arithmetic and copies ran while one was open for 3% of the time, Pallas kernels for 0%

profile of v7, /device:TPU:46, one launch (start us, length us, event | category | flops | bytes accessed | tf_op | source)
XLA Modules:
  0.0 235.2 jit_solution(2560375865014460852)
XLA Ops:
  4.9 4.3 %collective-permute-start = (bf16[520,256]{1,0:T(8,128)(2,1)S(1)}, bf16[520,256]{1,0:T(8,128)(2,1)S(1)}, u32[]{:S(2)}, u32[]{:S(2)}) collective-permute-start(bf16[520,256]{1,0:T(8,128)(2,1)S(1)} %constant_dynamic-update-slice_fusion), channel_id=1, source_target_pairs={{0,16},{8,24},{16,32},{24,40},{32,48},{40,56},{48,64},{56,72},{64,... | collective-permute-start | bytes 798728 | tf_op jit(solution)/shard_map/ppermute | solution.py:18
  9.1 26.7 %collective-permute-done = bf16[520,256]{1,0:T(8,128)(2,1)S(1)} collective-permute-done((bf16[520,256]{1,0:T(8,128)(2,1)S(1)}, bf16[520,256]{1,0:T(8,128)(2,1)S(1)}, u32[]{:S(2)}, u32[]{:S(2)}) %collective-permute-start) | collective-permute-done | bytes 266272 | tf_op jit(solution)/shard_map/ppermute | solution.py:18
  39.8 18.0 %collective-permute-done.1 = bf16[520,256]{1,0:T(8,128)(2,1)S(1)} collective-permute-done((bf16[520,256]{1,0:T(8,128)(2,1)S(1)}, bf16[520,256]{1,0:T(8,128)(2,1)S(1)}, u32[]{:S(2)}, u32[]{:S(2)}) %collective-permute-start.1) | collective-permute-done | bytes 266272 | tf_op jit(solution)/shard_map/ppermute | solution.py:18
  61.7 17.3 %collective-permute-done.3 = bf16[520,256]{1,0:T(8,128)(2,1)S(1)} collective-permute-done((bf16[520,256]{1,0:T(8,128)(2,1)S(1)}, bf16[520,256]{1,0:T(8,128)(2,1)S(1)}, u32[]{:S(2)}, u32[]{:S(2)}) %collective-permute-start.3) | collective-permute-done | bytes 266272 | tf_op jit(solution)/shard_map/ppermute | solution.py:18
  82.9 16.8 %collective-permute-done.5 = bf16[520,256]{1,0:T(8,128)(2,1)S(1)} collective-permute-done((bf16[520,256]{1,0:T(8,128)(2,1)S(1)}, bf16[520,256]{1,0:T(8,128)(2,1)S(1)}, u32[]{:S(2)}, u32[]{:S(2)}) %collective-permute-start.5) | collective-permute-done | bytes 266272 | tf_op jit(solution)/shard_map/ppermute | solution.py:18
  107.6 2.7 %collective-permute-start.8 = (bf16[128,256]{0,1:T(8,128)(2,1)S(1)}, bf16[128,256]{0,1:T(8,128)(2,1)}, u32[]{:S(2)}, u32[]{:S(2)}) collective-permute-start(bf16[128,256]{0,1:T(8,128)(2,1)S(1)} %pad_maximum_fusion.1), channel_id=1, source_target_pairs={{0,1},{1,0},{2,3},{3,2},{4,5},{5,4},{6,7},{7,6},{8,9},{9,8},{10,11... | collective-permute-start | bytes 196616 | tf_op jit(solution)/shard_map/ppermute | solution.py:23
  110.3 3.5 %collective-permute-done.8 = bf16[128,256]{0,1:T(8,128)(2,1)} collective-permute-done((bf16[128,256]{0,1:T(8,128)(2,1)S(1)}, bf16[128,256]{0,1:T(8,128)(2,1)}, u32[]{:S(2)}, u32[]{:S(2)}) %collective-permute-start.8) | collective-permute-done | bytes 65568 | tf_op jit(solution)/shard_map/ppermute | solution.py:23
  114.8 3.3 %collective-permute-start.9 = (bf16[128,512]{0,1:T(8,128)(2,1)S(1)}, bf16[128,512]{0,1:T(8,128)(2,1)}, u32[]{:S(2)}, u32[]{:S(2)}) collective-permute-start(bf16[128,512]{0,1:T(8,128)(2,1)S(1)} %maximum_select_fusion.6), channel_id=1, source_target_pairs={{0,2},{1,3},{2,0},{3,1},{4,6},{5,7},{6,4},{7,5},{8,10},{9,11},{10,... | collective-permute-start | bytes 393224 | tf_op jit(solution)/shard_map/ppermute | solution.py:23
  118.3 5.0 %collective-permute-done.9 = bf16[128,512]{0,1:T(8,128)(2,1)} collective-permute-done((bf16[128,512]{0,1:T(8,128)(2,1)S(1)}, bf16[128,512]{0,1:T(8,128)(2,1)}, u32[]{:S(2)}, u32[]{:S(2)}) %collective-permute-start.9) | collective-permute-done | bytes 131104 | tf_op jit(solution)/shard_map/ppermute | solution.py:23
  124.5 4.5 %collective-permute-start.10 = (bf16[128,1024]{0,1:T(8,128)(2,1)S(1)}, bf16[128,1024]{0,1:T(8,128)(2,1)}, u32[]{:S(2)}, u32[]{:S(2)}) collective-permute-start(bf16[128,1024]{0,1:T(8,128)(2,1)S(1)} %maximum_select_fusion.5), channel_id=1, source_target_pairs={{0,4},{1,5},{2,6},{3,7},{4,0},{5,1},{6,2},{7,3},{8,12},{9,13},{10,... | collective-permute-start | bytes 786440 | tf_op jit(solution)/shard_map/ppermute | solution.py:23
  129.0 3.7 %fusion.4 = f32[128,2304]{1,0:T(8,128)} fusion(bf16[256,2304]{1,0:T(8,128)(2,1)} %param.22, bf16[1152,256]{1,0:T(8,128)(2,1)} %bitcast.82, f32[128,1152]{0,1:T(8,128)} %copy-done.3, f32[128]{0:T(128)S(1)} %get-tuple-element.16, f32[128]{0:T(128)S(1)} %get-tuple-element.19, s32[128]{0:T(128)S(1)} %get-tuple-element.34, s32[128]{0:T(128)S(1)} %get-tuple-element.28, ...), kind=kOutput, calls=%fused_computation.15 | convolution fusion | flops 227852288 | bytes 3545600 | tf_op jit(solution)/shard_map/dot_general | solution.py:181
  133.4 4.9 %fusion = f32[128,2304]{1,0:T(8,128)} fusion(f32[128,2304]{1,0:T(8,128)} %fusion.4, bf16[576,2304]{1,0:T(8,128)(2,1)S(1)} %copy-done, bf16[576,2048]{1,0:T(8,128)(2,1)} %param.21, f32[128]{0:T(128)S(1)} %select_reduce_fusion.3, bf16[128,1024]{0,1:T(8,128)(2,1)S(1)} %maximum_select_fusion.5, bf16[128,1024]{0,1:T(8,128)(2,1)} %collective-permute-done.10, ...), kind=kOutput, calls=%fused_computation.1 | convolution fusion | flops 644751360 | bytes 7897601 | tf_op jit(solution)/shard_map/dot_general | solution.py:182
  139.6 3.9 %collective-permute-start.11 = (bf16[64,2304]{1,0:T(8,128)(2,1)S(1)}, bf16[64,2304]{1,0:T(8,128)(2,1)S(1)}, u32[]{:S(2)}, u32[]{:S(2)}) collective-permute-start(bf16[64,2304]{1,0:T(8,128)(2,1)S(1)} %select_convert_fusion), channel_id=1, source_target_pairs={{0,4},{1,5},{2,6},{3,7},{4,0},{5,1},{6,2},{7,3},{8,12},{9,13},{10,... | collective-permute-start | bytes 884744 | tf_op jit(solution)/shard_map/ppermute | solution.py:23
  143.6 4.7 %collective-permute-done.11 = bf16[64,2304]{1,0:T(8,128)(2,1)S(1)} collective-permute-done((bf16[64,2304]{1,0:T(8,128)(2,1)S(1)}, bf16[64,2304]{1,0:T(8,128)(2,1)S(1)}, u32[]{:S(2)}, u32[]{:S(2)}) %collective-permute-start.11) | collective-permute-done | bytes 294944 | tf_op jit(solution)/shard_map/ppermute | solution.py:23
  149.6 2.7 %collective-permute-start.12 = (bf16[64,2304]{1,0:T(8,128)(2,1)S(1)}, bf16[64,2304]{1,0:T(8,128)(2,1)S(1)}, u32[]{:S(2)}, u32[]{:S(2)}) collective-permute-start(bf16[64,2304]{1,0:T(8,128)(2,1)S(1)} %get-tuple-element.20), channel_id=1, source_target_pairs={{0,1},{1,0},{2,3},{3,2},{4,5},{5,4},{6,7},{7,6},{8,9},{9,8},{10,11... | collective-permute-start | bytes 884744 | tf_op jit(solution)/shard_map/ppermute | solution.py:23
  152.3 7.2 %collective-permute-done.12 = bf16[64,2304]{1,0:T(8,128)(2,1)S(1)} collective-permute-done((bf16[64,2304]{1,0:T(8,128)(2,1)S(1)}, bf16[64,2304]{1,0:T(8,128)(2,1)S(1)}, u32[]{:S(2)}, u32[]{:S(2)}) %collective-permute-start.12) | collective-permute-done | bytes 294944 | tf_op jit(solution)/shard_map/ppermute | solution.py:23
  161.7 8.1 %collective-permute-done.13 = bf16[64,2304]{1,0:T(8,128)(2,1)S(1)} collective-permute-done((bf16[64,2304]{1,0:T(8,128)(2,1)S(1)}, bf16[64,2304]{1,0:T(8,128)(2,1)S(1)}, u32[]{:S(2)}, u32[]{:S(2)}) %collective-permute-start.13) | collective-permute-done | bytes 294944 | tf_op jit(solution)/shard_map/ppermute | solution.py:23
  169.9 4.3 %collective-permute-start.14 = (bf16[64,2304]{1,0:T(8,128)(2,1)S(1)}, bf16[64,2304]{1,0:T(8,128)(2,1)S(1)}, u32[]{:S(2)}, u32[]{:S(2)}) collective-permute-start(bf16[64,2304]{1,0:T(8,128)(2,1)S(1)} %add_convert_fusion), channel_id=1, source_target_pairs={{0,4},{1,5},{2,6},{3,7},{4,0},{5,1},{6,2},{7,3},{8,12},{9,13},{10,... | collective-permute-start | bytes 884744 | tf_op jit(solution)/shard_map/ppermute | solution.py:23
  174.2 4.7 %collective-permute-done.14 = bf16[64,2304]{1,0:T(8,128)(2,1)S(1)} collective-permute-done((bf16[64,2304]{1,0:T(8,128)(2,1)S(1)}, bf16[64,2304]{1,0:T(8,128)(2,1)S(1)}, u32[]{:S(2)}, u32[]{:S(2)}) %collective-permute-start.14) | collective-permute-done | bytes 294944 | tf_op jit(solution)/shard_map/ppermute | solution.py:23
  191.6 5.5 %collective-permute-done.16 = bf16[256,256]{1,0:T(8,128)(2,1)S(1)} collective-permute-done((bf16[256,256]{1,0:T(8,128)(2,1)S(1)}, bf16[256,256]{1,0:T(8,128)(2,1)S(1)}, u32[]{:S(2)}, u32[]{:S(2)}) %collective-permute-start.16) | collective-permute-done | bytes 131104 | tf_op jit(solution)/shard_map/ppermute | solution.py:18
  197.1 9.6 %collective-permute-start.17 = (bf16[256,256]{1,0:T(8,128)(2,1)S(1)}, bf16[256,256]{1,0:T(8,128)(2,1)S(1)}, u32[]{:S(2)}, u32[]{:S(2)}) collective-permute-start(bf16[256,256]{1,0:T(8,128)(2,1)S(1)} %fusion.35), channel_id=1, source_target_pairs={{16,0},{24,8},{32,16},{40,24},{48,32},{56,40},{64,48},{72,56},{80,... | collective-permute-start | bytes 393224 | tf_op jit(solution)/shard_map/ppermute | solution.py:18
  209.2 10.7 %collective-permute-start.18 = (bf16[256,256]{1,0:T(8,128)(2,1)S(1)}, bf16[256,256]{1,0:T(8,128)(2,1)S(1)}, u32[]{:S(2)}, u32[]{:S(2)}) collective-permute-start(bf16[256,256]{1,0:T(8,128)(2,1)S(1)} %fusion.37), channel_id=1, source_target_pairs={{16,0},{24,8},{32,16},{40,24},{48,32},{56,40},{64,48},{72,56},{80,... | collective-permute-start | bytes 393224 | tf_op jit(solution)/shard_map/ppermute | solution.py:18
  219.9 2.5 %collective-permute-done.18 = bf16[256,256]{1,0:T(8,128)(2,1)S(1)} collective-permute-done((bf16[256,256]{1,0:T(8,128)(2,1)S(1)}, bf16[256,256]{1,0:T(8,128)(2,1)S(1)}, u32[]{:S(2)}, u32[]{:S(2)}) %collective-permute-start.18) | collective-permute-done | bytes 131104 | tf_op jit(solution)/shard_map/ppermute | solution.py:18
  222.4 9.5 %collective-permute-start.19 = (bf16[256,256]{1,0:T(8,128)(2,1)S(1)}, bf16[256,256]{1,0:T(8,128)(2,1)S(1)}, u32[]{:S(2)}, u32[]{:S(2)}) collective-permute-start(bf16[256,256]{1,0:T(8,128)(2,1)S(1)} %fusion.39), channel_id=1, source_target_pairs={{16,0},{24,8},{32,16},{40,24},{48,32},{56,40},{64,48},{72,56},{80,... | collective-permute-start | bytes 393224 | tf_op jit(solution)/shard_map/ppermute | solution.py:18
  (105 shorter events, 49.8 us)
Async XLA Ops:
  0.6 132.8 %copy-start = (bf16[576,2304]{1,0:T(8,128)(2,1)S(1)}, bf16[576,2304]{1,0:T(8,128)(2,1)}, u32[]{:S(2)}) copy-start(bf16[576,2304]{1,0:T(8,128)(2,1)} %param.23) | copy-start | bytes 7962628
  4.9 31.0 %collective-permute-start = (bf16[520,256]{1,0:T(8,128)(2,1)S(1)}, bf16[520,256]{1,0:T(8,128)(2,1)S(1)}, u32[]{:S(2)}, u32[]{:S(2)}) collective-permute-start(bf16[520,256]{1,0:T(8,128)(2,1)S(1)} %constant_dynamic-update-slice_fusion), channel_id=1, source_target_pairs={{0,16},{8,24},{16,32},{24,40},{32,48},{40,56},{48,64},{56,72},{64,... | collective-permute-start | bytes 798728 | tf_op jit(solution)/shard_map/ppermute | solution.py:18
  35.9 3.9 %collective-permute-start.2 = (bf16[520,256]{1,0:T(8,128)(2,1)S(1)}, bf16[520,256]{1,0:T(8,128)(2,1)S(1)}, u32[]{:S(2)}, u32[]{:S(2)}) collective-permute-start(bf16[520,256]{1,0:T(8,128)(2,1)S(1)} %broadcast_select_fusion.3), channel_id=1, source_target_pairs={{0,8},{8,0},{16,24},{24,16},{32,40},{40,32},{48,56},{56,48},{64,72... | collective-permute-start | bytes 798728 | tf_op jit(solution)/shard_map/ppermute | solution.py:23
  37.9 19.9 %collective-permute-start.1 = (bf16[520,256]{1,0:T(8,128)(2,1)S(1)}, bf16[520,256]{1,0:T(8,128)(2,1)S(1)}, u32[]{:S(2)}, u32[]{:S(2)}) collective-permute-start(bf16[520,256]{1,0:T(8,128)(2,1)S(1)} %collective-permute-done), channel_id=1, source_target_pairs={{0,16},{8,24},{16,32},{24,40},{32,48},{40,56},{48,64},{56,72},{64,... | collective-permute-start | bytes 798728 | tf_op jit(solution)/shard_map/ppermute | solution.py:18
  57.8 3.9 %collective-permute-start.4 = (bf16[520,256]{1,0:T(8,128)(2,1)S(1)}, bf16[520,256]{1,0:T(8,128)(2,1)S(1)}, u32[]{:S(2)}, u32[]{:S(2)}) collective-permute-start(bf16[520,256]{1,0:T(8,128)(2,1)S(1)} %broadcast_select_fusion.2), channel_id=1, source_target_pairs={{0,8},{8,0},{16,24},{24,16},{32,40},{40,32},{48,56},{56,48},{64,72... | collective-permute-start | bytes 798728 | tf_op jit(solution)/shard_map/ppermute | solution.py:23
  59.7 19.2 %collective-permute-start.3 = (bf16[520,256]{1,0:T(8,128)(2,1)S(1)}, bf16[520,256]{1,0:T(8,128)(2,1)S(1)}, u32[]{:S(2)}, u32[]{:S(2)}) collective-permute-start(bf16[520,256]{1,0:T(8,128)(2,1)S(1)} %collective-permute-done.1), channel_id=1, source_target_pairs={{0,16},{8,24},{16,32},{24,40},{32,48},{40,56},{48,64},{56,72},{64,... | collective-permute-start | bytes 798728 | tf_op jit(solution)/shard_map/ppermute | solution.py:18
  79.0 3.9 %collective-permute-start.6 = (bf16[520,256]{1,0:T(8,128)(2,1)S(1)}, bf16[520,256]{1,0:T(8,128)(2,1)S(1)}, u32[]{:S(2)}, u32[]{:S(2)}) collective-permute-start(bf16[520,256]{1,0:T(8,128)(2,1)S(1)} %broadcast_select_fusion.1), channel_id=1, source_target_pairs={{0,8},{8,0},{16,24},{24,16},{32,40},{40,32},{48,56},{56,48},{64,72... | collective-permute-start | bytes 798728 | tf_op jit(solution)/shard_map/ppermute | solution.py:23
  80.9 18.8 %collective-permute-start.5 = (bf16[520,256]{1,0:T(8,128)(2,1)S(1)}, bf16[520,256]{1,0:T(8,128)(2,1)S(1)}, u32[]{:S(2)}, u32[]{:S(2)}) collective-permute-start(bf16[520,256]{1,0:T(8,128)(2,1)S(1)} %collective-permute-done.3), channel_id=1, source_target_pairs={{0,16},{8,24},{16,32},{24,40},{32,48},{40,56},{48,64},{56,72},{64,... | collective-permute-start | bytes 798728 | tf_op jit(solution)/shard_map/ppermute | solution.py:18
  99.7 3.4 %collective-permute-start.7 = (bf16[520,256]{1,0:T(8,128)(2,1)S(1)}, bf16[520,256]{1,0:T(8,128)(2,1)S(1)}, u32[]{:S(2)}, u32[]{:S(2)}) collective-permute-start(bf16[520,256]{1,0:T(8,128)(2,1)S(1)} %broadcast_select_fusion), channel_id=1, source_target_pairs={{0,8},{8,0},{16,24},{24,16},{32,40},{40,32},{48,56},{56,48},{64,72... | collective-permute-start | bytes 798728 | tf_op jit(solution)/shard_map/ppermute | solution.py:23
  105.7 74.2 %copy-start.9 = (f32[128]{0:T(128)}, f32[128]{0:T(128)S(1)}, u32[]{:S(2)}) copy-start(f32[128]{0:T(128)S(1)} %get-tuple-element.19) | copy-start | bytes 1540
  106.2 73.7 %copy-start.10 = (f32[128]{0:T(128)}, f32[128]{0:T(128)S(1)}, u32[]{:S(2)}) copy-start(f32[128]{0:T(128)S(1)} %get-tuple-element.16) | copy-start | bytes 1540
  107.6 6.3 %collective-permute-start.8 = (bf16[128,256]{0,1:T(8,128)(2,1)S(1)}, bf16[128,256]{0,1:T(8,128)(2,1)}, u32[]{:S(2)}, u32[]{:S(2)}) collective-permute-start(bf16[128,256]{0,1:T(8,128)(2,1)S(1)} %pad_maximum_fusion.1), channel_id=1, source_target_pairs={{0,1},{1,0},{2,3},{3,2},{4,5},{5,4},{6,7},{7,6},{8,9},{9,8},{10,11... | collective-permute-start | bytes 196616 | tf_op jit(solution)/shard_map/ppermute | solution.py:23
  114.8 8.5 %collective-permute-start.9 = (bf16[128,512]{0,1:T(8,128)(2,1)S(1)}, bf16[128,512]{0,1:T(8,128)(2,1)}, u32[]{:S(2)}, u32[]{:S(2)}) collective-permute-start(bf16[128,512]{0,1:T(8,128)(2,1)S(1)} %maximum_select_fusion.6), channel_id=1, source_target_pairs={{0,2},{1,3},{2,0},{3,1},{4,6},{5,7},{6,4},{7,5},{8,10},{9,11},{10,... | collective-permute-start | bytes 393224 | tf_op jit(solution)/shard_map/ppermute | solution.py:23
  124.5 9.0 %collective-permute-start.10 = (bf16[128,1024]{0,1:T(8,128)(2,1)S(1)}, bf16[128,1024]{0,1:T(8,128)(2,1)}, u32[]{:S(2)}, u32[]{:S(2)}) collective-permute-start(bf16[128,1024]{0,1:T(8,128)(2,1)S(1)} %maximum_select_fusion.5), channel_id=1, source_target_pairs={{0,4},{1,5},{2,6},{3,7},{4,0},{5,1},{6,2},{7,3},{8,12},{9,13},{10,... | collective-permute-start | bytes 786440 | tf_op jit(solution)/shard_map/ppermute | solution.py:23
  139.6 8.6 %collective-permute-start.11 = (bf16[64,2304]{1,0:T(8,128)(2,1)S(1)}, bf16[64,2304]{1,0:T(8,128)(2,1)S(1)}, u32[]{:S(2)}, u32[]{:S(2)}) collective-permute-start(bf16[64,2304]{1,0:T(8,128)(2,1)S(1)} %select_convert_fusion), channel_id=1, source_target_pairs={{0,4},{1,5},{2,6},{3,7},{4,0},{5,1},{6,2},{7,3},{8,12},{9,13},{10,... | collective-permute-start | bytes 884744 | tf_op jit(solution)/shard_map/ppermute | solution.py:23
  149.6 9.9 %collective-permute-start.12 = (bf16[64,2304]{1,0:T(8,128)(2,1)S(1)}, bf16[64,2304]{1,0:T(8,128)(2,1)S(1)}, u32[]{:S(2)}, u32[]{:S(2)}) collective-permute-start(bf16[64,2304]{1,0:T(8,128)(2,1)S(1)} %get-tuple-element.20), channel_id=1, source_target_pairs={{0,1},{1,0},{2,3},{3,2},{4,5},{5,4},{6,7},{7,6},{8,9},{9,8},{10,11... | collective-permute-start | bytes 884744 | tf_op jit(solution)/shard_map/ppermute | solution.py:23
  159.5 19.4 %copy-start.11 = (bf16[256,2304]{1,0:T(8,128)(2,1)S(1)}, bf16[256,2304]{1,0:T(8,128)(2,1)}, u32[]{:S(2)}) copy-start(bf16[256,2304]{1,0:T(8,128)(2,1)} %param.22) | copy-start | bytes 3538948
  159.5 10.3 %collective-permute-start.13 = (bf16[64,2304]{1,0:T(8,128)(2,1)S(1)}, bf16[64,2304]{1,0:T(8,128)(2,1)S(1)}, u32[]{:S(2)}, u32[]{:S(2)}) collective-permute-start(bf16[64,2304]{1,0:T(8,128)(2,1)S(1)} %fusion.29), channel_id=1, source_target_pairs={{0,2},{1,3},{2,0},{3,1},{4,6},{5,7},{6,4},{7,5},{8,10},{9,11},{10,... | collective-permute-start | bytes 884744 | tf_op jit(solution)/shard_map/ppermute | solution.py:23
  169.9 9.0 %collective-permute-start.14 = (bf16[64,2304]{1,0:T(8,128)(2,1)S(1)}, bf16[64,2304]{1,0:T(8,128)(2,1)S(1)}, u32[]{:S(2)}, u32[]{:S(2)}) collective-permute-start(bf16[64,2304]{1,0:T(8,128)(2,1)S(1)} %add_convert_fusion), channel_id=1, source_target_pairs={{0,4},{1,5},{2,6},{3,7},{4,0},{5,1},{6,2},{7,3},{8,12},{9,13},{10,... | collective-permute-start | bytes 884744 | tf_op jit(solution)/shard_map/ppermute | solution.py:23
  184.2 4.1 %collective-permute-start.15 = (bf16[4,256,256]{2,1,0:T(8,128)(2,1)}, bf16[4,256,256]{2,1,0:T(8,128)(2,1)}, u32[]{:S(2)}, u32[]{:S(2)}) collective-permute-start(bf16[4,256,256]{2,1,0:T(8,128)(2,1)} %slice.88), channel_id=1, source_target_pairs={{0,8},{8,0},{16,24},{24,16},{32,40},{40,32},{48,56},{56,48},{64,72... | collective-permute-start | bytes 1572872 | tf_op jit(solution)/shard_map/ppermute | solution.py:23
  189.6 7.5 %collective-permute-start.16 = (bf16[256,256]{1,0:T(8,128)(2,1)S(1)}, bf16[256,256]{1,0:T(8,128)(2,1)S(1)}, u32[]{:S(2)}, u32[]{:S(2)}) collective-permute-start(bf16[256,256]{1,0:T(8,128)(2,1)S(1)} %fusion.45), channel_id=1, source_target_pairs={{16,0},{24,8},{32,16},{40,24},{48,32},{56,40},{64,48},{72,56},{80,... | collective-permute-start | bytes 393224 | tf_op jit(solution)/shard_map/ppermute | solution.py:18
  197.1 12.1 %collective-permute-start.17 = (bf16[256,256]{1,0:T(8,128)(2,1)S(1)}, bf16[256,256]{1,0:T(8,128)(2,1)S(1)}, u32[]{:S(2)}, u32[]{:S(2)}) collective-permute-start(bf16[256,256]{1,0:T(8,128)(2,1)S(1)} %fusion.35), channel_id=1, source_target_pairs={{16,0},{24,8},{32,16},{40,24},{48,32},{56,40},{64,48},{72,56},{80,... | collective-permute-start | bytes 393224 | tf_op jit(solution)/shard_map/ppermute | solution.py:18
  209.2 13.2 %collective-permute-start.18 = (bf16[256,256]{1,0:T(8,128)(2,1)S(1)}, bf16[256,256]{1,0:T(8,128)(2,1)S(1)}, u32[]{:S(2)}, u32[]{:S(2)}) collective-permute-start(bf16[256,256]{1,0:T(8,128)(2,1)S(1)} %fusion.37), channel_id=1, source_target_pairs={{16,0},{24,8},{32,16},{40,24},{48,32},{56,40},{64,48},{72,56},{80,... | collective-permute-start | bytes 393224 | tf_op jit(solution)/shard_map/ppermute | solution.py:18
  222.4 12.0 %collective-permute-start.19 = (bf16[256,256]{1,0:T(8,128)(2,1)S(1)}, bf16[256,256]{1,0:T(8,128)(2,1)S(1)}, u32[]{:S(2)}, u32[]{:S(2)}) collective-permute-start(bf16[256,256]{1,0:T(8,128)(2,1)S(1)} %fusion.39), channel_id=1, source_target_pairs={{16,0},{24,8},{32,16},{40,24},{48,32},{56,40},{64,48},{72,56},{80,... | collective-permute-start | bytes 393224 | tf_op jit(solution)/shard_map/ppermute | solution.py:18
  (11 other events, 43.7 us)

commit v8 on v6

--- a/solution.py
+++ b/solution.py
@@ -105,6 +105,31 @@
         for head, part in enumerate(rounded)
     ]
     return jnp.concatenate(mixed, 1).astype(jnp.bfloat16), rounded
+
+
+def project_while_gathering(value, weight, axis):
+    size = lax.axis_size(axis)
+    me = lax.axis_index(axis)
+    block = value.shape[1]
+
+    def product(part, first, count):
+        cols = lax.dynamic_slice_in_dim(weight, first * block, count * block, 1)
+        return trans_dot(part, cols)
+
+    total = product(value, me, 1)
+    held = value
+    bit = 1
+    while bit < size:
+        incoming = swapped(held, axis, bit)
+        total = total + product(incoming, ((me ^ bit) // bit) * bit, bit)
+        upper = (me // bit) % 2 == 1
+        held = jnp.where(
+            upper,
+            jnp.concatenate([incoming, held], 1),
+            jnp.concatenate([held, incoming], 1),
+        )
+        bit *= 2
+    return total
 
 
 def shards(
@@ -156,12 +181,9 @@
         teacher_query, keys_teacher, doc_marks, marks_all, DH_T, teacher_scale, rows
     )
     teacher_mix, _ = mix_values(probability, values_teacher, DH_T)
-    target_cols = lax.dot_general(
-        gather_doubling(teacher_mix, "head", 1),
-        teacher_out_proj,
-        (((1,), (1,)), ((), ())),
-        preferred_element_type=jnp.float32,
-    ).astype(jnp.bfloat16)
+    target_cols = project_while_gathering(teacher_mix, teacher_out_proj, "head").astype(
+        jnp.bfloat16
+    )
 
     probability = window_probs(
         student_query, keys_student, doc_marks, marks_all, DH_S, student_scale, rows
@@ -205,7 +227,7 @@
     grads = jnp.concatenate(
         [grad_k.reshape(blocks, rows, width), grad_v.reshape(blocks, rows, width)], 1
     )
-    from_partner = swapped(grads[1::2], "seq", 1)
+    from_partner = swapped(grads[1::2].astype(jnp.bfloat16), "seq", 1).astype(jnp.float32)
     nothing = jnp.zeros_like(from_partner[:1])
     added = jnp.where(
         core == 1,

time: 225 us -> 234 us (1.040)
  the two profiles are of different devices: /device:TPU:46 before, /device:TPU:40 now
where the time goes in v8:
time: 234 us; the launch traced here: 233 us
  waiting for transfers between devices  108 us (46%)
  starting transfers between devices  68.9 us (29%)
  local copies, waits for them, and re-layouts  28.6 us (12%)
  matrix products  18.5 us (8%)
  other arithmetic  8.3 us (4%)
    ppermute x8, waiting for transfers between devices, shifted(): return lax.ppermute(value, axis, pairs)  75.9 us
    ppermute x8, starting transfers between devices, shifted(): return lax.ppermute(value, axis, pairs)  40 us
    ppermute x9, waiting for transfers between devices, swapped(): return lax.ppermute(value, axis, [(i, i ^ bit) for i in range(length)])  31.7 us
    ppermute x9, starting transfers between devices, swapped(): return lax.ppermute(value, axis, [(i, i ^ bit) for i in range(length)])  28.8 us
    unnamed x53, local copies, waits for them, and re-layouts  19.7 us
    dot_general x7, matrix products, trans_dot(): lax.dot_general(left, right, (((1,), (1,)), ((), ())), preferred_element_...  7.91 us
  transfers between devices with their start and end apart: 17, of which 16 were waited for; matrix products, arithmetic and copies ran while one was open for 6% of the time, Pallas kernels for 0%

profile of v8, /device:TPU:40, one launch (start us, length us, event | category | flops | bytes accessed | tf_op | source)
XLA Modules:
  0.0 233.1 jit_solution(7074528867923893602)
XLA Ops:
  4.9 4.3 %collective-permute-start = (bf16[520,256]{1,0:T(8,128)(2,1)S(1)}, bf16[520,256]{1,0:T(8,128)(2,1)S(1)}, u32[]{:S(2)}, u32[]{:S(2)}) collective-permute-start(bf16[520,256]{1,0:T(8,128)(2,1)S(1)} %constant_dynamic-update-slice_fusion), channel_id=1, source_target_pairs={{0,16},{8,24},{16,32},{24,40},{32,48},{40,56},{48,64},{56,72},{64,... | collective-permute-start | bytes 798728 | tf_op jit(solution)/shard_map/ppermute | solution.py:18
  9.1 26.8 %collective-permute-done = bf16[520,256]{1,0:T(8,128)(2,1)S(1)} collective-permute-done((bf16[520,256]{1,0:T(8,128)(2,1)S(1)}, bf16[520,256]{1,0:T(8,128)(2,1)S(1)}, u32[]{:S(2)}, u32[]{:S(2)}) %collective-permute-start) | collective-permute-done | bytes 266272 | tf_op jit(solution)/shard_map/ppermute | solution.py:18
  37.8 15.9 %collective-permute-done.1 = bf16[520,256]{1,0:T(8,128)(2,1)S(1)} collective-permute-done((bf16[520,256]{1,0:T(8,128)(2,1)S(1)}, bf16[520,256]{1,0:T(8,128)(2,1)S(1)}, u32[]{:S(2)}, u32[]{:S(2)}) %collective-permute-start.1) | collective-permute-done | bytes 266272 | tf_op jit(solution)/shard_map/ppermute | solution.py:18
  57.1 11.5 %collective-permute-done.2 = bf16[520,256]{1,0:T(8,128)(2,1)} collective-permute-done((bf16[520,256]{1,0:T(8,128)(2,1)S(1)}, bf16[520,256]{1,0:T(8,128)(2,1)}, u32[]{:S(2)}, u32[]{:S(2)}) %collective-permute-start.2) | collective-permute-done | bytes 266272 | tf_op jit(solution)/shard_map/ppermute | solution.py:18
  73.0 9.6 %collective-permute-done.3 = bf16[520,256]{1,0:T(8,128)(2,1)S(1)} collective-permute-done((bf16[520,256]{1,0:T(8,128)(2,1)}, bf16[520,256]{1,0:T(8,128)(2,1)S(1)}, u32[]{:S(2)}, u32[]{:S(2)}) %collective-permute-start.3) | collective-permute-done | bytes 266272 | tf_op jit(solution)/shard_map/ppermute | solution.py:18
  87.7 2.9 %collective-permute-done.4 = bf16[4,520,256]{2,1,0:T(8,128)(2,1)} collective-permute-done((bf16[4,520,256]{2,1,0:T(8,128)(2,1)}, bf16[4,520,256]{2,1,0:T(8,128)(2,1)}, u32[]{:S(2)}, u32[]{:S(2)}) %collective-permute-start.4) | collective-permute-done | bytes 1064992 | tf_op jit(solution)/shard_map/ppermute | solution.py:23
  101.1 2.6 %fusion.65 = (bf16[9,128,256]{2,1,0:T(8,128)(2,1)S(1)}, bf16[9,128,256]{2,1,0:T(8,128)(2,1)S(1)}, bf16[9,128,256]{2,1,0:T(8,128)(2,1)}, bf16[9,128,256]{2,1,0:T(8,128)(2,1)S(1)}) fusion(bf16[9,520,256]{2,1,0:T(8,128)(2,1)} %bitcast_dynamic-update-slice_fusion.6), kind=kLoop, calls=%fused_computation.118 | loop fusion | bytes 4718592 | tf_op jit(solution)/shard_map/slice | solution.py:173
  107.7 3.4 %collective-permute-start.5 = (bf16[128,256]{0,1:T(8,128)(2,1)S(1)}, bf16[128,256]{0,1:T(8,128)(2,1)S(1)}, u32[]{:S(2)}, u32[]{:S(2)}) collective-permute-start(bf16[128,256]{0,1:T(8,128)(2,1)S(1)} %pad_maximum_fusion.1), channel_id=1, source_target_pairs={{0,1},{1,0},{2,3},{3,2},{4,5},{5,4},{6,7},{7,6},{8,9},{9,8},{10,11... | collective-permute-start | bytes 196616 | tf_op jit(solution)/shard_map/ppermute | solution.py:23
  114.5 4.9 %collective-permute-start.6 = (bf16[128,512]{0,1:T(8,128)(2,1)S(1)}, bf16[128,512]{0,1:T(8,128)(2,1)S(1)}, u32[]{:S(2)}, u32[]{:S(2)}) collective-permute-start(bf16[128,512]{0,1:T(8,128)(2,1)S(1)} %maximum_select_fusion.3), channel_id=1, source_target_pairs={{0,2},{1,3},{2,0},{3,1},{4,6},{5,7},{6,4},{7,5},{8,10},{9,11},{10,... | collective-permute-start | bytes 393224 | tf_op jit(solution)/shard_map/ppermute | solution.py:23
  119.5 3.7 %fusion.8 = f32[128,2304]{1,0:T(8,128)} fusion(bf16[256,2304]{1,0:T(8,128)(2,1)} %param.22, bf16[1152,256]{1,0:T(8,128)(2,1)} %bitcast.81, f32[128,1152]{0,1:T(8,128)} %copy-done.3, f32[128]{0:T(128)} %get-tuple-element.4, f32[128]{0:T(128)} %copy-done.10, s32[128]{0:T(128)S(1)} %get-tuple-element.24, s32[128]{0:T(128)S(1)} %get-tuple-element.18, ...), kind=kOutput, calls=%fused_computation.20 | convolution fusion | flops 227852288 | bytes 3545600 | tf_op jit(solution)/shard_map/dot_general | solution.py:197
  123.2 4.2 %collective-permute-start.7 = (bf16[128,1024]{0,1:T(8,128)(2,1)S(1)}, bf16[128,1024]{0,1:T(8,128)(2,1)S(1)}, u32[]{:S(2)}, u32[]{:S(2)}) collective-permute-start(bf16[128,1024]{0,1:T(8,128)(2,1)S(1)} %maximum_select_fusion.2), channel_id=1, source_target_pairs={{0,4},{1,5},{2,6},{3,7},{4,0},{5,1},{6,2},{7,3},{8,12},{9,13},{10,... | collective-permute-start | bytes 786440 | tf_op jit(solution)/shard_map/ppermute | solution.py:23
  132.6 2.6 %fusion.5 = f32[128,576]{1,0:T(8,128)} fusion(bf16[128,1024]{0,1:T(8,128)(2,1)S(1)} %collective-permute-done.7, bf16[576,2048]{1,0:T(8,128)(2,1)} %param.21, s32[]{:T(128)S(6)} %select_n.141), kind=kOutput, calls=%fused_computation.14 | convolution fusion | flops 150994944 | bytes 1736708 | tf_op jit(solution)/shard_map/dot_general | solution.py:83
  135.2 3.7 %fusion = f32[128,2304]{1,0:T(8,128)} fusion(f32[128,2304]{1,0:T(8,128)} %fusion.8, bf16[576,2304]{1,0:T(8,128)(2,1)S(1)} %copy-done, f32[128,576]{1,0:T(8,128)} %fusion.5, f32[128,576]{1,0:T(8,128)} %convolution_add_fusion.1, bf16[128,512]{0,1:T(8,128)(2,1)S(1)} %collective-permute-done.6, bf16[576,2048]{1,0:T(8,128)(2,1)} %param.21, s32[]{:T(128)S(6)} %select_n.135, ...), kind=kOutput, calls=%fused_computation.1 | convolution fusion | flops 416047104 | bytes 6390276 | tf_op jit(solution)/shard_map/dot_general | solution.py:198
  140.1 3.6 %collective-permute-start.8 = (bf16[64,2304]{1,0:T(8,128)(2,1)S(1)}, bf16[64,2304]{1,0:T(8,128)(2,1)S(1)}, u32[]{:S(2)}, u32[]{:S(2)}) collective-permute-start(bf16[64,2304]{1,0:T(8,128)(2,1)S(1)} %select_convert_fusion), channel_id=1, source_target_pairs={{0,4},{1,5},{2,6},{3,7},{4,0},{5,1},{6,2},{7,3},{8,12},{9,13},{10,... | collective-permute-start | bytes 884744 | tf_op jit(solution)/shard_map/ppermute | solution.py:23
  143.8 5.2 %collective-permute-done.8 = bf16[64,2304]{1,0:T(8,128)(2,1)S(1)} collective-permute-done((bf16[64,2304]{1,0:T(8,128)(2,1)S(1)}, bf16[64,2304]{1,0:T(8,128)(2,1)S(1)}, u32[]{:S(2)}, u32[]{:S(2)}) %collective-permute-start.8) | collective-permute-done | bytes 294944 | tf_op jit(solution)/shard_map/ppermute | solution.py:23
  152.7 6.8 %collective-permute-done.9 = bf16[64,2304]{1,0:T(8,128)(2,1)S(1)} collective-permute-done((bf16[64,2304]{1,0:T(8,128)(2,1)S(1)}, bf16[64,2304]{1,0:T(8,128)(2,1)S(1)}, u32[]{:S(2)}, u32[]{:S(2)}) %collective-permute-start.9) | collective-permute-done | bytes 294944 | tf_op jit(solution)/shard_map/ppermute | solution.py:23
  159.6 3.2 %collective-permute-start.10 = (bf16[64,2304]{1,0:T(8,128)(2,1)S(1)}, bf16[64,2304]{1,0:T(8,128)(2,1)S(1)}, u32[]{:S(2)}, u32[]{:S(2)}) collective-permute-start(bf16[64,2304]{1,0:T(8,128)(2,1)S(1)} %fusion.23), channel_id=1, source_target_pairs={{0,2},{1,3},{2,0},{3,1},{4,6},{5,7},{6,4},{7,5},{8,10},{9,11},{10,... | collective-permute-start | bytes 884744 | tf_op jit(solution)/shard_map/ppermute | solution.py:23
  162.8 7.0 %collective-permute-done.10 = bf16[64,2304]{1,0:T(8,128)(2,1)S(1)} collective-permute-done((bf16[64,2304]{1,0:T(8,128)(2,1)S(1)}, bf16[64,2304]{1,0:T(8,128)(2,1)S(1)}, u32[]{:S(2)}, u32[]{:S(2)}) %collective-permute-start.10) | collective-permute-done | bytes 294944 | tf_op jit(solution)/shard_map/ppermute | solution.py:23
  169.8 3.3 %collective-permute-start.11 = (bf16[64,2304]{1,0:T(8,128)(2,1)S(1)}, bf16[64,2304]{1,0:T(8,128)(2,1)S(1)}, u32[]{:S(2)}, u32[]{:S(2)}) collective-permute-start(bf16[64,2304]{1,0:T(8,128)(2,1)S(1)} %add_convert_fusion), channel_id=1, source_target_pairs={{0,4},{1,5},{2,6},{3,7},{4,0},{5,1},{6,2},{7,3},{8,12},{9,13},{10,... | collective-permute-start | bytes 884744 | tf_op jit(solution)/shard_map/ppermute | solution.py:23
  173.1 5.5 %collective-permute-done.11 = bf16[64,2304]{1,0:T(8,128)(2,1)S(1)} collective-permute-done((bf16[64,2304]{1,0:T(8,128)(2,1)S(1)}, bf16[64,2304]{1,0:T(8,128)(2,1)S(1)}, u32[]{:S(2)}, u32[]{:S(2)}) %collective-permute-start.11) | collective-permute-done | bytes 294944 | tf_op jit(solution)/shard_map/ppermute | solution.py:23
  191.0 5.5 %collective-permute-done.13 = bf16[256,256]{1,0:T(8,128)(2,1)S(1)} collective-permute-done((bf16[256,256]{1,0:T(8,128)(2,1)S(1)}, bf16[256,256]{1,0:T(8,128)(2,1)S(1)}, u32[]{:S(2)}, u32[]{:S(2)}) %collective-permute-start.13) | collective-permute-done | bytes 131104 | tf_op jit(solution)/shard_map/ppermute | solution.py:18
  196.6 9.0 %collective-permute-start.14 = (bf16[256,256]{1,0:T(8,128)(2,1)S(1)}, bf16[256,256]{1,0:T(8,128)(2,1)S(1)}, u32[]{:S(2)}, u32[]{:S(2)}) collective-permute-start(bf16[256,256]{1,0:T(8,128)(2,1)S(1)} %fusion.32), channel_id=1, source_target_pairs={{16,0},{24,8},{32,16},{40,24},{48,32},{56,40},{64,48},{72,56},{80,... | collective-permute-start | bytes 393224 | tf_op jit(solution)/shard_map/ppermute | solution.py:18
  208.2 10.0 %collective-permute-start.15 = (bf16[256,256]{1,0:T(8,128)(2,1)S(1)}, bf16[256,256]{1,0:T(8,128)(2,1)S(1)}, u32[]{:S(2)}, u32[]{:S(2)}) collective-permute-start(bf16[256,256]{1,0:T(8,128)(2,1)S(1)} %fusion.34), channel_id=1, source_target_pairs={{16,0},{24,8},{32,16},{40,24},{48,32},{56,40},{64,48},{72,56},{80,... | collective-permute-start | bytes 393224 | tf_op jit(solution)/shard_map/ppermute | solution.py:18
  220.7 9.1 %collective-permute-start.16 = (bf16[256,256]{1,0:T(8,128)(2,1)S(1)}, bf16[256,256]{1,0:T(8,128)(2,1)S(1)}, u32[]{:S(2)}, u32[]{:S(2)}) collective-permute-start(bf16[256,256]{1,0:T(8,128)(2,1)S(1)} %fusion.36), channel_id=1, source_target_pairs={{16,0},{24,8},{32,16},{40,24},{48,32},{56,40},{64,48},{72,56},{80,... | collective-permute-start | bytes 393224 | tf_op jit(solution)/shard_map/ppermute | solution.py:18
  (109 shorter events, 67.7 us)
Async XLA Ops:
  0.6 134.5 %copy-start = (bf16[576,2304]{1,0:T(8,128)(2,1)S(1)}, bf16[576,2304]{1,0:T(8,128)(2,1)}, u32[]{:S(2)}) copy-start(bf16[576,2304]{1,0:T(8,128)(2,1)} %param.23) | copy-start | bytes 7962628
  4.9 31.0 %collective-permute-start = (bf16[520,256]{1,0:T(8,128)(2,1)S(1)}, bf16[520,256]{1,0:T(8,128)(2,1)S(1)}, u32[]{:S(2)}, u32[]{:S(2)}) collective-permute-start(bf16[520,256]{1,0:T(8,128)(2,1)S(1)} %constant_dynamic-update-slice_fusion), channel_id=1, source_target_pairs={{0,16},{8,24},{16,32},{24,40},{32,48},{40,56},{48,64},{56,72},{64,... | collective-permute-start | bytes 798728 | tf_op jit(solution)/shard_map/ppermute | solution.py:18
  35.9 17.9 %collective-permute-start.1 = (bf16[520,256]{1,0:T(8,128)(2,1)S(1)}, bf16[520,256]{1,0:T(8,128)(2,1)S(1)}, u32[]{:S(2)}, u32[]{:S(2)}) collective-permute-start(bf16[520,256]{1,0:T(8,128)(2,1)S(1)} %collective-permute-done), channel_id=1, source_target_pairs={{0,16},{8,24},{16,32},{24,40},{32,48},{40,56},{48,64},{56,72},{64,... | collective-permute-start | bytes 798728 | tf_op jit(solution)/shard_map/ppermute | solution.py:18
  53.8 14.9 %collective-permute-start.2 = (bf16[520,256]{1,0:T(8,128)(2,1)S(1)}, bf16[520,256]{1,0:T(8,128)(2,1)}, u32[]{:S(2)}, u32[]{:S(2)}) collective-permute-start(bf16[520,256]{1,0:T(8,128)(2,1)S(1)} %collective-permute-done.1), channel_id=1, source_target_pairs={{0,16},{8,24},{16,32},{24,40},{32,48},{40,56},{48,64},{56,72},{64,... | collective-permute-start | bytes 798728 | tf_op jit(solution)/shard_map/ppermute | solution.py:18
  68.7 13.9 %collective-permute-start.3 = (bf16[520,256]{1,0:T(8,128)(2,1)}, bf16[520,256]{1,0:T(8,128)(2,1)S(1)}, u32[]{:S(2)}, u32[]{:S(2)}) collective-permute-start(bf16[520,256]{1,0:T(8,128)(2,1)} %collective-permute-done.2), channel_id=1, source_target_pairs={{0,16},{8,24},{16,32},{24,40},{32,48},{40,56},{48,64},{56,72},{64,... | collective-permute-start | bytes 798728 | tf_op jit(solution)/shard_map/ppermute | solution.py:18
  85.6 4.9 %collective-permute-start.4 = (bf16[4,520,256]{2,1,0:T(8,128)(2,1)}, bf16[4,520,256]{2,1,0:T(8,128)(2,1)}, u32[]{:S(2)}, u32[]{:S(2)}) collective-permute-start(bf16[4,520,256]{2,1,0:T(8,128)(2,1)} %constant_dynamic-slice_fusion), channel_id=1, source_target_pairs={{0,8},{8,0},{16,24},{24,16},{32,40},{40,32},{48,56},{56,48},{64,72... | collective-permute-start | bytes 3194888 | tf_op jit(solution)/shard_map/ppermute | solution.py:23
  107.7 6.2 %copy-start.6 = (bf16[128,128]{0,1:T(8,128)(2,1)}, bf16[128,128]{0,1:T(8,128)(2,1)S(1)}, u32[]{:S(2)}) copy-start(bf16[128,128]{0,1:T(8,128)(2,1)S(1)} %convolution_convert_fusion.2) | copy-start | bytes 98308
  107.7 6.2 %collective-permute-start.5 = (bf16[128,256]{0,1:T(8,128)(2,1)S(1)}, bf16[128,256]{0,1:T(8,128)(2,1)S(1)}, u32[]{:S(2)}, u32[]{:S(2)}) collective-permute-start(bf16[128,256]{0,1:T(8,128)(2,1)S(1)} %pad_maximum_fusion.1), channel_id=1, source_target_pairs={{0,1},{1,0},{2,3},{3,2},{4,5},{5,4},{6,7},{7,6},{8,9},{9,8},{10,11... | collective-permute-start | bytes 196616 | tf_op jit(solution)/shard_map/ppermute | solution.py:23
  114.5 8.6 %collective-permute-start.6 = (bf16[128,512]{0,1:T(8,128)(2,1)S(1)}, bf16[128,512]{0,1:T(8,128)(2,1)S(1)}, u32[]{:S(2)}, u32[]{:S(2)}) collective-permute-start(bf16[128,512]{0,1:T(8,128)(2,1)S(1)} %maximum_select_fusion.3), channel_id=1, source_target_pairs={{0,2},{1,3},{2,0},{3,1},{4,6},{5,7},{6,4},{7,5},{8,10},{9,11},{10,... | collective-permute-start | bytes 393224 | tf_op jit(solution)/shard_map/ppermute | solution.py:23
  123.2 9.4 %collective-permute-start.7 = (bf16[128,1024]{0,1:T(8,128)(2,1)S(1)}, bf16[128,1024]{0,1:T(8,128)(2,1)S(1)}, u32[]{:S(2)}, u32[]{:S(2)}) collective-permute-start(bf16[128,1024]{0,1:T(8,128)(2,1)S(1)} %maximum_select_fusion.2), channel_id=1, source_target_pairs={{0,4},{1,5},{2,6},{3,7},{4,0},{5,1},{6,2},{7,3},{8,12},{9,13},{10,... | collective-permute-start | bytes 786440 | tf_op jit(solution)/shard_map/ppermute | solution.py:23
  128.7 6.5 %copy-start.13 = (f32[128]{0:T(128)S(1)}, f32[128]{0:T(128)}, u32[]{:S(2)}) copy-start(f32[128]{0:T(128)} %select_reduce_fusion.3) | copy-start | bytes 1540
  140.1 8.9 %collective-permute-start.8 = (bf16[64,2304]{1,0:T(8,128)(2,1)S(1)}, bf16[64,2304]{1,0:T(8,128)(2,1)S(1)}, u32[]{:S(2)}, u32[]{:S(2)}) collective-permute-start(bf16[64,2304]{1,0:T(8,128)(2,1)S(1)} %select_convert_fusion), channel_id=1, source_target_pairs={{0,4},{1,5},{2,6},{3,7},{4,0},{5,1},{6,2},{7,3},{8,12},{9,13},{10,... | collective-permute-start | bytes 884744 | tf_op jit(solution)/shard_map/ppermute | solution.py:23
  150.3 28.3 %copy-start.14 = (bf16[256,2304]{1,0:T(8,128)(2,1)S(1)}, bf16[256,2304]{1,0:T(8,128)(2,1)}, u32[]{:S(2)}) copy-start(bf16[256,2304]{1,0:T(8,128)(2,1)} %param.22) | copy-start | bytes 3538948
  150.3 9.2 %collective-permute-start.9 = (bf16[64,2304]{1,0:T(8,128)(2,1)S(1)}, bf16[64,2304]{1,0:T(8,128)(2,1)S(1)}, u32[]{:S(2)}, u32[]{:S(2)}) collective-permute-start(bf16[64,2304]{1,0:T(8,128)(2,1)S(1)} %get-tuple-element.8), channel_id=1, source_target_pairs={{0,1},{1,0},{2,3},{3,2},{4,5},{5,4},{6,7},{7,6},{8,9},{9,8},{10,11... | collective-permute-start | bytes 884744 | tf_op jit(solution)/shard_map/ppermute | solution.py:23
  159.6 10.1 %collective-permute-start.10 = (bf16[64,2304]{1,0:T(8,128)(2,1)S(1)}, bf16[64,2304]{1,0:T(8,128)(2,1)S(1)}, u32[]{:S(2)}, u32[]{:S(2)}) collective-permute-start(bf16[64,2304]{1,0:T(8,128)(2,1)S(1)} %fusion.23), channel_id=1, source_target_pairs={{0,2},{1,3},{2,0},{3,1},{4,6},{5,7},{6,4},{7,5},{8,10},{9,11},{10,... | collective-permute-start | bytes 884744 | tf_op jit(solution)/shard_map/ppermute | solution.py:23
  169.8 9.3 %copy-start.4 = (f32[128,1152]{0,1:T(8,128)S(1)}, f32[128,1152]{0,1:T(8,128)}, u32[]{:S(2)}) copy-start(f32[128,1152]{0,1:T(8,128)} %copy-done.3) | copy-start | bytes 1769476
  169.8 9.3 %copy-start.11 = (f32[128]{0:T(128)S(1)}, f32[128]{0:T(128)}, u32[]{:S(2)}) copy-start(f32[128]{0:T(128)} %copy-done.10) | copy-start | bytes 1540
  169.8 9.3 %copy-start.12 = (f32[128]{0:T(128)S(1)}, f32[128]{0:T(128)}, u32[]{:S(2)}) copy-start(f32[128]{0:T(128)} %get-tuple-element.4) | copy-start | bytes 1540
  169.8 8.7 %collective-permute-start.11 = (bf16[64,2304]{1,0:T(8,128)(2,1)S(1)}, bf16[64,2304]{1,0:T(8,128)(2,1)S(1)}, u32[]{:S(2)}, u32[]{:S(2)}) collective-permute-start(bf16[64,2304]{1,0:T(8,128)(2,1)S(1)} %add_convert_fusion), channel_id=1, source_target_pairs={{0,4},{1,5},{2,6},{3,7},{4,0},{5,1},{6,2},{7,3},{8,12},{9,13},{10,... | collective-permute-start | bytes 884744 | tf_op jit(solution)/shard_map/ppermute | solution.py:23
  183.6 4.1 %collective-permute-start.12 = (bf16[4,256,256]{2,1,0:T(8,128)(2,1)}, bf16[4,256,256]{2,1,0:T(8,128)(2,1)}, u32[]{:S(2)}, u32[]{:S(2)}) collective-permute-start(bf16[4,256,256]{2,1,0:T(8,128)(2,1)} %slice.104), channel_id=1, source_target_pairs={{0,8},{8,0},{16,24},{24,16},{32,40},{40,32},{48,56},{56,48},{64,72... | collective-permute-start | bytes 1572872 | tf_op jit(solution)/shard_map/ppermute | solution.py:23
  189.1 7.5 %collective-permute-start.13 = (bf16[256,256]{1,0:T(8,128)(2,1)S(1)}, bf16[256,256]{1,0:T(8,128)(2,1)S(1)}, u32[]{:S(2)}, u32[]{:S(2)}) collective-permute-start(bf16[256,256]{1,0:T(8,128)(2,1)S(1)} %fusion.42), channel_id=1, source_target_pairs={{16,0},{24,8},{32,16},{40,24},{48,32},{56,40},{64,48},{72,56},{80,... | collective-permute-start | bytes 393224 | tf_op jit(solution)/shard_map/ppermute | solution.py:18
  196.6 11.5 %collective-permute-start.14 = (bf16[256,256]{1,0:T(8,128)(2,1)S(1)}, bf16[256,256]{1,0:T(8,128)(2,1)S(1)}, u32[]{:S(2)}, u32[]{:S(2)}) collective-permute-start(bf16[256,256]{1,0:T(8,128)(2,1)S(1)} %fusion.32), channel_id=1, source_target_pairs={{16,0},{24,8},{32,16},{40,24},{48,32},{56,40},{64,48},{72,56},{80,... | collective-permute-start | bytes 393224 | tf_op jit(solution)/shard_map/ppermute | solution.py:18
  208.2 12.5 %collective-permute-start.15 = (bf16[256,256]{1,0:T(8,128)(2,1)S(1)}, bf16[256,256]{1,0:T(8,128)(2,1)S(1)}, u32[]{:S(2)}, u32[]{:S(2)}) collective-permute-start(bf16[256,256]{1,0:T(8,128)(2,1)S(1)} %fusion.34), channel_id=1, source_target_pairs={{16,0},{24,8},{32,16},{40,24},{48,32},{56,40},{64,48},{72,56},{80,... | collective-permute-start | bytes 393224 | tf_op jit(solution)/shard_map/ppermute | solution.py:18
  220.7 11.6 %collective-permute-start.16 = (bf16[256,256]{1,0:T(8,128)(2,1)S(1)}, bf16[256,256]{1,0:T(8,128)(2,1)S(1)}, u32[]{:S(2)}, u32[]{:S(2)}) collective-permute-start(bf16[256,256]{1,0:T(8,128)(2,1)S(1)} %fusion.36), channel_id=1, source_target_pairs={{16,0},{24,8},{32,16},{40,24},{48,32},{56,40},{64,48},{72,56},{80,... | collective-permute-start | bytes 393224 | tf_op jit(solution)/shard_map/ppermute | solution.py:18
  (11 other events, 20.2 us)

commit v9 on v6

--- a/solution.py
+++ b/solution.py
@@ -205,7 +205,7 @@
     grads = jnp.concatenate(
         [grad_k.reshape(blocks, rows, width), grad_v.reshape(blocks, rows, width)], 1
     )
-    from_partner = swapped(grads[1::2], "seq", 1)
+    from_partner = swapped(grads[1::2].astype(jnp.bfloat16), "seq", 1).astype(jnp.float32)
     nothing = jnp.zeros_like(from_partner[:1])
     added = jnp.where(
         core == 1,

time: 225 us -> 223 us (level)
  waiting for transfers between devices: 116 us -> 113 us
    ppermute x9, waiting for transfers between devices: 39.8 us -> 37.1 us  [swapped(): return lax.ppermute(value, axis, [(i, i ^ bit) for i in range(length)])]
    unnamed x45 -> x47, local copies, waits for them, and re-layouts: 10.9 us -> 10.3 us
  transfers between devices with their start and end apart: 17 -> 17, of which waited for: 17 -> 17; matrix products, arithmetic and copies ran while one was open for 4% -> 5% of each run, Pallas kernels for 0% -> 0%
where the time goes in v9:
time: 223 us; the launch traced here: 222 us
  waiting for transfers between devices  113 us (51%)
  starting transfers between devices  68.7 us (31%)
  local copies, waits for them, and re-layouts  15 us (7%)
  matrix products  13.4 us (6%)
  other arithmetic  10.5 us (5%)
    ppermute x8, waiting for transfers between devices, shifted(): return lax.ppermute(value, axis, pairs)  75.9 us
    ppermute x8, starting transfers between devices, shifted(): return lax.ppermute(value, axis, pairs)  41.6 us
    ppermute x9, waiting for transfers between devices, swapped(): return lax.ppermute(value, axis, [(i, i ^ bit) for i in range(length)])  37.1 us
    ppermute x9, starting transfers between devices, swapped(): return lax.ppermute(value, axis, [(i, i ^ bit) for i in range(length)])  27.1 us
    unnamed x47, local copies, waits for them, and re-layouts  10.3 us
    dot_general x1, matrix products, shards(): jnp.dot(target_cols, match_proj, preferred_element_type=jnp.float32)  4.88 us
  transfers between devices with their start and end apart: 17, of which 17 were waited for; matrix products, arithmetic and copies ran while one was open for 5% of the time, Pallas kernels for 0%

profile of v9, /device:TPU:46, one launch (start us, length us, event | category | flops | bytes accessed | tf_op | source)
XLA Modules:
  0.0 221.8 jit_solution(11259775858446723980)
XLA Ops:
  4.9 4.3 %collective-permute-start = (bf16[520,256]{1,0:T(8,128)(2,1)S(1)}, bf16[520,256]{1,0:T(8,128)(2,1)S(1)}, u32[]{:S(2)}, u32[]{:S(2)}) collective-permute-start(bf16[520,256]{1,0:T(8,128)(2,1)S(1)} %constant_dynamic-update-slice_fusion), channel_id=1, source_target_pairs={{0,16},{8,24},{16,32},{24,40},{32,48},{40,56},{48,64},{56,72},{64,... | collective-permute-start | bytes 798728 | tf_op jit(solution)/shard_map/ppermute | solution.py:18
  9.1 26.8 %collective-permute-done = bf16[520,256]{1,0:T(8,128)(2,1)S(1)} collective-permute-done((bf16[520,256]{1,0:T(8,128)(2,1)S(1)}, bf16[520,256]{1,0:T(8,128)(2,1)S(1)}, u32[]{:S(2)}, u32[]{:S(2)}) %collective-permute-start) | collective-permute-done | bytes 266272 | tf_op jit(solution)/shard_map/ppermute | solution.py:18
  37.8 15.9 %collective-permute-done.1 = bf16[520,256]{1,0:T(8,128)(2,1)S(1)} collective-permute-done((bf16[520,256]{1,0:T(8,128)(2,1)S(1)}, bf16[520,256]{1,0:T(8,128)(2,1)S(1)}, u32[]{:S(2)}, u32[]{:S(2)}) %collective-permute-start.1) | collective-permute-done | bytes 266272 | tf_op jit(solution)/shard_map/ppermute | solution.py:18
  57.1 11.6 %collective-permute-done.2 = bf16[520,256]{1,0:T(8,128)(2,1)} collective-permute-done((bf16[520,256]{1,0:T(8,128)(2,1)S(1)}, bf16[520,256]{1,0:T(8,128)(2,1)}, u32[]{:S(2)}, u32[]{:S(2)}) %collective-permute-start.2) | collective-permute-done | bytes 266272 | tf_op jit(solution)/shard_map/ppermute | solution.py:18
  73.0 9.5 %collective-permute-done.3 = bf16[520,256]{1,0:T(8,128)(2,1)S(1)} collective-permute-done((bf16[520,256]{1,0:T(8,128)(2,1)}, bf16[520,256]{1,0:T(8,128)(2,1)S(1)}, u32[]{:S(2)}, u32[]{:S(2)}) %collective-permute-start.3) | collective-permute-done | bytes 266272 | tf_op jit(solution)/shard_map/ppermute | solution.py:18
  86.5 2.6 %collective-permute-done.4 = bf16[4,520,256]{2,1,0:T(8,128)(2,1)S(1)} collective-permute-done((bf16[4,520,256]{2,1,0:T(8,128)(2,1)S(1)}, bf16[4,520,256]{2,1,0:T(8,128)(2,1)S(1)}, u32[]{:S(2)}, u32[]{:S(2)}) %collective-permute-start.4) | collective-permute-done | bytes 1064992 | tf_op jit(solution)/shard_map/ppermute | solution.py:23
  94.5 2.7 %collective-permute-start.5 = (bf16[128,256]{0,1:T(8,128)(2,1)S(1)}, bf16[128,256]{0,1:T(8,128)(2,1)}, u32[]{:S(2)}, u32[]{:S(2)}) collective-permute-start(bf16[128,256]{0,1:T(8,128)(2,1)S(1)} %pad_maximum_fusion.1), channel_id=1, source_target_pairs={{0,1},{1,0},{2,3},{3,2},{4,5},{5,4},{6,7},{7,6},{8,9},{9,8},{10,11... | collective-permute-start | bytes 196616 | tf_op jit(solution)/shard_map/ppermute | solution.py:23
  97.3 3.5 %collective-permute-done.5 = bf16[128,256]{0,1:T(8,128)(2,1)} collective-permute-done((bf16[128,256]{0,1:T(8,128)(2,1)S(1)}, bf16[128,256]{0,1:T(8,128)(2,1)}, u32[]{:S(2)}, u32[]{:S(2)}) %collective-permute-start.5) | collective-permute-done | bytes 65568 | tf_op jit(solution)/shard_map/ppermute | solution.py:23
  101.7 3.3 %collective-permute-start.6 = (bf16[128,512]{0,1:T(8,128)(2,1)S(1)}, bf16[128,512]{0,1:T(8,128)(2,1)}, u32[]{:S(2)}, u32[]{:S(2)}) collective-permute-start(bf16[128,512]{0,1:T(8,128)(2,1)S(1)} %maximum_select_fusion.6), channel_id=1, source_target_pairs={{0,2},{1,3},{2,0},{3,1},{4,6},{5,7},{6,4},{7,5},{8,10},{9,11},{10,... | collective-permute-start | bytes 393224 | tf_op jit(solution)/shard_map/ppermute | solution.py:23
  105.2 5.0 %collective-permute-done.6 = bf16[128,512]{0,1:T(8,128)(2,1)} collective-permute-done((bf16[128,512]{0,1:T(8,128)(2,1)S(1)}, bf16[128,512]{0,1:T(8,128)(2,1)}, u32[]{:S(2)}, u32[]{:S(2)}) %collective-permute-start.6) | collective-permute-done | bytes 131104 | tf_op jit(solution)/shard_map/ppermute | solution.py:23
  111.4 4.2 %collective-permute-start.7 = (bf16[128,1024]{0,1:T(8,128)(2,1)S(1)}, bf16[128,1024]{0,1:T(8,128)(2,1)}, u32[]{:S(2)}, u32[]{:S(2)}) collective-permute-start(bf16[128,1024]{0,1:T(8,128)(2,1)S(1)} %maximum_select_fusion.5), channel_id=1, source_target_pairs={{0,4},{1,5},{2,6},{3,7},{4,0},{5,1},{6,2},{7,3},{8,12},{9,13},{10,... | collective-permute-start | bytes 786440 | tf_op jit(solution)/shard_map/ppermute | solution.py:23
  115.6 3.6 %fusion.4 = f32[128,2304]{1,0:T(8,128)} fusion(bf16[256,2304]{1,0:T(8,128)(2,1)} %param.22, bf16[1152,256]{1,0:T(8,128)(2,1)} %bitcast.79, f32[128,1152]{0,1:T(8,128)} %copy-done.3, f32[128]{0:T(128)S(1)} %get-tuple-element.4, f32[128]{0:T(128)S(1)} %get-tuple-element.7, s32[128]{0:T(128)S(1)} %get-tuple-element.24, s32[128]{0:T(128)S(1)} %get-tuple-element.18, ...), kind=kOutput, calls=%fused_computation.15 | convolution fusion | flops 227852288 | bytes 3545600 | tf_op jit(solution)/shard_map/dot_general | solution.py:175
  120.0 4.9 %fusion = f32[128,2304]{1,0:T(8,128)} fusion(f32[128,2304]{1,0:T(8,128)} %fusion.4, bf16[576,2304]{1,0:T(8,128)(2,1)S(1)} %copy-done, bf16[576,2048]{1,0:T(8,128)(2,1)} %param.21, f32[128]{0:T(128)S(1)} %select_reduce_fusion.3, bf16[128,1024]{0,1:T(8,128)(2,1)S(1)} %maximum_select_fusion.5, bf16[128,1024]{0,1:T(8,128)(2,1)} %collective-permute-done.7, ...), kind=kOutput, calls=%fused_computation.1 | convolution fusion | flops 644751360 | bytes 7897601 | tf_op jit(solution)/shard_map/dot_general | solution.py:176
  126.2 3.9 %collective-permute-start.8 = (bf16[64,2304]{1,0:T(8,128)(2,1)S(1)}, bf16[64,2304]{1,0:T(8,128)(2,1)S(1)}, u32[]{:S(2)}, u32[]{:S(2)}) collective-permute-start(bf16[64,2304]{1,0:T(8,128)(2,1)S(1)} %select_convert_fusion), channel_id=1, source_target_pairs={{0,4},{1,5},{2,6},{3,7},{4,0},{5,1},{6,2},{7,3},{8,12},{9,13},{10,... | collective-permute-start | bytes 884744 | tf_op jit(solution)/shard_map/ppermute | solution.py:23
  130.1 4.7 %collective-permute-done.8 = bf16[64,2304]{1,0:T(8,128)(2,1)S(1)} collective-permute-done((bf16[64,2304]{1,0:T(8,128)(2,1)S(1)}, bf16[64,2304]{1,0:T(8,128)(2,1)S(1)}, u32[]{:S(2)}, u32[]{:S(2)}) %collective-permute-start.8) | collective-permute-done | bytes 294944 | tf_op jit(solution)/shard_map/ppermute | solution.py:23
  136.1 2.9 %collective-permute-start.9 = (bf16[64,2304]{1,0:T(8,128)(2,1)S(1)}, bf16[64,2304]{1,0:T(8,128)(2,1)S(1)}, u32[]{:S(2)}, u32[]{:S(2)}) collective-permute-start(bf16[64,2304]{1,0:T(8,128)(2,1)S(1)} %get-tuple-element.8), channel_id=1, source_target_pairs={{0,1},{1,0},{2,3},{3,2},{4,5},{5,4},{6,7},{7,6},{8,9},{9,8},{10,11... | collective-permute-start | bytes 884744 | tf_op jit(solution)/shard_map/ppermute | solution.py:23
  139.0 7.3 %collective-permute-done.9 = bf16[64,2304]{1,0:T(8,128)(2,1)S(1)} collective-permute-done((bf16[64,2304]{1,0:T(8,128)(2,1)S(1)}, bf16[64,2304]{1,0:T(8,128)(2,1)S(1)}, u32[]{:S(2)}, u32[]{:S(2)}) %collective-permute-start.9) | collective-permute-done | bytes 294944 | tf_op jit(solution)/shard_map/ppermute | solution.py:23
  148.3 8.2 %collective-permute-done.10 = bf16[64,2304]{1,0:T(8,128)(2,1)S(1)} collective-permute-done((bf16[64,2304]{1,0:T(8,128)(2,1)S(1)}, bf16[64,2304]{1,0:T(8,128)(2,1)S(1)}, u32[]{:S(2)}, u32[]{:S(2)}) %collective-permute-start.10) | collective-permute-done | bytes 294944 | tf_op jit(solution)/shard_map/ppermute | solution.py:23
  156.6 4.3 %collective-permute-start.11 = (bf16[64,2304]{1,0:T(8,128)(2,1)S(1)}, bf16[64,2304]{1,0:T(8,128)(2,1)S(1)}, u32[]{:S(2)}, u32[]{:S(2)}) collective-permute-start(bf16[64,2304]{1,0:T(8,128)(2,1)S(1)} %add_convert_fusion), channel_id=1, source_target_pairs={{0,4},{1,5},{2,6},{3,7},{4,0},{5,1},{6,2},{7,3},{8,12},{9,13},{10,... | collective-permute-start | bytes 884744 | tf_op jit(solution)/shard_map/ppermute | solution.py:23
  160.9 4.7 %collective-permute-done.11 = bf16[64,2304]{1,0:T(8,128)(2,1)S(1)} collective-permute-done((bf16[64,2304]{1,0:T(8,128)(2,1)S(1)}, bf16[64,2304]{1,0:T(8,128)(2,1)S(1)}, u32[]{:S(2)}, u32[]{:S(2)}) %collective-permute-start.11) | collective-permute-done | bytes 294944 | tf_op jit(solution)/shard_map/ppermute | solution.py:23
  178.3 5.5 %collective-permute-done.13 = bf16[256,256]{1,0:T(8,128)(2,1)S(1)} collective-permute-done((bf16[256,256]{1,0:T(8,128)(2,1)S(1)}, bf16[256,256]{1,0:T(8,128)(2,1)S(1)}, u32[]{:S(2)}, u32[]{:S(2)}) %collective-permute-start.13) | collective-permute-done | bytes 131104 | tf_op jit(solution)/shard_map/ppermute | solution.py:18
  183.9 9.5 %collective-permute-start.14 = (bf16[256,256]{1,0:T(8,128)(2,1)S(1)}, bf16[256,256]{1,0:T(8,128)(2,1)S(1)}, u32[]{:S(2)}, u32[]{:S(2)}) collective-permute-start(bf16[256,256]{1,0:T(8,128)(2,1)S(1)} %fusion.35), channel_id=1, source_target_pairs={{16,0},{24,8},{32,16},{40,24},{48,32},{56,40},{64,48},{72,56},{80,... | collective-permute-start | bytes 393224 | tf_op jit(solution)/shard_map/ppermute | solution.py:18
  195.9 10.6 %collective-permute-start.15 = (bf16[256,256]{1,0:T(8,128)(2,1)S(1)}, bf16[256,256]{1,0:T(8,128)(2,1)S(1)}, u32[]{:S(2)}, u32[]{:S(2)}) collective-permute-start(bf16[256,256]{1,0:T(8,128)(2,1)S(1)} %fusion.37), channel_id=1, source_target_pairs={{16,0},{24,8},{32,16},{40,24},{48,32},{56,40},{64,48},{72,56},{80,... | collective-permute-start | bytes 393224 | tf_op jit(solution)/shard_map/ppermute | solution.py:18
  209.1 9.5 %collective-permute-start.16 = (bf16[256,256]{1,0:T(8,128)(2,1)S(1)}, bf16[256,256]{1,0:T(8,128)(2,1)S(1)}, u32[]{:S(2)}, u32[]{:S(2)}) collective-permute-start(bf16[256,256]{1,0:T(8,128)(2,1)S(1)} %fusion.39), channel_id=1, source_target_pairs={{16,0},{24,8},{32,16},{40,24},{48,32},{56,40},{64,48},{72,56},{80,... | collective-permute-start | bytes 393224 | tf_op jit(solution)/shard_map/ppermute | solution.py:18
  (100 shorter events, 51.5 us)
Async XLA Ops:
  0.6 119.4 %copy-start = (bf16[576,2304]{1,0:T(8,128)(2,1)S(1)}, bf16[576,2304]{1,0:T(8,128)(2,1)}, u32[]{:S(2)}) copy-start(bf16[576,2304]{1,0:T(8,128)(2,1)} %param.23) | copy-start | bytes 7962628
  4.9 31.0 %collective-permute-start = (bf16[520,256]{1,0:T(8,128)(2,1)S(1)}, bf16[520,256]{1,0:T(8,128)(2,1)S(1)}, u32[]{:S(2)}, u32[]{:S(2)}) collective-permute-start(bf16[520,256]{1,0:T(8,128)(2,1)S(1)} %constant_dynamic-update-slice_fusion), channel_id=1, source_target_pairs={{0,16},{8,24},{16,32},{24,40},{32,48},{40,56},{48,64},{56,72},{64,... | collective-permute-start | bytes 798728 | tf_op jit(solution)/shard_map/ppermute | solution.py:18
  35.9 17.9 %collective-permute-start.1 = (bf16[520,256]{1,0:T(8,128)(2,1)S(1)}, bf16[520,256]{1,0:T(8,128)(2,1)S(1)}, u32[]{:S(2)}, u32[]{:S(2)}) collective-permute-start(bf16[520,256]{1,0:T(8,128)(2,1)S(1)} %collective-permute-done), channel_id=1, source_target_pairs={{0,16},{8,24},{16,32},{24,40},{32,48},{40,56},{48,64},{56,72},{64,... | collective-permute-start | bytes 798728 | tf_op jit(solution)/shard_map/ppermute | solution.py:18
  53.8 14.9 %collective-permute-start.2 = (bf16[520,256]{1,0:T(8,128)(2,1)S(1)}, bf16[520,256]{1,0:T(8,128)(2,1)}, u32[]{:S(2)}, u32[]{:S(2)}) collective-permute-start(bf16[520,256]{1,0:T(8,128)(2,1)S(1)} %collective-permute-done.1), channel_id=1, source_target_pairs={{0,16},{8,24},{16,32},{24,40},{32,48},{40,56},{48,64},{56,72},{64,... | collective-permute-start | bytes 798728 | tf_op jit(solution)/shard_map/ppermute | solution.py:18
  68.7 13.9 %collective-permute-start.3 = (bf16[520,256]{1,0:T(8,128)(2,1)}, bf16[520,256]{1,0:T(8,128)(2,1)S(1)}, u32[]{:S(2)}, u32[]{:S(2)}) collective-permute-start(bf16[520,256]{1,0:T(8,128)(2,1)} %collective-permute-done.2), channel_id=1, source_target_pairs={{0,16},{8,24},{16,32},{24,40},{32,48},{40,56},{48,64},{56,72},{64,... | collective-permute-start | bytes 798728 | tf_op jit(solution)/shard_map/ppermute | solution.py:18
  84.6 4.6 %collective-permute-start.4 = (bf16[4,520,256]{2,1,0:T(8,128)(2,1)S(1)}, bf16[4,520,256]{2,1,0:T(8,128)(2,1)S(1)}, u32[]{:S(2)}, u32[]{:S(2)}) collective-permute-start(bf16[4,520,256]{2,1,0:T(8,128)(2,1)S(1)} %constant_dynamic-slice_fusion), channel_id=1, source_target_pairs={{0,8},{8,0},{16,24},{24,16},{32,40},{40,32},{48,56},{56,48},{64,72... | collective-permute-start | bytes 3194888 | tf_op jit(solution)/shard_map/ppermute | solution.py:23
  92.6 74.0 %copy-start.9 = (f32[128]{0:T(128)}, f32[128]{0:T(128)S(1)}, u32[]{:S(2)}) copy-start(f32[128]{0:T(128)S(1)} %get-tuple-element.7) | copy-start | bytes 1540
  93.1 73.5 %copy-start.10 = (f32[128]{0:T(128)}, f32[128]{0:T(128)S(1)}, u32[]{:S(2)}) copy-start(f32[128]{0:T(128)S(1)} %get-tuple-element.4) | copy-start | bytes 1540
  93.9 11.2 %copy-start.13 = (f32[16]{0:T(128)S(1)}, f32[16]{0:T(128)}, u32[]{:S(2)}) copy-start(f32[16]{0:T(128)} %param.20) | copy-start | bytes 196
  93.9 11.2 %copy-start.14 = (s32[128]{0:T(128)S(1)}, s32[128]{0:T(128)}, u32[]{:S(2)}) copy-start(s32[128]{0:T(128)} %param.19) | copy-start | bytes 1540
  94.5 6.3 %collective-permute-start.5 = (bf16[128,256]{0,1:T(8,128)(2,1)S(1)}, bf16[128,256]{0,1:T(8,128)(2,1)}, u32[]{:S(2)}, u32[]{:S(2)}) collective-permute-start(bf16[128,256]{0,1:T(8,128)(2,1)S(1)} %pad_maximum_fusion.1), channel_id=1, source_target_pairs={{0,1},{1,0},{2,3},{3,2},{4,5},{5,4},{6,7},{7,6},{8,9},{9,8},{10,11... | collective-permute-start | bytes 196616 | tf_op jit(solution)/shard_map/ppermute | solution.py:23
  101.7 8.5 %collective-permute-start.6 = (bf16[128,512]{0,1:T(8,128)(2,1)S(1)}, bf16[128,512]{0,1:T(8,128)(2,1)}, u32[]{:S(2)}, u32[]{:S(2)}) collective-permute-start(bf16[128,512]{0,1:T(8,128)(2,1)S(1)} %maximum_select_fusion.6), channel_id=1, source_target_pairs={{0,2},{1,3},{2,0},{3,1},{4,6},{5,7},{6,4},{7,5},{8,10},{9,11},{10,... | collective-permute-start | bytes 393224 | tf_op jit(solution)/shard_map/ppermute | solution.py:23
  111.4 8.6 %collective-permute-start.7 = (bf16[128,1024]{0,1:T(8,128)(2,1)S(1)}, bf16[128,1024]{0,1:T(8,128)(2,1)}, u32[]{:S(2)}, u32[]{:S(2)}) collective-permute-start(bf16[128,1024]{0,1:T(8,128)(2,1)S(1)} %maximum_select_fusion.5), channel_id=1, source_target_pairs={{0,4},{1,5},{2,6},{3,7},{4,0},{5,1},{6,2},{7,3},{8,12},{9,13},{10,... | collective-permute-start | bytes 786440 | tf_op jit(solution)/shard_map/ppermute | solution.py:23
  126.2 8.6 %collective-permute-start.8 = (bf16[64,2304]{1,0:T(8,128)(2,1)S(1)}, bf16[64,2304]{1,0:T(8,128)(2,1)S(1)}, u32[]{:S(2)}, u32[]{:S(2)}) collective-permute-start(bf16[64,2304]{1,0:T(8,128)(2,1)S(1)} %select_convert_fusion), channel_id=1, source_target_pairs={{0,4},{1,5},{2,6},{3,7},{4,0},{5,1},{6,2},{7,3},{8,12},{9,13},{10,... | collective-permute-start | bytes 884744 | tf_op jit(solution)/shard_map/ppermute | solution.py:23
  136.1 29.5 %copy-start.11 = (bf16[256,2304]{1,0:T(8,128)(2,1)S(1)}, bf16[256,2304]{1,0:T(8,128)(2,1)}, u32[]{:S(2)}) copy-start(bf16[256,2304]{1,0:T(8,128)(2,1)} %param.22) | copy-start | bytes 3538948
  136.1 10.2 %collective-permute-start.9 = (bf16[64,2304]{1,0:T(8,128)(2,1)S(1)}, bf16[64,2304]{1,0:T(8,128)(2,1)S(1)}, u32[]{:S(2)}, u32[]{:S(2)}) collective-permute-start(bf16[64,2304]{1,0:T(8,128)(2,1)S(1)} %get-tuple-element.8), channel_id=1, source_target_pairs={{0,1},{1,0},{2,3},{3,2},{4,5},{5,4},{6,7},{7,6},{8,9},{9,8},{10,11... | collective-permute-start | bytes 884744 | tf_op jit(solution)/shard_map/ppermute | solution.py:23
  146.4 10.1 %collective-permute-start.10 = (bf16[64,2304]{1,0:T(8,128)(2,1)S(1)}, bf16[64,2304]{1,0:T(8,128)(2,1)S(1)}, u32[]{:S(2)}, u32[]{:S(2)}) collective-permute-start(bf16[64,2304]{1,0:T(8,128)(2,1)S(1)} %fusion.29), channel_id=1, source_target_pairs={{0,2},{1,3},{2,0},{3,1},{4,6},{5,7},{6,4},{7,5},{8,10},{9,11},{10,... | collective-permute-start | bytes 884744 | tf_op jit(solution)/shard_map/ppermute | solution.py:23
  156.6 9.6 %copy-start.4 = (f32[128,1152]{0,1:T(8,128)S(1)}, f32[128,1152]{0,1:T(8,128)}, u32[]{:S(2)}) copy-start(f32[128,1152]{0,1:T(8,128)} %copy-done.3) | copy-start | bytes 1769476
  156.6 9.0 %collective-permute-start.11 = (bf16[64,2304]{1,0:T(8,128)(2,1)S(1)}, bf16[64,2304]{1,0:T(8,128)(2,1)S(1)}, u32[]{:S(2)}, u32[]{:S(2)}) collective-permute-start(bf16[64,2304]{1,0:T(8,128)(2,1)S(1)} %add_convert_fusion), channel_id=1, source_target_pairs={{0,4},{1,5},{2,6},{3,7},{4,0},{5,1},{6,2},{7,3},{8,12},{9,13},{10,... | collective-permute-start | bytes 884744 | tf_op jit(solution)/shard_map/ppermute | solution.py:23
  170.9 4.1 %collective-permute-start.12 = (bf16[4,256,256]{2,1,0:T(8,128)(2,1)}, bf16[4,256,256]{2,1,0:T(8,128)(2,1)}, u32[]{:S(2)}, u32[]{:S(2)}) collective-permute-start(bf16[4,256,256]{2,1,0:T(8,128)(2,1)} %slice.104), channel_id=1, source_target_pairs={{0,8},{8,0},{16,24},{24,16},{32,40},{40,32},{48,56},{56,48},{64,72... | collective-permute-start | bytes 1572872 | tf_op jit(solution)/shard_map/ppermute | solution.py:23
  176.4 7.5 %collective-permute-start.13 = (bf16[256,256]{1,0:T(8,128)(2,1)S(1)}, bf16[256,256]{1,0:T(8,128)(2,1)S(1)}, u32[]{:S(2)}, u32[]{:S(2)}) collective-permute-start(bf16[256,256]{1,0:T(8,128)(2,1)S(1)} %fusion.45), channel_id=1, source_target_pairs={{16,0},{24,8},{32,16},{40,24},{48,32},{56,40},{64,48},{72,56},{80,... | collective-permute-start | bytes 393224 | tf_op jit(solution)/shard_map/ppermute | solution.py:18
  183.9 12.1 %collective-permute-start.14 = (bf16[256,256]{1,0:T(8,128)(2,1)S(1)}, bf16[256,256]{1,0:T(8,128)(2,1)S(1)}, u32[]{:S(2)}, u32[]{:S(2)}) collective-permute-start(bf16[256,256]{1,0:T(8,128)(2,1)S(1)} %fusion.35), channel_id=1, source_target_pairs={{16,0},{24,8},{32,16},{40,24},{48,32},{56,40},{64,48},{72,56},{80,... | collective-permute-start | bytes 393224 | tf_op jit(solution)/shard_map/ppermute | solution.py:18
  195.9 13.1 %collective-permute-start.15 = (bf16[256,256]{1,0:T(8,128)(2,1)S(1)}, bf16[256,256]{1,0:T(8,128)(2,1)S(1)}, u32[]{:S(2)}, u32[]{:S(2)}) collective-permute-start(bf16[256,256]{1,0:T(8,128)(2,1)S(1)} %fusion.37), channel_id=1, source_target_pairs={{16,0},{24,8},{32,16},{40,24},{48,32},{56,40},{64,48},{72,56},{80,... | collective-permute-start | bytes 393224 | tf_op jit(solution)/shard_map/ppermute | solution.py:18
  209.1 12.0 %collective-permute-start.16 = (bf16[256,256]{1,0:T(8,128)(2,1)S(1)}, bf16[256,256]{1,0:T(8,128)(2,1)S(1)}, u32[]{:S(2)}, u32[]{:S(2)}) collective-permute-start(bf16[256,256]{1,0:T(8,128)(2,1)S(1)} %fusion.39), channel_id=1, source_target_pairs={{16,0},{24,8},{32,16},{40,24},{48,32},{56,40},{64,48},{72,56},{80,... | collective-permute-start | bytes 393224 | tf_op jit(solution)/shard_map/ppermute | solution.py:18
  (8 other events, 11.7 us)

commit v10 on v9

--- a/solution.py
+++ b/solution.py
@@ -206,16 +206,17 @@
         [grad_k.reshape(blocks, rows, width), grad_v.reshape(blocks, rows, width)], 1
     )
     from_partner = swapped(grads[1::2].astype(jnp.bfloat16), "seq", 1).astype(jnp.float32)
-    nothing = jnp.zeros_like(from_partner[:1])
-    added = jnp.where(
-        core == 1,
-        jnp.concatenate([from_partner, nothing], 0),
-        jnp.concatenate([nothing, from_partner], 0),
-    )
-    even = grads[0::2] + added
-    total = even[0]
-    for k in range(1, steps + 1):
-        total = even[k] + shifted(total.astype(jnp.bfloat16), "seq", -2).astype(jnp.float32)
+    nothing = jnp.zeros_like(from_partner[0])
+    evens = steps + 1
+
+    def even(k):
+        after = from_partner[k] if k < evens - 1 else nothing
+        before = from_partner[k - 1] if k > 0 else nothing
+        return grads[2 * k] + jnp.where(core == 1, after, before)
+
+    total = even(0)
+    for k in range(1, evens):
+        total = even(k) + shifted(total.astype(jnp.bfloat16), "seq", -2).astype(jnp.float32)
     return (grad_q, total[:rows], total[rows:])
 
 

time: 223 us -> 224 us (level)
    unnamed x47 -> x51, local copies, waits for them, and re-layouts: 10.3 us -> 10.3 us
  transfers between devices with their start and end apart: 17 -> 17, of which waited for: 17 -> 17; matrix products, arithmetic and copies ran while one was open for 5% -> 4% of each run, Pallas kernels for 0% -> 0%
where the time goes in v10:
time: 224 us; the launch traced here: 223 us
  waiting for transfers between devices  115 us (51%)
  starting transfers between devices  68.7 us (31%)
  local copies, waits for them, and re-layouts  15 us (7%)
  matrix products  13.4 us (6%)
  other arithmetic  9.62 us (4%)
    ppermute x8, waiting for transfers between devices, shifted(): return lax.ppermute(value, axis, pairs)  75.9 us
    ppermute x8, starting transfers between devices, shifted(): return lax.ppermute(value, axis, pairs)  41.5 us
    ppermute x9, waiting for transfers between devices, swapped(): return lax.ppermute(value, axis, [(i, i ^ bit) for i in range(length)])  39 us
    ppermute x9, starting transfers between devices, swapped(): return lax.ppermute(value, axis, [(i, i ^ bit) for i in range(length)])  27.1 us
    unnamed x51, local copies, waits for them, and re-layouts  10.3 us
    dot_general x1, matrix products, shards(): jnp.dot(target_cols, match_proj, preferred_element_type=jnp.float32)  4.91 us
  transfers between devices with their start and end apart: 17, of which 17 were waited for; matrix products, arithmetic and copies ran while one was open for 4% of the time, Pallas kernels for 0%

profile of v10, /device:TPU:46, one launch (start us, length us, event | category | flops | bytes accessed | tf_op | source)
XLA Modules:
  0.0 222.8 jit_solution(8261285521174985492)
XLA Ops:
  4.9 4.3 %collective-permute-start = (bf16[520,256]{1,0:T(8,128)(2,1)S(1)}, bf16[520,256]{1,0:T(8,128)(2,1)S(1)}, u32[]{:S(2)}, u32[]{:S(2)}) collective-permute-start(bf16[520,256]{1,0:T(8,128)(2,1)S(1)} %constant_dynamic-update-slice_fusion), channel_id=1, source_target_pairs={{0,16},{8,24},{16,32},{24,40},{32,48},{40,56},{48,64},{56,72},{64,... | collective-permute-start | bytes 798728 | tf_op jit(solution)/shard_map/ppermute | solution.py:18
  9.1 26.8 %collective-permute-done = bf16[520,256]{1,0:T(8,128)(2,1)S(1)} collective-permute-done((bf16[520,256]{1,0:T(8,128)(2,1)S(1)}, bf16[520,256]{1,0:T(8,128)(2,1)S(1)}, u32[]{:S(2)}, u32[]{:S(2)}) %collective-permute-start) | collective-permute-done | bytes 266272 | tf_op jit(solution)/shard_map/ppermute | solution.py:18
  37.8 15.9 %collective-permute-done.1 = bf16[520,256]{1,0:T(8,128)(2,1)S(1)} collective-permute-done((bf16[520,256]{1,0:T(8,128)(2,1)S(1)}, bf16[520,256]{1,0:T(8,128)(2,1)S(1)}, u32[]{:S(2)}, u32[]{:S(2)}) %collective-permute-start.1) | collective-permute-done | bytes 266272 | tf_op jit(solution)/shard_map/ppermute | solution.py:18
  57.1 11.6 %collective-permute-done.2 = bf16[520,256]{1,0:T(8,128)(2,1)} collective-permute-done((bf16[520,256]{1,0:T(8,128)(2,1)S(1)}, bf16[520,256]{1,0:T(8,128)(2,1)}, u32[]{:S(2)}, u32[]{:S(2)}) %collective-permute-start.2) | collective-permute-done | bytes 266272 | tf_op jit(solution)/shard_map/ppermute | solution.py:18
  73.0 9.6 %collective-permute-done.3 = bf16[520,256]{1,0:T(8,128)(2,1)S(1)} collective-permute-done((bf16[520,256]{1,0:T(8,128)(2,1)}, bf16[520,256]{1,0:T(8,128)(2,1)S(1)}, u32[]{:S(2)}, u32[]{:S(2)}) %collective-permute-start.3) | collective-permute-done | bytes 266272 | tf_op jit(solution)/shard_map/ppermute | solution.py:18
  86.5 2.6 %collective-permute-done.4 = bf16[4,520,256]{2,1,0:T(8,128)(2,1)S(1)} collective-permute-done((bf16[4,520,256]{2,1,0:T(8,128)(2,1)S(1)}, bf16[4,520,256]{2,1,0:T(8,128)(2,1)S(1)}, u32[]{:S(2)}, u32[]{:S(2)}) %collective-permute-start.4) | collective-permute-done | bytes 1064992 | tf_op jit(solution)/shard_map/ppermute | solution.py:23
  94.5 2.7 %collective-permute-start.5 = (bf16[128,256]{0,1:T(8,128)(2,1)S(1)}, bf16[128,256]{0,1:T(8,128)(2,1)}, u32[]{:S(2)}, u32[]{:S(2)}) collective-permute-start(bf16[128,256]{0,1:T(8,128)(2,1)S(1)} %pad_maximum_fusion.1), channel_id=1, source_target_pairs={{0,1},{1,0},{2,3},{3,2},{4,5},{5,4},{6,7},{7,6},{8,9},{9,8},{10,11... | collective-permute-start | bytes 196616 | tf_op jit(solution)/shard_map/ppermute | solution.py:23
  97.3 3.5 %collective-permute-done.5 = bf16[128,256]{0,1:T(8,128)(2,1)} collective-permute-done((bf16[128,256]{0,1:T(8,128)(2,1)S(1)}, bf16[128,256]{0,1:T(8,128)(2,1)}, u32[]{:S(2)}, u32[]{:S(2)}) %collective-permute-start.5) | collective-permute-done | bytes 65568 | tf_op jit(solution)/shard_map/ppermute | solution.py:23
  101.8 3.3 %collective-permute-start.6 = (bf16[128,512]{0,1:T(8,128)(2,1)S(1)}, bf16[128,512]{0,1:T(8,128)(2,1)}, u32[]{:S(2)}, u32[]{:S(2)}) collective-permute-start(bf16[128,512]{0,1:T(8,128)(2,1)S(1)} %maximum_select_fusion.6), channel_id=1, source_target_pairs={{0,2},{1,3},{2,0},{3,1},{4,6},{5,7},{6,4},{7,5},{8,10},{9,11},{10,... | collective-permute-start | bytes 393224 | tf_op jit(solution)/shard_map/ppermute | solution.py:23
  105.2 5.0 %collective-permute-done.6 = bf16[128,512]{0,1:T(8,128)(2,1)} collective-permute-done((bf16[128,512]{0,1:T(8,128)(2,1)S(1)}, bf16[128,512]{0,1:T(8,128)(2,1)}, u32[]{:S(2)}, u32[]{:S(2)}) %collective-permute-start.6) | collective-permute-done | bytes 131104 | tf_op jit(solution)/shard_map/ppermute | solution.py:23
  111.4 4.2 %collective-permute-start.7 = (bf16[128,1024]{0,1:T(8,128)(2,1)S(1)}, bf16[128,1024]{0,1:T(8,128)(2,1)}, u32[]{:S(2)}, u32[]{:S(2)}) collective-permute-start(bf16[128,1024]{0,1:T(8,128)(2,1)S(1)} %maximum_select_fusion.5), channel_id=1, source_target_pairs={{0,4},{1,5},{2,6},{3,7},{4,0},{5,1},{6,2},{7,3},{8,12},{9,13},{10,... | collective-permute-start | bytes 786440 | tf_op jit(solution)/shard_map/ppermute | solution.py:23
  115.6 3.7 %fusion.5 = f32[128,2304]{1,0:T(8,128)} fusion(bf16[256,2304]{1,0:T(8,128)(2,1)} %param.22, bf16[1152,256]{1,0:T(8,128)(2,1)} %bitcast.87, f32[128,1152]{0,1:T(8,128)} %copy-done.5, f32[128]{0:T(128)S(1)} %get-tuple-element.4, f32[128]{0:T(128)S(1)} %get-tuple-element.7, s32[128]{0:T(128)S(1)} %get-tuple-element.24, s32[128]{0:T(128)S(1)} %get-tuple-element.18, ...), kind=kOutput, calls=%fused_computation.25 | convolution fusion | flops 227852288 | bytes 3545600 | tf_op jit(solution)/shard_map/dot_general | solution.py:175
  120.0 4.9 %fusion = f32[128,2304]{1,0:T(8,128)} fusion(f32[128,2304]{1,0:T(8,128)} %fusion.5, bf16[576,2304]{1,0:T(8,128)(2,1)S(1)} %copy-done, bf16[576,2048]{1,0:T(8,128)(2,1)} %param.21, f32[128]{0:T(128)S(1)} %select_reduce_fusion.3, bf16[128,1024]{0,1:T(8,128)(2,1)S(1)} %maximum_select_fusion.5, bf16[128,1024]{0,1:T(8,128)(2,1)} %collective-permute-done.7, ...), kind=kOutput, calls=%fused_computation.12 | convolution fusion | flops 644751360 | bytes 7897601 | tf_op jit(solution)/shard_map/dot_general | solution.py:176
  126.2 3.9 %collective-permute-start.8 = (bf16[64,2304]{1,0:T(8,128)(2,1)S(1)}, bf16[64,2304]{1,0:T(8,128)(2,1)S(1)}, u32[]{:S(2)}, u32[]{:S(2)}) collective-permute-start(bf16[64,2304]{1,0:T(8,128)(2,1)S(1)} %select_convert_fusion), channel_id=1, source_target_pairs={{0,4},{1,5},{2,6},{3,7},{4,0},{5,1},{6,2},{7,3},{8,12},{9,13},{10,... | collective-permute-start | bytes 884744 | tf_op jit(solution)/shard_map/ppermute | solution.py:23
  130.2 4.7 %collective-permute-done.8 = bf16[64,2304]{1,0:T(8,128)(2,1)S(1)} collective-permute-done((bf16[64,2304]{1,0:T(8,128)(2,1)S(1)}, bf16[64,2304]{1,0:T(8,128)(2,1)S(1)}, u32[]{:S(2)}, u32[]{:S(2)}) %collective-permute-start.8) | collective-permute-done | bytes 294944 | tf_op jit(solution)/shard_map/ppermute | solution.py:23
  136.2 2.9 %collective-permute-start.9 = (bf16[64,2304]{1,0:T(8,128)(2,1)S(1)}, bf16[64,2304]{1,0:T(8,128)(2,1)S(1)}, u32[]{:S(2)}, u32[]{:S(2)}) collective-permute-start(bf16[64,2304]{1,0:T(8,128)(2,1)S(1)} %get-tuple-element.8), channel_id=1, source_target_pairs={{0,1},{1,0},{2,3},{3,2},{4,5},{5,4},{6,7},{7,6},{8,9},{9,8},{10,11... | collective-permute-start | bytes 884744 | tf_op jit(solution)/shard_map/ppermute | solution.py:23
  139.1 7.3 %collective-permute-done.9 = bf16[64,2304]{1,0:T(8,128)(2,1)S(1)} collective-permute-done((bf16[64,2304]{1,0:T(8,128)(2,1)S(1)}, bf16[64,2304]{1,0:T(8,128)(2,1)S(1)}, u32[]{:S(2)}, u32[]{:S(2)}) %collective-permute-start.9) | collective-permute-done | bytes 294944 | tf_op jit(solution)/shard_map/ppermute | solution.py:23
  148.3 8.2 %collective-permute-done.10 = bf16[64,2304]{1,0:T(8,128)(2,1)S(1)} collective-permute-done((bf16[64,2304]{1,0:T(8,128)(2,1)S(1)}, bf16[64,2304]{1,0:T(8,128)(2,1)S(1)}, u32[]{:S(2)}, u32[]{:S(2)}) %collective-permute-start.10) | collective-permute-done | bytes 294944 | tf_op jit(solution)/shard_map/ppermute | solution.py:23
  156.6 4.3 %collective-permute-start.11 = (bf16[64,2304]{1,0:T(8,128)(2,1)S(1)}, bf16[64,2304]{1,0:T(8,128)(2,1)S(1)}, u32[]{:S(2)}, u32[]{:S(2)}) collective-permute-start(bf16[64,2304]{1,0:T(8,128)(2,1)S(1)} %add_convert_fusion), channel_id=1, source_target_pairs={{0,4},{1,5},{2,6},{3,7},{4,0},{5,1},{6,2},{7,3},{8,12},{9,13},{10,... | collective-permute-start | bytes 884744 | tf_op jit(solution)/shard_map/ppermute | solution.py:23
  161.0 4.7 %collective-permute-done.11 = bf16[64,2304]{1,0:T(8,128)(2,1)S(1)} collective-permute-done((bf16[64,2304]{1,0:T(8,128)(2,1)S(1)}, bf16[64,2304]{1,0:T(8,128)(2,1)S(1)}, u32[]{:S(2)}, u32[]{:S(2)}) %collective-permute-start.11) | collective-permute-done | bytes 294944 | tf_op jit(solution)/shard_map/ppermute | solution.py:23
  179.2 5.5 %collective-permute-done.13 = bf16[256,256]{1,0:T(8,128)(2,1)S(1)} collective-permute-done((bf16[256,256]{1,0:T(8,128)(2,1)S(1)}, bf16[256,256]{1,0:T(8,128)(2,1)S(1)}, u32[]{:S(2)}, u32[]{:S(2)}) %collective-permute-start.13) | collective-permute-done | bytes 131104 | tf_op jit(solution)/shard_map/ppermute | solution.py:18
  184.8 9.6 %collective-permute-start.14 = (bf16[256,256]{1,0:T(8,128)(2,1)S(1)}, bf16[256,256]{1,0:T(8,128)(2,1)S(1)}, u32[]{:S(2)}, u32[]{:S(2)}) collective-permute-start(bf16[256,256]{1,0:T(8,128)(2,1)S(1)} %fusion.54), channel_id=1, source_target_pairs={{16,0},{24,8},{32,16},{40,24},{48,32},{56,40},{64,48},{72,56},{80,... | collective-permute-start | bytes 393224 | tf_op jit(solution)/shard_map/ppermute | solution.py:18
  196.9 10.5 %collective-permute-start.15 = (bf16[256,256]{1,0:T(8,128)(2,1)S(1)}, bf16[256,256]{1,0:T(8,128)(2,1)S(1)}, u32[]{:S(2)}, u32[]{:S(2)}) collective-permute-start(bf16[256,256]{1,0:T(8,128)(2,1)S(1)} %fusion.55), channel_id=1, source_target_pairs={{16,0},{24,8},{32,16},{40,24},{48,32},{56,40},{64,48},{72,56},{80,... | collective-permute-start | bytes 393224 | tf_op jit(solution)/shard_map/ppermute | solution.py:18
  210.0 9.5 %collective-permute-start.16 = (bf16[256,256]{1,0:T(8,128)(2,1)S(1)}, bf16[256,256]{1,0:T(8,128)(2,1)S(1)}, u32[]{:S(2)}, u32[]{:S(2)}) collective-permute-start(bf16[256,256]{1,0:T(8,128)(2,1)S(1)} %fusion.56), channel_id=1, source_target_pairs={{16,0},{24,8},{32,16},{40,24},{48,32},{56,40},{64,48},{72,56},{80,... | collective-permute-start | bytes 393224 | tf_op jit(solution)/shard_map/ppermute | solution.py:18
  (102 shorter events, 52.4 us)
Async XLA Ops:
  0.6 119.4 %copy-start = (bf16[576,2304]{1,0:T(8,128)(2,1)S(1)}, bf16[576,2304]{1,0:T(8,128)(2,1)}, u32[]{:S(2)}) copy-start(bf16[576,2304]{1,0:T(8,128)(2,1)} %param.23) | copy-start | bytes 7962628
  4.9 31.0 %collective-permute-start = (bf16[520,256]{1,0:T(8,128)(2,1)S(1)}, bf16[520,256]{1,0:T(8,128)(2,1)S(1)}, u32[]{:S(2)}, u32[]{:S(2)}) collective-permute-start(bf16[520,256]{1,0:T(8,128)(2,1)S(1)} %constant_dynamic-update-slice_fusion), channel_id=1, source_target_pairs={{0,16},{8,24},{16,32},{24,40},{32,48},{40,56},{48,64},{56,72},{64,... | collective-permute-start | bytes 798728 | tf_op jit(solution)/shard_map/ppermute | solution.py:18
  35.9 17.9 %collective-permute-start.1 = (bf16[520,256]{1,0:T(8,128)(2,1)S(1)}, bf16[520,256]{1,0:T(8,128)(2,1)S(1)}, u32[]{:S(2)}, u32[]{:S(2)}) collective-permute-start(bf16[520,256]{1,0:T(8,128)(2,1)S(1)} %collective-permute-done), channel_id=1, source_target_pairs={{0,16},{8,24},{16,32},{24,40},{32,48},{40,56},{48,64},{56,72},{64,... | collective-permute-start | bytes 798728 | tf_op jit(solution)/shard_map/ppermute | solution.py:18
  53.8 14.9 %collective-permute-start.2 = (bf16[520,256]{1,0:T(8,128)(2,1)S(1)}, bf16[520,256]{1,0:T(8,128)(2,1)}, u32[]{:S(2)}, u32[]{:S(2)}) collective-permute-start(bf16[520,256]{1,0:T(8,128)(2,1)S(1)} %collective-permute-done.1), channel_id=1, source_target_pairs={{0,16},{8,24},{16,32},{24,40},{32,48},{40,56},{48,64},{56,72},{64,... | collective-permute-start | bytes 798728 | tf_op jit(solution)/shard_map/ppermute | solution.py:18
  68.7 13.9 %collective-permute-start.3 = (bf16[520,256]{1,0:T(8,128)(2,1)}, bf16[520,256]{1,0:T(8,128)(2,1)S(1)}, u32[]{:S(2)}, u32[]{:S(2)}) collective-permute-start(bf16[520,256]{1,0:T(8,128)(2,1)} %collective-permute-done.2), channel_id=1, source_target_pairs={{0,16},{8,24},{16,32},{24,40},{32,48},{40,56},{48,64},{56,72},{64,... | collective-permute-start | bytes 798728 | tf_op jit(solution)/shard_map/ppermute | solution.py:18
  84.6 4.6 %collective-permute-start.4 = (bf16[4,520,256]{2,1,0:T(8,128)(2,1)S(1)}, bf16[4,520,256]{2,1,0:T(8,128)(2,1)S(1)}, u32[]{:S(2)}, u32[]{:S(2)}) collective-permute-start(bf16[4,520,256]{2,1,0:T(8,128)(2,1)S(1)} %constant_dynamic-slice_fusion), channel_id=1, source_target_pairs={{0,8},{8,0},{16,24},{24,16},{32,40},{40,32},{48,56},{56,48},{64,72... | collective-permute-start | bytes 3194888 | tf_op jit(solution)/shard_map/ppermute | solution.py:23
  92.6 74.1 %copy-start.11 = (f32[128]{0:T(128)}, f32[128]{0:T(128)S(1)}, u32[]{:S(2)}) copy-start(f32[128]{0:T(128)S(1)} %get-tuple-element.7) | copy-start | bytes 1540
  93.1 73.5 %copy-start.12 = (f32[128]{0:T(128)}, f32[128]{0:T(128)S(1)}, u32[]{:S(2)}) copy-start(f32[128]{0:T(128)S(1)} %get-tuple-element.4) | copy-start | bytes 1540
  94.0 11.2 %copy-start.15 = (f32[16]{0:T(128)S(1)}, f32[16]{0:T(128)}, u32[]{:S(2)}) copy-start(f32[16]{0:T(128)} %param.20) | copy-start | bytes 196
  94.0 11.2 %copy-start.16 = (s32[128]{0:T(128)S(1)}, s32[128]{0:T(128)}, u32[]{:S(2)}) copy-start(s32[128]{0:T(128)} %param.19) | copy-start | bytes 1540
  94.5 6.3 %collective-permute-start.5 = (bf16[128,256]{0,1:T(8,128)(2,1)S(1)}, bf16[128,256]{0,1:T(8,128)(2,1)}, u32[]{:S(2)}, u32[]{:S(2)}) collective-permute-start(bf16[128,256]{0,1:T(8,128)(2,1)S(1)} %pad_maximum_fusion.1), channel_id=1, source_target_pairs={{0,1},{1,0},{2,3},{3,2},{4,5},{5,4},{6,7},{7,6},{8,9},{9,8},{10,11... | collective-permute-start | bytes 196616 | tf_op jit(solution)/shard_map/ppermute | solution.py:23
  101.8 8.5 %collective-permute-start.6 = (bf16[128,512]{0,1:T(8,128)(2,1)S(1)}, bf16[128,512]{0,1:T(8,128)(2,1)}, u32[]{:S(2)}, u32[]{:S(2)}) collective-permute-start(bf16[128,512]{0,1:T(8,128)(2,1)S(1)} %maximum_select_fusion.6), channel_id=1, source_target_pairs={{0,2},{1,3},{2,0},{3,1},{4,6},{5,7},{6,4},{7,5},{8,10},{9,11},{10,... | collective-permute-start | bytes 393224 | tf_op jit(solution)/shard_map/ppermute | solution.py:23
  111.4 8.6 %collective-permute-start.7 = (bf16[128,1024]{0,1:T(8,128)(2,1)S(1)}, bf16[128,1024]{0,1:T(8,128)(2,1)}, u32[]{:S(2)}, u32[]{:S(2)}) collective-permute-start(bf16[128,1024]{0,1:T(8,128)(2,1)S(1)} %maximum_select_fusion.5), channel_id=1, source_target_pairs={{0,4},{1,5},{2,6},{3,7},{4,0},{5,1},{6,2},{7,3},{8,12},{9,13},{10,... | collective-permute-start | bytes 786440 | tf_op jit(solution)/shard_map/ppermute | solution.py:23
  126.2 8.6 %collective-permute-start.8 = (bf16[64,2304]{1,0:T(8,128)(2,1)S(1)}, bf16[64,2304]{1,0:T(8,128)(2,1)S(1)}, u32[]{:S(2)}, u32[]{:S(2)}) collective-permute-start(bf16[64,2304]{1,0:T(8,128)(2,1)S(1)} %select_convert_fusion), channel_id=1, source_target_pairs={{0,4},{1,5},{2,6},{3,7},{4,0},{5,1},{6,2},{7,3},{8,12},{9,13},{10,... | collective-permute-start | bytes 884744 | tf_op jit(solution)/shard_map/ppermute | solution.py:23
  136.2 29.5 %copy-start.13 = (bf16[256,2304]{1,0:T(8,128)(2,1)S(1)}, bf16[256,2304]{1,0:T(8,128)(2,1)}, u32[]{:S(2)}) copy-start(bf16[256,2304]{1,0:T(8,128)(2,1)} %param.22) | copy-start | bytes 3538948
  136.2 10.2 %collective-permute-start.9 = (bf16[64,2304]{1,0:T(8,128)(2,1)S(1)}, bf16[64,2304]{1,0:T(8,128)(2,1)S(1)}, u32[]{:S(2)}, u32[]{:S(2)}) collective-permute-start(bf16[64,2304]{1,0:T(8,128)(2,1)S(1)} %get-tuple-element.8), channel_id=1, source_target_pairs={{0,1},{1,0},{2,3},{3,2},{4,5},{5,4},{6,7},{7,6},{8,9},{9,8},{10,11... | collective-permute-start | bytes 884744 | tf_op jit(solution)/shard_map/ppermute | solution.py:23
  146.4 10.1 %collective-permute-start.10 = (bf16[64,2304]{1,0:T(8,128)(2,1)S(1)}, bf16[64,2304]{1,0:T(8,128)(2,1)S(1)}, u32[]{:S(2)}, u32[]{:S(2)}) collective-permute-start(bf16[64,2304]{1,0:T(8,128)(2,1)S(1)} %fusion.30), channel_id=1, source_target_pairs={{0,2},{1,3},{2,0},{3,1},{4,6},{5,7},{6,4},{7,5},{8,10},{9,11},{10,... | collective-permute-start | bytes 884744 | tf_op jit(solution)/shard_map/ppermute | solution.py:23
  156.6 9.6 %copy-start.6 = (f32[128,1152]{0,1:T(8,128)S(1)}, f32[128,1152]{0,1:T(8,128)}, u32[]{:S(2)}) copy-start(f32[128,1152]{0,1:T(8,128)} %copy-done.5) | copy-start | bytes 1769476
  156.6 9.0 %collective-permute-start.11 = (bf16[64,2304]{1,0:T(8,128)(2,1)S(1)}, bf16[64,2304]{1,0:T(8,128)(2,1)S(1)}, u32[]{:S(2)}, u32[]{:S(2)}) collective-permute-start(bf16[64,2304]{1,0:T(8,128)(2,1)S(1)} %add_convert_fusion), channel_id=1, source_target_pairs={{0,4},{1,5},{2,6},{3,7},{4,0},{5,1},{6,2},{7,3},{8,12},{9,13},{10,... | collective-permute-start | bytes 884744 | tf_op jit(solution)/shard_map/ppermute | solution.py:23
  170.9 4.1 %collective-permute-start.12 = (bf16[4,256,256]{2,1,0:T(8,128)(2,1)}, bf16[4,256,256]{2,1,0:T(8,128)(2,1)}, u32[]{:S(2)}, u32[]{:S(2)}) collective-permute-start(bf16[4,256,256]{2,1,0:T(8,128)(2,1)} %slice.116), channel_id=1, source_target_pairs={{0,8},{8,0},{16,24},{24,16},{32,40},{40,32},{48,56},{56,48},{64,72... | collective-permute-start | bytes 1572872 | tf_op jit(solution)/shard_map/ppermute | solution.py:23
  177.3 7.4 %collective-permute-start.13 = (bf16[256,256]{1,0:T(8,128)(2,1)S(1)}, bf16[256,256]{1,0:T(8,128)(2,1)S(1)}, u32[]{:S(2)}, u32[]{:S(2)}) collective-permute-start(bf16[256,256]{1,0:T(8,128)(2,1)S(1)} %fusion.61), channel_id=1, source_target_pairs={{16,0},{24,8},{32,16},{40,24},{48,32},{56,40},{64,48},{72,56},{80,... | collective-permute-start | bytes 393224 | tf_op jit(solution)/shard_map/ppermute | solution.py:18
  184.8 12.1 %collective-permute-start.14 = (bf16[256,256]{1,0:T(8,128)(2,1)S(1)}, bf16[256,256]{1,0:T(8,128)(2,1)S(1)}, u32[]{:S(2)}, u32[]{:S(2)}) collective-permute-start(bf16[256,256]{1,0:T(8,128)(2,1)S(1)} %fusion.54), channel_id=1, source_target_pairs={{16,0},{24,8},{32,16},{40,24},{48,32},{56,40},{64,48},{72,56},{80,... | collective-permute-start | bytes 393224 | tf_op jit(solution)/shard_map/ppermute | solution.py:18
  196.9 13.0 %collective-permute-start.15 = (bf16[256,256]{1,0:T(8,128)(2,1)S(1)}, bf16[256,256]{1,0:T(8,128)(2,1)S(1)}, u32[]{:S(2)}, u32[]{:S(2)}) collective-permute-start(bf16[256,256]{1,0:T(8,128)(2,1)S(1)} %fusion.55), channel_id=1, source_target_pairs={{16,0},{24,8},{32,16},{40,24},{48,32},{56,40},{64,48},{72,56},{80,... | collective-permute-start | bytes 393224 | tf_op jit(solution)/shard_map/ppermute | solution.py:18
  210.0 12.1 %collective-permute-start.16 = (bf16[256,256]{1,0:T(8,128)(2,1)S(1)}, bf16[256,256]{1,0:T(8,128)(2,1)S(1)}, u32[]{:S(2)}, u32[]{:S(2)}) collective-permute-start(bf16[256,256]{1,0:T(8,128)(2,1)S(1)} %fusion.56), channel_id=1, source_target_pairs={{16,0},{24,8},{32,16},{40,24},{48,32},{56,40},{64,48},{72,56},{80,... | collective-permute-start | bytes 393224 | tf_op jit(solution)/shard_map/ppermute | solution.py:18
  (10 other events, 23.6 us)

commit v11 on v9

--- a/solution.py
+++ b/solution.py
@@ -130,7 +130,10 @@
     student_scale = DH_S ** (-0.5)
     doc_marks = segment_ids + 1
     mark_rows = jnp.pad(doc_marks.astype(jnp.bfloat16), (0, 8 * width - rows)).reshape(8, width)
-    own = jnp.concatenate([teacher_key, teacher_value, student_key, student_value, mark_rows], 0)
+    own = jnp.concatenate(
+        [jnp.stack([teacher_key, teacher_value, student_key, student_value]).reshape(4 * rows, width), mark_rows],
+        0,
+    )
     chain = [own]
     for _ in range(steps):
         chain.append(shifted(chain[-1], "seq", 2))

time: 223 us -> 221 us (level)
  local copies, waits for them, and re-layouts: 15 us -> 10.9 us
    unnamed x47 -> x42, local copies, waits for them, and re-layouts: 10.3 us -> 6.24 us
where the time goes in v11:
time: 221 us; the launch traced here: 219 us
  waiting for transfers between devices  113 us (51%)
  starting transfers between devices  68.7 us (31%)
  matrix products  13.4 us (6%)
  other arithmetic  12.2 us (6%)
  local copies, waits for them, and re-layouts  10.9 us (5%)
    ppermute x8, waiting for transfers between devices, shifted(): return lax.ppermute(value, axis, pairs)  75.9 us
    ppermute x8, starting transfers between devices, shifted(): return lax.ppermute(value, axis, pairs)  41.6 us
    ppermute x9, waiting for transfers between devices, swapped(): return lax.ppermute(value, axis, [(i, i ^ bit) for i in range(length)])  37.1 us
    ppermute x9, starting transfers between devices, swapped(): return lax.ppermute(value, axis, [(i, i ^ bit) for i in range(length)])  27.1 us
    unnamed x42, local copies, waits for them, and re-layouts  6.24 us
    dot_general x1, matrix products, shards(): jnp.dot(target_cols, match_proj, preferred_element_type=jnp.float32)  4.88 us
  transfers between devices with their start and end apart: 17, of which 17 were waited for; matrix products, arithmetic and copies ran while one was open for 5% of the time, Pallas kernels for 0%

profile of v11, /device:TPU:46, one launch (start us, length us, event | category | flops | bytes accessed | tf_op | source)
XLA Modules:
  0.0 219.5 jit_solution(15495217431191264988)
XLA Ops:
  2.5 4.3 %collective-permute-start = (bf16[520,256]{1,0:T(8,128)(2,1)S(1)}, bf16[520,256]{1,0:T(8,128)(2,1)S(1)}, u32[]{:S(2)}, u32[]{:S(2)}) collective-permute-start(bf16[520,256]{1,0:T(8,128)(2,1)S(1)} %pad_maximum_fusion.1), channel_id=1, source_target_pairs={{0,16},{8,24},{16,32},{24,40},{32,48},{40,56},{48,64},{56,72},{64,... | collective-permute-start | bytes 798728 | tf_op jit(solution)/shard_map/ppermute | solution.py:18
  6.8 26.8 %collective-permute-done = bf16[520,256]{1,0:T(8,128)(2,1)S(1)} collective-permute-done((bf16[520,256]{1,0:T(8,128)(2,1)S(1)}, bf16[520,256]{1,0:T(8,128)(2,1)S(1)}, u32[]{:S(2)}, u32[]{:S(2)}) %collective-permute-start) | collective-permute-done | bytes 266272 | tf_op jit(solution)/shard_map/ppermute | solution.py:18
  35.4 15.9 %collective-permute-done.1 = bf16[520,256]{1,0:T(8,128)(2,1)S(1)} collective-permute-done((bf16[520,256]{1,0:T(8,128)(2,1)S(1)}, bf16[520,256]{1,0:T(8,128)(2,1)S(1)}, u32[]{:S(2)}, u32[]{:S(2)}) %collective-permute-start.1) | collective-permute-done | bytes 266272 | tf_op jit(solution)/shard_map/ppermute | solution.py:18
  54.7 11.6 %collective-permute-done.2 = bf16[520,256]{1,0:T(8,128)(2,1)} collective-permute-done((bf16[520,256]{1,0:T(8,128)(2,1)S(1)}, bf16[520,256]{1,0:T(8,128)(2,1)}, u32[]{:S(2)}, u32[]{:S(2)}) %collective-permute-start.2) | collective-permute-done | bytes 266272 | tf_op jit(solution)/shard_map/ppermute | solution.py:18
  70.6 9.5 %collective-permute-done.3 = bf16[520,256]{1,0:T(8,128)(2,1)S(1)} collective-permute-done((bf16[520,256]{1,0:T(8,128)(2,1)}, bf16[520,256]{1,0:T(8,128)(2,1)S(1)}, u32[]{:S(2)}, u32[]{:S(2)}) %collective-permute-start.3) | collective-permute-done | bytes 266272 | tf_op jit(solution)/shard_map/ppermute | solution.py:18
  84.2 2.6 %collective-permute-done.4 = bf16[4,520,256]{2,1,0:T(8,128)(2,1)S(1)} collective-permute-done((bf16[4,520,256]{2,1,0:T(8,128)(2,1)S(1)}, bf16[4,520,256]{2,1,0:T(8,128)(2,1)S(1)}, u32[]{:S(2)}, u32[]{:S(2)}) %collective-permute-start.4) | collective-permute-done | bytes 1064992 | tf_op jit(solution)/shard_map/ppermute | solution.py:23
  92.1 2.7 %collective-permute-start.5 = (bf16[128,256]{0,1:T(8,128)(2,1)S(1)}, bf16[128,256]{0,1:T(8,128)(2,1)}, u32[]{:S(2)}, u32[]{:S(2)}) collective-permute-start(bf16[128,256]{0,1:T(8,128)(2,1)S(1)} %pad_maximum_fusion.3), channel_id=1, source_target_pairs={{0,1},{1,0},{2,3},{3,2},{4,5},{5,4},{6,7},{7,6},{8,9},{9,8},{10,11... | collective-permute-start | bytes 196616 | tf_op jit(solution)/shard_map/ppermute | solution.py:23
  94.9 3.5 %collective-permute-done.5 = bf16[128,256]{0,1:T(8,128)(2,1)} collective-permute-done((bf16[128,256]{0,1:T(8,128)(2,1)S(1)}, bf16[128,256]{0,1:T(8,128)(2,1)}, u32[]{:S(2)}, u32[]{:S(2)}) %collective-permute-start.5) | collective-permute-done | bytes 65568 | tf_op jit(solution)/shard_map/ppermute | solution.py:23
  99.4 3.3 %collective-permute-start.6 = (bf16[128,512]{0,1:T(8,128)(2,1)S(1)}, bf16[128,512]{0,1:T(8,128)(2,1)}, u32[]{:S(2)}, u32[]{:S(2)}) collective-permute-start(bf16[128,512]{0,1:T(8,128)(2,1)S(1)} %maximum_select_fusion.6), channel_id=1, source_target_pairs={{0,2},{1,3},{2,0},{3,1},{4,6},{5,7},{6,4},{7,5},{8,10},{9,11},{10,... | collective-permute-start | bytes 393224 | tf_op jit(solution)/shard_map/ppermute | solution.py:23
  102.8 5.0 %collective-permute-done.6 = bf16[128,512]{0,1:T(8,128)(2,1)} collective-permute-done((bf16[128,512]{0,1:T(8,128)(2,1)S(1)}, bf16[128,512]{0,1:T(8,128)(2,1)}, u32[]{:S(2)}, u32[]{:S(2)}) %collective-permute-start.6) | collective-permute-done | bytes 131104 | tf_op jit(solution)/shard_map/ppermute | solution.py:23
  109.0 4.2 %collective-permute-start.7 = (bf16[128,1024]{0,1:T(8,128)(2,1)S(1)}, bf16[128,1024]{0,1:T(8,128)(2,1)}, u32[]{:S(2)}, u32[]{:S(2)}) collective-permute-start(bf16[128,1024]{0,1:T(8,128)(2,1)S(1)} %maximum_select_fusion.5), channel_id=1, source_target_pairs={{0,4},{1,5},{2,6},{3,7},{4,0},{5,1},{6,2},{7,3},{8,12},{9,13},{10,... | collective-permute-start | bytes 786440 | tf_op jit(solution)/shard_map/ppermute | solution.py:23
  113.2 3.6 %fusion.4 = f32[128,2304]{1,0:T(8,128)} fusion(bf16[256,2304]{1,0:T(8,128)(2,1)} %param.22, bf16[1152,256]{1,0:T(8,128)(2,1)} %bitcast.87, f32[128,1152]{0,1:T(8,128)} %copy-done.3, f32[128]{0:T(128)S(1)} %get-tuple-element.4, f32[128]{0:T(128)S(1)} %get-tuple-element.7, s32[128]{0:T(128)S(1)} %get-tuple-element.24, s32[128]{0:T(128)S(1)} %get-tuple-element.18, ...), kind=kOutput, calls=%fused_computation.15 | convolution fusion | flops 227852288 | bytes 3545600 | tf_op jit(solution)/shard_map/dot_general | solution.py:178
  117.6 4.9 %fusion = f32[128,2304]{1,0:T(8,128)} fusion(f32[128,2304]{1,0:T(8,128)} %fusion.4, bf16[576,2304]{1,0:T(8,128)(2,1)S(1)} %copy-done, bf16[576,2048]{1,0:T(8,128)(2,1)} %param.21, f32[128]{0:T(128)S(1)} %select_reduce_fusion.3, bf16[128,1024]{0,1:T(8,128)(2,1)S(1)} %maximum_select_fusion.5, bf16[128,1024]{0,1:T(8,128)(2,1)} %collective-permute-done.7, ...), kind=kOutput, calls=%fused_computation.1 | convolution fusion | flops 644751360 | bytes 7897601 | tf_op jit(solution)/shard_map/dot_general | solution.py:179
  123.8 3.9 %collective-permute-start.8 = (bf16[64,2304]{1,0:T(8,128)(2,1)S(1)}, bf16[64,2304]{1,0:T(8,128)(2,1)S(1)}, u32[]{:S(2)}, u32[]{:S(2)}) collective-permute-start(bf16[64,2304]{1,0:T(8,128)(2,1)S(1)} %select_convert_fusion), channel_id=1, source_target_pairs={{0,4},{1,5},{2,6},{3,7},{4,0},{5,1},{6,2},{7,3},{8,12},{9,13},{10,... | collective-permute-start | bytes 884744 | tf_op jit(solution)/shard_map/ppermute | solution.py:23
  127.8 4.7 %collective-permute-done.8 = bf16[64,2304]{1,0:T(8,128)(2,1)S(1)} collective-permute-done((bf16[64,2304]{1,0:T(8,128)(2,1)S(1)}, bf16[64,2304]{1,0:T(8,128)(2,1)S(1)}, u32[]{:S(2)}, u32[]{:S(2)}) %collective-permute-start.8) | collective-permute-done | bytes 294944 | tf_op jit(solution)/shard_map/ppermute | solution.py:23
  133.8 2.9 %collective-permute-start.9 = (bf16[64,2304]{1,0:T(8,128)(2,1)S(1)}, bf16[64,2304]{1,0:T(8,128)(2,1)S(1)}, u32[]{:S(2)}, u32[]{:S(2)}) collective-permute-start(bf16[64,2304]{1,0:T(8,128)(2,1)S(1)} %get-tuple-element.8), channel_id=1, source_target_pairs={{0,1},{1,0},{2,3},{3,2},{4,5},{5,4},{6,7},{7,6},{8,9},{9,8},{10,11... | collective-permute-start | bytes 884744 | tf_op jit(solution)/shard_map/ppermute | solution.py:23
  136.7 7.3 %collective-permute-done.9 = bf16[64,2304]{1,0:T(8,128)(2,1)S(1)} collective-permute-done((bf16[64,2304]{1,0:T(8,128)(2,1)S(1)}, bf16[64,2304]{1,0:T(8,128)(2,1)S(1)}, u32[]{:S(2)}, u32[]{:S(2)}) %collective-permute-start.9) | collective-permute-done | bytes 294944 | tf_op jit(solution)/shard_map/ppermute | solution.py:23
  145.9 8.2 %collective-permute-done.10 = bf16[64,2304]{1,0:T(8,128)(2,1)S(1)} collective-permute-done((bf16[64,2304]{1,0:T(8,128)(2,1)S(1)}, bf16[64,2304]{1,0:T(8,128)(2,1)S(1)}, u32[]{:S(2)}, u32[]{:S(2)}) %collective-permute-start.10) | collective-permute-done | bytes 294944 | tf_op jit(solution)/shard_map/ppermute | solution.py:23
  154.2 4.3 %collective-permute-start.11 = (bf16[64,2304]{1,0:T(8,128)(2,1)S(1)}, bf16[64,2304]{1,0:T(8,128)(2,1)S(1)}, u32[]{:S(2)}, u32[]{:S(2)}) collective-permute-start(bf16[64,2304]{1,0:T(8,128)(2,1)S(1)} %add_convert_fusion), channel_id=1, source_target_pairs={{0,4},{1,5},{2,6},{3,7},{4,0},{5,1},{6,2},{7,3},{8,12},{9,13},{10,... | collective-permute-start | bytes 884744 | tf_op jit(solution)/shard_map/ppermute | solution.py:23
  158.6 4.7 %collective-permute-done.11 = bf16[64,2304]{1,0:T(8,128)(2,1)S(1)} collective-permute-done((bf16[64,2304]{1,0:T(8,128)(2,1)S(1)}, bf16[64,2304]{1,0:T(8,128)(2,1)S(1)}, u32[]{:S(2)}, u32[]{:S(2)}) %collective-permute-start.11) | collective-permute-done | bytes 294944 | tf_op jit(solution)/shard_map/ppermute | solution.py:23
  175.9 5.5 %collective-permute-done.13 = bf16[256,256]{1,0:T(8,128)(2,1)S(1)} collective-permute-done((bf16[256,256]{1,0:T(8,128)(2,1)S(1)}, bf16[256,256]{1,0:T(8,128)(2,1)S(1)}, u32[]{:S(2)}, u32[]{:S(2)}) %collective-permute-start.13) | collective-permute-done | bytes 131104 | tf_op jit(solution)/shard_map/ppermute | solution.py:18
  181.5 9.5 %collective-permute-start.14 = (bf16[256,256]{1,0:T(8,128)(2,1)S(1)}, bf16[256,256]{1,0:T(8,128)(2,1)S(1)}, u32[]{:S(2)}, u32[]{:S(2)}) collective-permute-start(bf16[256,256]{1,0:T(8,128)(2,1)S(1)} %fusion.35), channel_id=1, source_target_pairs={{16,0},{24,8},{32,16},{40,24},{48,32},{56,40},{64,48},{72,56},{80,... | collective-permute-start | bytes 393224 | tf_op jit(solution)/shard_map/ppermute | solution.py:18
  193.6 10.6 %collective-permute-start.15 = (bf16[256,256]{1,0:T(8,128)(2,1)S(1)}, bf16[256,256]{1,0:T(8,128)(2,1)S(1)}, u32[]{:S(2)}, u32[]{:S(2)}) collective-permute-start(bf16[256,256]{1,0:T(8,128)(2,1)S(1)} %fusion.37), channel_id=1, source_target_pairs={{16,0},{24,8},{32,16},{40,24},{48,32},{56,40},{64,48},{72,56},{80,... | collective-permute-start | bytes 393224 | tf_op jit(solution)/shard_map/ppermute | solution.py:18
  206.7 9.5 %collective-permute-start.16 = (bf16[256,256]{1,0:T(8,128)(2,1)S(1)}, bf16[256,256]{1,0:T(8,128)(2,1)S(1)}, u32[]{:S(2)}, u32[]{:S(2)}) collective-permute-start(bf16[256,256]{1,0:T(8,128)(2,1)S(1)} %fusion.39), channel_id=1, source_target_pairs={{16,0},{24,8},{32,16},{40,24},{48,32},{56,40},{64,48},{72,56},{80,... | collective-permute-start | bytes 393224 | tf_op jit(solution)/shard_map/ppermute | solution.py:18
  (97 shorter events, 49.1 us)
Async XLA Ops:
  0.6 117.0 %copy-start = (bf16[576,2304]{1,0:T(8,128)(2,1)S(1)}, bf16[576,2304]{1,0:T(8,128)(2,1)}, u32[]{:S(2)}) copy-start(bf16[576,2304]{1,0:T(8,128)(2,1)} %param.23) | copy-start | bytes 7962628
  2.5 31.0 %collective-permute-start = (bf16[520,256]{1,0:T(8,128)(2,1)S(1)}, bf16[520,256]{1,0:T(8,128)(2,1)S(1)}, u32[]{:S(2)}, u32[]{:S(2)}) collective-permute-start(bf16[520,256]{1,0:T(8,128)(2,1)S(1)} %pad_maximum_fusion.1), channel_id=1, source_target_pairs={{0,16},{8,24},{16,32},{24,40},{32,48},{40,56},{48,64},{56,72},{64,... | collective-permute-start | bytes 798728 | tf_op jit(solution)/shard_map/ppermute | solution.py:18
  33.5 17.9 %collective-permute-start.1 = (bf16[520,256]{1,0:T(8,128)(2,1)S(1)}, bf16[520,256]{1,0:T(8,128)(2,1)S(1)}, u32[]{:S(2)}, u32[]{:S(2)}) collective-permute-start(bf16[520,256]{1,0:T(8,128)(2,1)S(1)} %collective-permute-done), channel_id=1, source_target_pairs={{0,16},{8,24},{16,32},{24,40},{32,48},{40,56},{48,64},{56,72},{64,... | collective-permute-start | bytes 798728 | tf_op jit(solution)/shard_map/ppermute | solution.py:18
  51.4 14.9 %collective-permute-start.2 = (bf16[520,256]{1,0:T(8,128)(2,1)S(1)}, bf16[520,256]{1,0:T(8,128)(2,1)}, u32[]{:S(2)}, u32[]{:S(2)}) collective-permute-start(bf16[520,256]{1,0:T(8,128)(2,1)S(1)} %collective-permute-done.1), channel_id=1, source_target_pairs={{0,16},{8,24},{16,32},{24,40},{32,48},{40,56},{48,64},{56,72},{64,... | collective-permute-start | bytes 798728 | tf_op jit(solution)/shard_map/ppermute | solution.py:18
  66.3 13.9 %collective-permute-start.3 = (bf16[520,256]{1,0:T(8,128)(2,1)}, bf16[520,256]{1,0:T(8,128)(2,1)S(1)}, u32[]{:S(2)}, u32[]{:S(2)}) collective-permute-start(bf16[520,256]{1,0:T(8,128)(2,1)} %collective-permute-done.2), channel_id=1, source_target_pairs={{0,16},{8,24},{16,32},{24,40},{32,48},{40,56},{48,64},{56,72},{64,... | collective-permute-start | bytes 798728 | tf_op jit(solution)/shard_map/ppermute | solution.py:18
  82.2 4.6 %collective-permute-start.4 = (bf16[4,520,256]{2,1,0:T(8,128)(2,1)S(1)}, bf16[4,520,256]{2,1,0:T(8,128)(2,1)S(1)}, u32[]{:S(2)}, u32[]{:S(2)}) collective-permute-start(bf16[4,520,256]{2,1,0:T(8,128)(2,1)S(1)} %constant_dynamic-slice_fusion), channel_id=1, source_target_pairs={{0,8},{8,0},{16,24},{24,16},{32,40},{40,32},{48,56},{56,48},{64,72... | collective-permute-start | bytes 3194888 | tf_op jit(solution)/shard_map/ppermute | solution.py:23
  90.2 74.0 %copy-start.9 = (f32[128]{0:T(128)}, f32[128]{0:T(128)S(1)}, u32[]{:S(2)}) copy-start(f32[128]{0:T(128)S(1)} %get-tuple-element.7) | copy-start | bytes 1540
  90.7 73.5 %copy-start.10 = (f32[128]{0:T(128)}, f32[128]{0:T(128)S(1)}, u32[]{:S(2)}) copy-start(f32[128]{0:T(128)S(1)} %get-tuple-element.4) | copy-start | bytes 1540
  91.6 11.2 %copy-start.13 = (f32[16]{0:T(128)S(1)}, f32[16]{0:T(128)}, u32[]{:S(2)}) copy-start(f32[16]{0:T(128)} %param.20) | copy-start | bytes 196
  91.6 11.2 %copy-start.14 = (s32[128]{0:T(128)S(1)}, s32[128]{0:T(128)}, u32[]{:S(2)}) copy-start(s32[128]{0:T(128)} %param.19) | copy-start | bytes 1540
  92.1 6.3 %collective-permute-start.5 = (bf16[128,256]{0,1:T(8,128)(2,1)S(1)}, bf16[128,256]{0,1:T(8,128)(2,1)}, u32[]{:S(2)}, u32[]{:S(2)}) collective-permute-start(bf16[128,256]{0,1:T(8,128)(2,1)S(1)} %pad_maximum_fusion.3), channel_id=1, source_target_pairs={{0,1},{1,0},{2,3},{3,2},{4,5},{5,4},{6,7},{7,6},{8,9},{9,8},{10,11... | collective-permute-start | bytes 196616 | tf_op jit(solution)/shard_map/ppermute | solution.py:23
  99.4 8.5 %collective-permute-start.6 = (bf16[128,512]{0,1:T(8,128)(2,1)S(1)}, bf16[128,512]{0,1:T(8,128)(2,1)}, u32[]{:S(2)}, u32[]{:S(2)}) collective-permute-start(bf16[128,512]{0,1:T(8,128)(2,1)S(1)} %maximum_select_fusion.6), channel_id=1, source_target_pairs={{0,2},{1,3},{2,0},{3,1},{4,6},{5,7},{6,4},{7,5},{8,10},{9,11},{10,... | collective-permute-start | bytes 393224 | tf_op jit(solution)/shard_map/ppermute | solution.py:23
  109.0 8.6 %collective-permute-start.7 = (bf16[128,1024]{0,1:T(8,128)(2,1)S(1)}, bf16[128,1024]{0,1:T(8,128)(2,1)}, u32[]{:S(2)}, u32[]{:S(2)}) collective-permute-start(bf16[128,1024]{0,1:T(8,128)(2,1)S(1)} %maximum_select_fusion.5), channel_id=1, source_target_pairs={{0,4},{1,5},{2,6},{3,7},{4,0},{5,1},{6,2},{7,3},{8,12},{9,13},{10,... | collective-permute-start | bytes 786440 | tf_op jit(solution)/shard_map/ppermute | solution.py:23
  123.8 8.6 %collective-permute-start.8 = (bf16[64,2304]{1,0:T(8,128)(2,1)S(1)}, bf16[64,2304]{1,0:T(8,128)(2,1)S(1)}, u32[]{:S(2)}, u32[]{:S(2)}) collective-permute-start(bf16[64,2304]{1,0:T(8,128)(2,1)S(1)} %select_convert_fusion), channel_id=1, source_target_pairs={{0,4},{1,5},{2,6},{3,7},{4,0},{5,1},{6,2},{7,3},{8,12},{9,13},{10,... | collective-permute-start | bytes 884744 | tf_op jit(solution)/shard_map/ppermute | solution.py:23
  133.8 29.5 %copy-start.11 = (bf16[256,2304]{1,0:T(8,128)(2,1)S(1)}, bf16[256,2304]{1,0:T(8,128)(2,1)}, u32[]{:S(2)}) copy-start(bf16[256,2304]{1,0:T(8,128)(2,1)} %param.22) | copy-start | bytes 3538948
  133.8 10.2 %collective-permute-start.9 = (bf16[64,2304]{1,0:T(8,128)(2,1)S(1)}, bf16[64,2304]{1,0:T(8,128)(2,1)S(1)}, u32[]{:S(2)}, u32[]{:S(2)}) collective-permute-start(bf16[64,2304]{1,0:T(8,128)(2,1)S(1)} %get-tuple-element.8), channel_id=1, source_target_pairs={{0,1},{1,0},{2,3},{3,2},{4,5},{5,4},{6,7},{7,6},{8,9},{9,8},{10,11... | collective-permute-start | bytes 884744 | tf_op jit(solution)/shard_map/ppermute | solution.py:23
  144.0 10.1 %collective-permute-start.10 = (bf16[64,2304]{1,0:T(8,128)(2,1)S(1)}, bf16[64,2304]{1,0:T(8,128)(2,1)S(1)}, u32[]{:S(2)}, u32[]{:S(2)}) collective-permute-start(bf16[64,2304]{1,0:T(8,128)(2,1)S(1)} %fusion.29), channel_id=1, source_target_pairs={{0,2},{1,3},{2,0},{3,1},{4,6},{5,7},{6,4},{7,5},{8,10},{9,11},{10,... | collective-permute-start | bytes 884744 | tf_op jit(solution)/shard_map/ppermute | solution.py:23
  154.2 9.6 %copy-start.4 = (f32[128,1152]{0,1:T(8,128)S(1)}, f32[128,1152]{0,1:T(8,128)}, u32[]{:S(2)}) copy-start(f32[128,1152]{0,1:T(8,128)} %copy-done.3) | copy-start | bytes 1769476
  154.2 9.0 %collective-permute-start.11 = (bf16[64,2304]{1,0:T(8,128)(2,1)S(1)}, bf16[64,2304]{1,0:T(8,128)(2,1)S(1)}, u32[]{:S(2)}, u32[]{:S(2)}) collective-permute-start(bf16[64,2304]{1,0:T(8,128)(2,1)S(1)} %add_convert_fusion), channel_id=1, source_target_pairs={{0,4},{1,5},{2,6},{3,7},{4,0},{5,1},{6,2},{7,3},{8,12},{9,13},{10,... | collective-permute-start | bytes 884744 | tf_op jit(solution)/shard_map/ppermute | solution.py:23
  168.5 4.1 %collective-permute-start.12 = (bf16[4,256,256]{2,1,0:T(8,128)(2,1)}, bf16[4,256,256]{2,1,0:T(8,128)(2,1)}, u32[]{:S(2)}, u32[]{:S(2)}) collective-permute-start(bf16[4,256,256]{2,1,0:T(8,128)(2,1)} %slice.104), channel_id=1, source_target_pairs={{0,8},{8,0},{16,24},{24,16},{32,40},{40,32},{48,56},{56,48},{64,72... | collective-permute-start | bytes 1572872 | tf_op jit(solution)/shard_map/ppermute | solution.py:23
  174.0 7.5 %collective-permute-start.13 = (bf16[256,256]{1,0:T(8,128)(2,1)S(1)}, bf16[256,256]{1,0:T(8,128)(2,1)S(1)}, u32[]{:S(2)}, u32[]{:S(2)}) collective-permute-start(bf16[256,256]{1,0:T(8,128)(2,1)S(1)} %fusion.45), channel_id=1, source_target_pairs={{16,0},{24,8},{32,16},{40,24},{48,32},{56,40},{64,48},{72,56},{80,... | collective-permute-start | bytes 393224 | tf_op jit(solution)/shard_map/ppermute | solution.py:18
  181.5 12.1 %collective-permute-start.14 = (bf16[256,256]{1,0:T(8,128)(2,1)S(1)}, bf16[256,256]{1,0:T(8,128)(2,1)S(1)}, u32[]{:S(2)}, u32[]{:S(2)}) collective-permute-start(bf16[256,256]{1,0:T(8,128)(2,1)S(1)} %fusion.35), channel_id=1, source_target_pairs={{16,0},{24,8},{32,16},{40,24},{48,32},{56,40},{64,48},{72,56},{80,... | collective-permute-start | bytes 393224 | tf_op jit(solution)/shard_map/ppermute | solution.py:18
  193.6 13.1 %collective-permute-start.15 = (bf16[256,256]{1,0:T(8,128)(2,1)S(1)}, bf16[256,256]{1,0:T(8,128)(2,1)S(1)}, u32[]{:S(2)}, u32[]{:S(2)}) collective-permute-start(bf16[256,256]{1,0:T(8,128)(2,1)S(1)} %fusion.37), channel_id=1, source_target_pairs={{16,0},{24,8},{32,16},{40,24},{48,32},{56,40},{64,48},{72,56},{80,... | collective-permute-start | bytes 393224 | tf_op jit(solution)/shard_map/ppermute | solution.py:18
  206.7 12.0 %collective-permute-start.16 = (bf16[256,256]{1,0:T(8,128)(2,1)S(1)}, bf16[256,256]{1,0:T(8,128)(2,1)S(1)}, u32[]{:S(2)}, u32[]{:S(2)}) collective-permute-start(bf16[256,256]{1,0:T(8,128)(2,1)S(1)} %fusion.39), channel_id=1, source_target_pairs={{16,0},{24,8},{32,16},{40,24},{48,32},{56,40},{64,48},{72,56},{80,... | collective-permute-start | bytes 393224 | tf_op jit(solution)/shard_map/ppermute | solution.py:18
  (8 other events, 11.7 us)
